TPU v7x, 256 devices: a whole 4x4x8 slice. The times are simulated.
256 devices in a mesh: gz: 32 (over y_lo, z, core), gy: 8 (over x, y_hi).
Axes of the slice: x: 4, y: 4 (y_hi: 2, y_lo: 2; y = y_hi * 2 + y_lo), z: 8, core: 2. Of those that a mesh axis runs over, the one named last changes fastest.
Arguments:
- density: float32 [320, 128, 2048], P('gz', 'gy'), may hold values from -6 to 6
- dilations: int32 [3], replicated, may hold values from 1 to 4, as said below
- owner_rank: int32 [65536, 1], P(('gz', 'gy')), may hold values from 0 to 7; in each aligned block of 256 rows (0 to 255, 256 to 511, ...) at most 128 rows name the same one
- owner_slot: int32 [65536], P(('gz', 'gy')), may hold values from 0 to 255
- base_cell: int32 [65536], P(('gz', 'gy')), may hold values from 0 to 276479
- corner_weights: float32 [8, 65536], P(None, ('gz', 'gy')), may hold values from 0.05 to 1
Outputs:
- response: float32 [320, 128, 2048], P('gz', 'gy')
- catalogue: float32 [3, 65536], P(None, ('gz', 'gy'))
Inputs may be any that keep to these rules, and one draw needn't show every extreme that they name: `dilations`: one level has dilation 4 and another has dilation 1. `owner_rank`: the entries listed on one device name one owner at most 128 times; some owner is named exactly 128 times by some device.
All inputs are finite; a program needn't handle non-finite values.
Results may differ from a plain program's by a relative error of at most 0.00014.
Values sent between devices are 32-bit elements; how exact they have to be, the bound alone decides.
No kernel may reach another device: no remote copies, remote signals or barrier semaphores. Data moves between devices by JAX's collectives and lax.ppermute only.
A program may use at most 192 MiB of HBM per device.

v0:
```python
import jax
import jax.numpy as jnp
from jax import lax
from jax.experimental import pallas as pl
from jax.experimental.pallas import tpu as pltpu
from jax.sharding import PartitionSpec as P

SCALES = 3
HALO = 9
HOWN = 256
DMAX = 4


tap_weights = (0.0625, 0.25, 0.375, 0.25, 0.0625)
hessian_scale = 4.0


def with_halo(block, sides, width):
    for axis, dim in sides:
        count = lax.axis_size(axis)
        forward = [(i, i + 1) for i in range(count - 1)]
        forward.append((count - 1, 0))
        backward = [(target, source) for source, target in forward]
        low = lax.ppermute(
            lax.slice_in_dim(block, block.shape[dim] - width, None, axis=dim), axis, forward
        )
        high = lax.ppermute(lax.slice_in_dim(block, 0, width, axis=dim), axis, backward)
        block = jnp.concatenate([low, block, high], axis=dim)
    return block


def smooth_padded(field_data, dilation, along_dim, extent):
    running = None
    for offset in range(5):
        start_at = HALO - 1 + (offset - 2) * dilation
        summand = tap_weights[offset] * lax.dynamic_slice_in_dim(
            field_data, start_at, extent + 2, along_dim
        )
        running = summand if running is None else running + summand
    return running


def smooth_periodic(field_data, dilation):
    running = None
    for offset in range(5):
        summand = tap_weights[offset] * jnp.roll(field_data, -(offset - 2) * dilation, axis=2)
        running = summand if running is None else running + summand
    return running


def level_kernel(level_index, first, slab_depth, band_rows, row_length):
    planes = slab_depth + 2

    def compute(dilation, a_scr, s_scr, feature_ref, prev_ref, best_ref):
        def smooth_plane(plane, carry):
            along_z = None
            for offset in range(5):
                summand = tap_weights[offset] * a_scr[HALO - 1 + plane + (offset - 2) * dilation]
                along_z = summand if along_z is None else along_z + summand
            running = None
            for offset in range(5):
                shift = (-(offset - 2) * dilation) % row_length
                moved = along_z if shift == 0 else pltpu.roll(along_z, shift, 1)
                summand = tap_weights[offset] * moved
                running = summand if running is None else running + summand
            s_scr[plane] = running
            return carry

        lax.fori_loop(0, planes, smooth_plane, 0)

        def feature_plane(z, carry):
            for half in range(band_rows // 8):
                y0 = half * 8

                def at(dz, dy):
                    return s_scr[z + 1 + dz, pl.ds(1 + y0 + dy, 8), :]

                centre = at(0, 0)
                above_z = at(1, 0)
                below_z = at(-1, 0)
                above_y = at(0, 1)
                below_y = at(0, -1)

                def left(v):
                    return pltpu.roll(v, row_length - 1, 1)

                def right(v):
                    return pltpu.roll(v, 1, 1)

                curve_zz = hessian_scale * (above_z - 2.0 * centre + below_z)
                curve_yy = hessian_scale * (above_y - 2.0 * centre + below_y)
                curve_xx = hessian_scale * (left(centre) - 2.0 * centre + right(centre))
                curve_zy = (hessian_scale * 0.25) * (at(1, 1) - at(1, -1) - at(-1, 1) + at(-1, -1))
                curve_zx = (hessian_scale * 0.25) * (
                    left(above_z) - right(above_z) - left(below_z) + right(below_z)
                )
                curve_yx = (hessian_scale * 0.25) * (
                    left(above_y) - right(above_y) - left(below_y) + right(below_y)
                )
                trace_sum = curve_xx + curve_yy + curve_zz
                minor_sum = (
                    curve_xx * curve_yy
                    + curve_xx * curve_zz
                    + curve_yy * curve_zz
                    - curve_zy * curve_zy
                    - curve_zx * curve_zx
                    - curve_yx * curve_yx
                )
                value = (trace_sum * trace_sum / 3.0 - minor_sum) * (1.0 / (1.0 + jnp.exp(trace_sum)))
                feature_ref[z, pl.ds(y0, 8), :] = value
                if first:
                    best_ref[z, pl.ds(y0, 8), :] = value
                else:
                    best_ref[z, pl.ds(y0, 8), :] = jnp.maximum(prev_ref[z, pl.ds(y0, 8), :], value)
            return carry

        lax.fori_loop(0, slab_depth, feature_plane, 0)

    def kernel(*refs):
        if first:
            dil_ref, lo_hbm, mid_hbm, hi_hbm, feature_ref, best_ref, a_scr, s_scr, sems = refs
            prev_ref = None
        else:
            (dil_ref, lo_hbm, mid_hbm, hi_hbm, prev_ref, feature_ref, best_ref,
             a_scr, s_scr, sems) = refs
        copies = [
            pltpu.make_async_copy(lo_hbm, a_scr.at[pl.ds(0, HALO)], sems.at[0]),
            pltpu.make_async_copy(mid_hbm, a_scr.at[pl.ds(HALO, slab_depth)], sems.at[1]),
            pltpu.make_async_copy(hi_hbm, a_scr.at[pl.ds(HALO + slab_depth, HALO)], sems.at[2]),
        ]
        for copy in copies:
            copy.start()
        for copy in copies:
            copy.wait()
        dilation = dil_ref[level_index]
        for value in range(1, DMAX + 1):

            @pl.when(dilation == value)
            def _():
                compute(value, a_scr, s_scr, feature_ref, prev_ref, best_ref)

    def run(dilations, low, middle, high, prev):
        block = jax.ShapeDtypeStruct((slab_depth, band_rows, row_length), jnp.float32)
        anywhere = pl.BlockSpec(memory_space=pl.ANY)
        in_vmem = pl.BlockSpec(memory_space=pltpu.VMEM)
        in_specs = [pl.BlockSpec(memory_space=pltpu.SMEM), anywhere, anywhere, anywhere]
        operands = [dilations, low, middle, high]
        if not first:
            in_specs.append(in_vmem)
            operands.append(prev)
        return pl.pallas_call(
            kernel,
            out_shape=(block, block),
            in_specs=in_specs,
            out_specs=(in_vmem, in_vmem),
            scratch_shapes=[
                pltpu.VMEM((planes + 2 * HALO - 2, band_rows + 2, row_length), jnp.float32),
                pltpu.VMEM((planes, band_rows + 2, row_length), jnp.float32),
                pltpu.SemaphoreType.DMA((3,)),
            ],
            compiler_params=pltpu.CompilerParams(vmem_limit_bytes=56 * 1024 * 1024),
        )(*operands)

    return run


def z_neighbours(block, width):
    count = lax.axis_size("gz")
    forward = [(i, i + 1) for i in range(count - 1)]
    forward.append((count - 1, 0))
    backward = [(target, source) for source, target in forward]
    low = lax.ppermute(lax.slice_in_dim(block, block.shape[0] - width, None, axis=0), "gz", forward)
    high = lax.ppermute(lax.slice_in_dim(block, 0, width, axis=0), "gz", backward)
    return low, high


def invariants(curve_zz, curve_yy, curve_xx, curve_zy, curve_zx, curve_yx):
    trace_sum = curve_xx + curve_yy + curve_zz
    minor_sum = (
        curve_xx * curve_yy
        + curve_xx * curve_zz
        + curve_yy * curve_zz
        - curve_zy * curve_zy
        - curve_zx * curve_zx
        - curve_yx * curve_yx
    )
    return (trace_sum * trace_sum / 3.0 - minor_sum) * jax.nn.sigmoid(-trace_sum)


def signature(smoothed):
    centre = smoothed[1:-1, 1:-1]
    above_z = smoothed[2:, 1:-1]
    below_z = smoothed[:-2, 1:-1]
    above_y = smoothed[1:-1, 2:]
    below_y = smoothed[1:-1, :-2]
    curve_zz = hessian_scale * (above_z - 2.0 * centre + below_z)
    curve_yy = hessian_scale * (above_y - 2.0 * centre + below_y)
    curve_xx = hessian_scale * (jnp.roll(centre, -1, 2) - 2.0 * centre + jnp.roll(centre, 1, 2))
    curve_zy = (
        hessian_scale
        * 0.25
        * (smoothed[2:, 2:] - smoothed[2:, :-2] - smoothed[:-2, 2:] + smoothed[:-2, :-2])
    )
    curve_zx = (
        hessian_scale
        * 0.25
        * (
            jnp.roll(above_z, -1, 2)
            - jnp.roll(above_z, 1, 2)
            - jnp.roll(below_z, -1, 2)
            + jnp.roll(below_z, 1, 2)
        )
    )
    curve_yx = (
        hessian_scale
        * 0.25
        * (
            jnp.roll(above_y, -1, 2)
            - jnp.roll(above_y, 1, 2)
            - jnp.roll(below_y, -1, 2)
            + jnp.roll(below_y, 1, 2)
        )
    )
    return invariants(curve_zz, curve_yy, curve_xx, curve_zy, curve_zx, curve_yx)


def per_device(density, dilations, owner_rank, owner_slot, base_cell, corner_weights):
    slab_depth = density.shape[0]
    band_rows = density.shape[1]
    row_length = density.shape[2]
    banded = with_halo(density, (("gy", 1),), HALO)
    response = None
    features = []
    for level_index in range(SCALES):
        dilation = dilations[level_index]
        along_y = smooth_padded(banded, dilation, 1, band_rows)
        low, high = z_neighbours(along_y, HALO)
        run = level_kernel(level_index, level_index == 0, slab_depth, band_rows, row_length)
        feature, response = run(dilations, low, along_y, high, response)
        features.append(feature.reshape(slab_depth * band_rows, row_length))
    plane = (band_rows - 1) * row_length
    z_index = base_cell // plane
    remainder = base_cell % plane
    y_index = remainder // row_length
    x_index = remainder % row_length
    entries = base_cell.shape[0]
    steps = jnp.arange(2, dtype=jnp.int32)
    target_x = ((x_index[:, None] + steps[None, :]) % row_length).reshape(-1)
    pick_x = (
        jnp.arange(row_length, dtype=jnp.int32)[:, None] == target_x[None, :]
    ).astype(jnp.float32)
    cells = jnp.arange(slab_depth * band_rows, dtype=jnp.int32)[:, None, None]
    weight_grid = None
    for step_z in (0, 1):
        for step_y in (0, 1):
            row = (z_index + step_z) * band_rows + y_index + step_y
            corner = 4 * step_z + 2 * step_y
            weights = jnp.stack([corner_weights[corner], corner_weights[corner + 1]], axis=1)
            term = jnp.where(cells == row[None, :, None], weights[None, :, :], 0.0)
            weight_grid = term if weight_grid is None else weight_grid + term
    weight_grid = weight_grid.reshape(slab_depth * band_rows, entries * 2)
    partials = []
    for feature in features:
        picked = jnp.dot(
            feature, pick_x, precision=lax.Precision.HIGHEST, preferred_element_type=jnp.float32
        )
        partials.append(jnp.sum((picked * weight_grid).reshape(-1, entries, 2), axis=(0, 2)))
    partial_value = jnp.stack(partials)
    owner_group = owner_rank[:, 0]
    groups = lax.axis_size("gy")
    column = owner_group * HOWN + owner_slot
    onehot = (column[:, None] == jnp.arange(groups * HOWN, dtype=jnp.int32)[None, :]).astype(
        jnp.float32
    )
    spread = jnp.dot(
        partial_value, onehot, precision=lax.Precision.HIGHEST, preferred_element_type=jnp.float32
    )
    exchanged = lax.all_to_all(
        spread.reshape(SCALES, groups, HOWN), "gy", split_axis=1, concat_axis=1, tiled=True
    )
    catalogue = jnp.sum(exchanged, axis=1)
    return (response, catalogue)


def solution(mesh):
    placed = (
        P("gz", "gy", None),
        P(),
        P(("gz", "gy"), None),
        P(("gz", "gy")),
        P(("gz", "gy")),
        P(None, ("gz", "gy")),
    )
    return jax.shard_map(
        per_device,
        mesh=mesh,
        in_specs=placed,
        out_specs=(P("gz", "gy", None), P(None, ("gz", "gy"))),
        check_vma=False,
    )
```

profile of v0, /device:TPU:2, one launch (start us, length us, event | category | flops | bytes accessed | tf_op | source)
XLA Modules:
  0.0 185.5 jit_solution(18002259531530055279)
XLA Ops:
  0.6 2.0 %fusion.24 = (f32[10,9,2048]{2,1,0:T(8,128)S(1)}, f32[10,9,2048]{2,1,0:T(8,128)S(1)}) fusion(f32[10,16,2048]{2,1,0:T(8,128)} %param.6), kind=kLoop, calls=%fused_computation.67 | loop fusion | bytes 2949120 | tf_op jit(solution)/shard_map/slice | solution.py:25
  3.1 3.2 %collective-permute-start.1 = (f32[10,9,2048]{2,0,1:T(8,128)S(1)}, f32[10,9,2048]{2,0,1:T(8,128)S(1)}, u32[]{:S(2)}, u32[]{:S(2)}) collective-permute-start(f32[10,9,2048]{2,0,1:T(8,128)S(1)} %copy.30), channel_id=1, source_target_pairs={{1,0},{2,1},{3,2},{4,3},{5,4},{6,5},{7,6},{0,7},{9,8},{10,9},{11,1... | collective-permute-start | bytes 2211848 | tf_op jit(solution)/shard_map/ppermute | solution.py:27
  18.1 0.7 pad_maximum_fusion.3
  18.8 0.8 copy.24
  19.6 1.6 broadcast_in_dim.94
  21.9 0.8 copy.20
  22.7 1.6 broadcast_in_dim.85
  24.3 0.8 copy.26
  25.1 1.6 broadcast_in_dim.98
  26.8 0.8 copy.22
  27.6 1.6 broadcast_in_dim.90
  29.2 1.3 broadcast_add_fusion.1
  30.5 0.8 iota_add_fusion
  31.2 1.0 add.344
  32.4 25.3 %collective-permute-done.1 = f32[10,9,2048]{2,0,1:T(8,128)S(1)} collective-permute-done((f32[10,9,2048]{2,0,1:T(8,128)S(1)}, f32[10,9,2048]{2,0,1:T(8,128)S(1)}, u32[]{:S(2)}, u32[]{:S(2)}) %collective-permute-start.1) | collective-permute-done | bytes 737312 | tf_op jit(solution)/shard_map/ppermute | solution.py:27
  58.2 1.7 copy.18
  60.3 5.9 %multiply_add_fusion = (f32[10,18,2048]{2,1,0:T(8,128)S(1)}, f32[10,18,2048]{2,1,0:T(8,128)S(1)}, f32[10,18,2048]{2,1,0:T(8,128)}) fusion(f32[10,34,2048]{2,1,0:T(8,128)S(1)} %pad_maximum_fusion, s32[]{:T(128)S(6)} %select_n.93, s32[]{:T(128)S(6)} %select_n.92, s32[]{:T(128)S(6)} %select_n.91, s32[]{:T(128)S(6)} %select_n.90, s32[]{:T(128)S(6)} %select_n.89, ...), kind=kLoop, calls=%fused_computation.11 | loop fusion | flops 9216000 | bytes 23593008 | tf_op jit(solution)/shard_map/add | solution.py:39
  66.3 2.6 %fusion.21 = (f32[9,18,2048]{2,1,0:T(8,128)}, f32[9,18,2048]{2,1,0:T(8,128)}) fusion(f32[10,18,2048]{2,1,0:T(8,128)S(1)} %get-tuple-element.20.refs_2_), kind=kLoop, calls=%fused_computation.64 | loop fusion | bytes 5308416 | tf_op jit(solution)/shard_map/slice | solution.py:173
  68.9 5.4 %collective-permute-start.7 = (f32[9,18,2048]{2,1,0:T(8,128)}, f32[9,18,2048]{2,1,0:T(8,128)}, u32[]{:S(2)}, u32[]{:S(2)}) collective-permute-start(f32[9,18,2048]{2,1,0:T(8,128)} %get-tuple-element.23), channel_id=1, source_target_pairs={{8,0},{16,8},{24,16},{32,24},{40,32},{48,40},{56,48},{64,56},{72,6... | collective-permute-start | bytes 3981320 | tf_op jit(solution)/shard_map/ppermute | solution.py:173
  74.3 0.7 iota_compare_fusion.20
  75.6 0.8 copy.23
  76.5 2.2 %fusion.22 = (f32[9,18,2048]{2,1,0:T(8,128)}, f32[9,18,2048]{2,1,0:T(8,128)}) fusion(f32[10,18,2048]{2,1,0:T(8,128)S(1)} %get-tuple-element.21.refs_2_), kind=kLoop, calls=%fused_computation.65 | loop fusion | bytes 5308416 | tf_op jit(solution)/shard_map/slice | solution.py:173
  78.6 3.9 %collective-permute-start.5 = (f32[9,18,2048]{2,1,0:T(8,128)}, f32[9,18,2048]{2,1,0:T(8,128)}, u32[]{:S(2)}, u32[]{:S(2)}) collective-permute-start(f32[9,18,2048]{2,1,0:T(8,128)} %get-tuple-element.25), channel_id=1, source_target_pairs={{8,0},{16,8},{24,16},{32,24},{40,32},{48,40},{56,48},{64,56},{72,6... | collective-permute-start | bytes 3981320 | tf_op jit(solution)/shard_map/ppermute | solution.py:173
  82.9 3.9 %collective-permute-start.3 = (f32[9,18,2048]{2,1,0:T(8,128)S(1)}, f32[9,18,2048]{2,1,0:T(8,128)}, u32[]{:S(2)}, u32[]{:S(2)}) collective-permute-start(f32[9,18,2048]{2,1,0:T(8,128)S(1)} %get-tuple-element.27), channel_id=1, source_target_pairs={{8,0},{16,8},{24,16},{32,24},{40,32},{48,40},{56,48},{64,56},{72,6... | collective-permute-start | bytes 3981320 | tf_op jit(solution)/shard_map/ppermute | solution.py:173
  86.9 7.8 %collective-permute-done.7.refs_3_ = f32[9,18,2048]{2,1,0:T(8,128)} collective-permute-done((f32[9,18,2048]{2,1,0:T(8,128)}, f32[9,18,2048]{2,1,0:T(8,128)}, u32[]{:S(2)}, u32[]{:S(2)}) %collective-permute-start.7) | collective-permute-done | bytes 1327136 | tf_op jit(solution)/shard_map/ppermute | solution.py:173
  94.7 0.7 iota_compare_fusion.18
  95.5 0.9 broadcast_in_dim.96
  96.4 2.0 %broadcast_in_dim.97 = pred[160,512]{0,1:T(32,128)(4,1)} reshape(pred[160,256,2]{0,2,1:T(4,128)(4,1)} %broadcast_in_dim.96) | data formatting | bytes 163840 | tf_op jit(solution)/shard_map/jit(_where)/broadcast_in_dim | solution.py:259
  98.4 1.6 copy.27
  100.0 1.8 broadcast_in_dim.83
  101.8 2.0 %broadcast_in_dim.84 = pred[160,512]{0,1:T(32,128)(4,1)} reshape(pred[160,256,2]{0,2,1:T(4,128)(4,1)} %broadcast_in_dim.83) | data formatting | bytes 163840 | tf_op jit(solution)/shard_map/jit(_where)/broadcast_in_dim | solution.py:259
  103.8 1.6 copy.21
  105.4 1.8 broadcast_in_dim.92
  107.2 2.0 %broadcast_in_dim.93 = pred[160,512]{0,1:T(32,128)(4,1)} reshape(pred[160,256,2]{0,2,1:T(4,128)(4,1)} %broadcast_in_dim.92) | data formatting | bytes 163840 | tf_op jit(solution)/shard_map/jit(_where)/broadcast_in_dim | solution.py:259
  109.2 1.0 copy.25
  110.2 0.7 broadcast_multiply_fusion
  111.6 13.1 %shard_map.77 = (f32[10,16,2048]{2,1,0:T(8,128)}, f32[10,16,2048]{2,1,0:T(8,128)}) custom-call(s32[3]{0:T(128)} %refs_0_.5, f32[9,18,2048]{2,1,0:T(8,128)} %collective-permute-done.6.refs_1_, f32[10,18,2048]{2,1,0:T(8,128)} %copy-done, f32[9,18,2048]{2,1,0:T(8,128)} %collective-permute-done.7.refs_3_), custom_call_target="tpu_custom_call" | custom-call | tf_op jit(solution)/shard_map/pallas_call | solution.py:151
  124.7 3.7 %fusion.12 = f32[512]{0:T(512)} fusion(f32[160,2048]{1,0:T(8,128)} %bitcast.66, s32[512]{0:T(512)S(1)} %add_select_fusion, pred[160,512]{1,0:T(32,128)(4,1)S(1)} %copy-done.7, f32[512]{0:T(512)S(1)} %copy-done.21, pred[160,512]{1,0:T(32,128)(4,1)S(1)} %copy.25, f32[512]{0:T(512)S(1)} %copy-done.19, pred[160,512]{1,0:T(32,128)(4,1)S(1)} %copy-done.4, ...), kind=kOutput, calls=%fused_computation.19 | convolution fusion | flops 2015051264 | bytes 1650688 | tf_op jit(solution)/shard_map/dot_general | solution.py:264
  128.4 1.5 reduce_sum.45
  129.9 13.8 %shard_map.78 = (f32[10,16,2048]{2,1,0:T(8,128)}, f32[10,16,2048]{2,1,0:T(8,128)}) custom-call(s32[3]{0:T(128)} %refs_0_.5, f32[9,18,2048]{2,1,0:T(8,128)} %collective-permute-done.4.refs_1_, f32[10,18,2048]{2,1,0:T(8,128)} %copy-done.2, f32[9,18,2048]{2,1,0:T(8,128)} %collective-permute-done.5.refs_3_, f32[10,16,2048]{2,1,0:T(8,128)} %get-tuple-element.8.refs_4_), custom_call_target="tpu_custom_call" | custom-call | tf_op jit(solution)/shard_map/pallas_call | solution.py:151
  143.7 3.7 %fusion.11 = f32[512]{0:T(512)} fusion(f32[160,2048]{1,0:T(8,128)} %bitcast.65, s32[512]{0:T(512)S(1)} %copy-done.24, pred[160,512]{1,0:T(32,128)(4,1)S(1)} %copy-done.8, f32[512]{0:T(512)S(1)} %copy-done.21, pred[160,512]{1,0:T(32,128)(4,1)S(1)} %copy-done.14, f32[512]{0:T(512)S(1)} %copy-done.19, pred[160,512]{1,0:T(32,128)(4,1)S(1)} %copy-done.5, ...), kind=kOutput, calls=%fused_computation.18 | convolution fusion | flops 2015051264 | bytes 1650688 | tf_op jit(solution)/shard_map/dot_general | solution.py:264
  147.4 1.5 reduce_sum.51
  148.9 1.6 reduce_sum.46
  150.5 1.6 reduce_sum.62
  152.1 13.7 %shard_map.79 = (f32[10,16,2048]{2,1,0:T(8,128)}, f32[10,16,2048]{2,1,0:T(8,128)}) custom-call(s32[3]{0:T(128)} %refs_0_.5, f32[9,18,2048]{2,1,0:T(8,128)} %collective-permute-done.2.refs_1_, f32[10,18,2048]{2,1,0:T(8,128)} %get-tuple-element.22.refs_2_, f32[9,18,2048]{2,1,0:T(8,128)} %collective-permute-done.3.refs_3_, f32[10,16,2048]{2,1,0:T(8,128)} %get-tuple-element.9.refs_4_), custom_call_target="tpu_custom_call" | custom-call | tf_op jit(solution)/shard_map/pallas_call | solution.py:151
  165.9 3.1 %fusion.10 = f32[512]{0:T(512)S(1)} fusion(f32[160,2048]{1,0:T(8,128)} %bitcast.64, s32[512]{0:T(512)S(1)} %copy-done.25, pred[160,512]{1,0:T(32,128)(4,1)S(1)} %copy-done.9, f32[512]{0:T(512)S(1)} %copy-done.21, pred[160,512]{1,0:T(32,128)(4,1)S(1)} %copy-done.15, f32[512]{0:T(512)S(1)} %copy-done.19, pred[160,512]{1,0:T(32,128)(4,1)S(1)} %copy-done.6, ...), kind=kOutput, calls=%fused_computation.17 | convolution fusion | flops 2015051264 | bytes 1650688 | tf_op jit(solution)/shard_map/dot_general | solution.py:264
  169.3 0.8 fusion.6
  170.1 14.8 %all_to_all.5 = f32[3,8,256]{2,0,1:T(4,128)S(1)} all-to-all(f32[3,8,256]{2,0,1:T(4,128)S(1)} %bitcast.59), channel_id=1, replica_groups=mesh['gz'=32,'gy'=8] {'gy'}, dimensions={1} | all-to-all | bytes 49152 | tf_op jit(solution)/shard_map/all_to_all | solution.py:278
  (86 shorter events, 6.7 us)
Async XLA Ops:
  2.6 4.6 %copy-start.17 = (f32[8,256]{1,0:T(8,128)S(1)}, f32[8,256]{1,0:T(8,128)}, u32[]{:S(2)}) copy-start(f32[8,256]{1,0:T(8,128)} %param.11) | copy-start | bytes 24580
  2.6 5.2 %copy-start.16 = (s32[3]{0:T(128)S(1)}, s32[3]{0:T(128)}, u32[]{:S(2)}) copy-start(s32[3]{0:T(128)} %refs_0_.5) | copy-start | bytes 40
  3.1 54.6 %collective-permute-start.1 = (f32[10,9,2048]{2,0,1:T(8,128)S(1)}, f32[10,9,2048]{2,0,1:T(8,128)S(1)}, u32[]{:S(2)}, u32[]{:S(2)}) collective-permute-start(f32[10,9,2048]{2,0,1:T(8,128)S(1)} %copy.30), channel_id=1, source_target_pairs={{1,0},{2,1},{3,2},{4,3},{5,4},{6,5},{7,6},{0,7},{9,8},{10,9},{11,1... | collective-permute-start | bytes 2211848 | tf_op jit(solution)/shard_map/ppermute | solution.py:27
  6.8 51.3 %collective-permute-start = (f32[10,9,2048]{2,0,1:T(8,128)S(1)}, f32[10,9,2048]{2,0,1:T(8,128)}, u32[]{:S(2)}, u32[]{:S(2)}) collective-permute-start(f32[10,9,2048]{2,0,1:T(8,128)S(1)} %copy.29), channel_id=1, source_target_pairs={{0,1},{1,2},{2,3},{3,4},{4,5},{5,6},{6,7},{7,0},{8,9},{9,10},{10,1... | collective-permute-start | bytes 2211848 | tf_op jit(solution)/shard_map/ppermute | solution.py:24
  32.3 27.6 %copy-start.3 = (f32[10,16,2048]{2,1,0:T(8,128)S(1)}, f32[10,16,2048]{2,1,0:T(8,128)}, u32[]{:S(2)}) copy-start(f32[10,16,2048]{2,1,0:T(8,128)} %param.6) | copy-start | bytes 3932164
  66.3 2.6 %copy-start = (f32[10,18,2048]{2,1,0:T(8,128)}, f32[10,18,2048]{2,1,0:T(8,128)S(1)}, u32[]{:S(2)}) copy-start(f32[10,18,2048]{2,1,0:T(8,128)S(1)} %get-tuple-element.20.refs_2_) | copy-start | bytes 4423684
  66.3 10.2 %copy-start.2 = (f32[10,18,2048]{2,1,0:T(8,128)}, f32[10,18,2048]{2,1,0:T(8,128)S(1)}, u32[]{:S(2)}) copy-start(f32[10,18,2048]{2,1,0:T(8,128)S(1)} %get-tuple-element.21.refs_2_) | copy-start | bytes 4423684
  68.9 25.8 %collective-permute-start.7 = (f32[9,18,2048]{2,1,0:T(8,128)}, f32[9,18,2048]{2,1,0:T(8,128)}, u32[]{:S(2)}, u32[]{:S(2)}) collective-permute-start(f32[9,18,2048]{2,1,0:T(8,128)} %get-tuple-element.23), channel_id=1, source_target_pairs={{8,0},{16,8},{24,16},{32,24},{40,32},{48,40},{56,48},{64,56},{72,6... | collective-permute-start | bytes 3981320 | tf_op jit(solution)/shard_map/ppermute | solution.py:173
  76.5 35.1 %collective-permute-start.6 = (f32[9,18,2048]{2,1,0:T(8,128)}, f32[9,18,2048]{2,1,0:T(8,128)}, u32[]{:S(2)}, u32[]{:S(2)}) collective-permute-start(f32[9,18,2048]{2,1,0:T(8,128)} %get-tuple-element.24), channel_id=1, source_target_pairs={{0,8},{8,16},{16,24},{24,32},{32,40},{40,48},{48,56},{56,64},{64,7... | collective-permute-start | bytes 3981320 | tf_op jit(solution)/shard_map/ppermute | solution.py:172
  76.5 6.0 %copy-start.1 = (f32[10,18,2048]{2,1,0:T(8,128)S(1)}, f32[10,18,2048]{2,1,0:T(8,128)}, u32[]{:S(2)}) copy-start(f32[10,18,2048]{2,1,0:T(8,128)} %get-tuple-element.22.refs_2_) | copy-start | bytes 4423684
  78.6 51.2 %collective-permute-start.5 = (f32[9,18,2048]{2,1,0:T(8,128)}, f32[9,18,2048]{2,1,0:T(8,128)}, u32[]{:S(2)}, u32[]{:S(2)}) collective-permute-start(f32[9,18,2048]{2,1,0:T(8,128)} %get-tuple-element.25), channel_id=1, source_target_pairs={{8,0},{16,8},{24,16},{32,24},{40,32},{48,40},{56,48},{64,56},{72,6... | collective-permute-start | bytes 3981320 | tf_op jit(solution)/shard_map/ppermute | solution.py:173
  82.5 47.4 %collective-permute-start.4 = (f32[9,18,2048]{2,1,0:T(8,128)}, f32[9,18,2048]{2,1,0:T(8,128)}, u32[]{:S(2)}, u32[]{:S(2)}) collective-permute-start(f32[9,18,2048]{2,1,0:T(8,128)} %get-tuple-element.26), channel_id=1, source_target_pairs={{0,8},{8,16},{16,24},{24,32},{32,40},{40,48},{48,56},{56,64},{64,7... | collective-permute-start | bytes 3981320 | tf_op jit(solution)/shard_map/ppermute | solution.py:172
  82.5 12.2 %copy-start.18 = (s32[256]{0:T(256)S(1)}, s32[256]{0:T(256)}, u32[]{:S(2)}) copy-start(s32[256]{0:T(256)} %get-tuple-element.17) | copy-start | bytes 3076
  82.9 28.0 %copy-start.28 = (s32[256]{0:T(256)S(1)}, s32[256]{0:T(256)}, u32[]{:S(2)}) copy-start(s32[256]{0:T(256)} %param.9) | copy-start | bytes 3076
  82.9 69.2 %collective-permute-start.3 = (f32[9,18,2048]{2,1,0:T(8,128)S(1)}, f32[9,18,2048]{2,1,0:T(8,128)}, u32[]{:S(2)}, u32[]{:S(2)}) collective-permute-start(f32[9,18,2048]{2,1,0:T(8,128)S(1)} %get-tuple-element.27), channel_id=1, source_target_pairs={{8,0},{16,8},{24,16},{32,24},{40,32},{48,40},{56,48},{64,56},{72,6... | collective-permute-start | bytes 3981320 | tf_op jit(solution)/shard_map/ppermute | solution.py:173
  94.7 57.4 %collective-permute-start.2 = (f32[9,18,2048]{2,1,0:T(8,128)S(1)}, f32[9,18,2048]{2,1,0:T(8,128)}, u32[]{:S(2)}, u32[]{:S(2)}) collective-permute-start(f32[9,18,2048]{2,1,0:T(8,128)S(1)} %get-tuple-element.28), channel_id=1, source_target_pairs={{0,8},{8,16},{16,24},{24,32},{32,40},{40,48},{48,56},{56,64},{64,7... | collective-permute-start | bytes 3981320 | tf_op jit(solution)/shard_map/ppermute | solution.py:172
  110.2 14.5 %copy-start.13 = (pred[160,512]{1,0:T(32,128)(4,1)}, pred[160,512]{1,0:T(32,128)(4,1)S(1)}, u32[]{:S(2)}) copy-start(pred[160,512]{1,0:T(32,128)(4,1)S(1)} %copy.25) | copy-start | bytes 245764
  111.5 13.2 %copy-start.23 = (s32[512]{0:T(512)}, s32[512]{0:T(512)S(1)}, u32[]{:S(2)}) copy-start(s32[512]{0:T(512)S(1)} %add_select_fusion) | copy-start | bytes 6148
  111.5 13.2 %copy-start.4 = (pred[160,512]{1,0:T(32,128)(4,1)S(1)}, pred[160,512]{1,0:T(32,128)(4,1)}, u32[]{:S(2)}) copy-start(pred[160,512]{1,0:T(32,128)(4,1)} %copy.23) | copy-start | bytes 245764
  111.5 13.2 %copy-start.7 = (pred[160,512]{1,0:T(32,128)(4,1)S(1)}, pred[160,512]{1,0:T(32,128)(4,1)}, u32[]{:S(2)}) copy-start(pred[160,512]{1,0:T(32,128)(4,1)} %copy.27) | copy-start | bytes 245764
  111.5 13.2 %copy-start.10 = (pred[160,512]{1,0:T(32,128)(4,1)S(1)}, pred[160,512]{1,0:T(32,128)(4,1)}, u32[]{:S(2)}) copy-start(pred[160,512]{1,0:T(32,128)(4,1)} %copy.21) | copy-start | bytes 245764
  111.5 13.2 %copy-start.19 = (f32[512]{0:T(512)S(1)}, f32[512]{0:T(512)}, u32[]{:S(2)}) copy-start(f32[512]{0:T(512)} %broadcast_in_dim.94) | copy-start | bytes 6148
  111.5 13.2 %copy-start.20 = (f32[512]{0:T(512)S(1)}, f32[512]{0:T(512)}, u32[]{:S(2)}) copy-start(f32[512]{0:T(512)} %broadcast_in_dim.85) | copy-start | bytes 6148
  111.5 13.2 %copy-start.21 = (f32[512]{0:T(512)S(1)}, f32[512]{0:T(512)}, u32[]{:S(2)}) copy-start(f32[512]{0:T(512)} %broadcast_in_dim.98) | copy-start | bytes 6148
  111.5 13.2 %copy-start.22 = (f32[512]{0:T(512)S(1)}, f32[512]{0:T(512)}, u32[]{:S(2)}) copy-start(f32[512]{0:T(512)} %broadcast_in_dim.90) | copy-start | bytes 6148
  129.9 13.8 %copy-start.5 = (pred[160,512]{1,0:T(32,128)(4,1)S(1)}, pred[160,512]{1,0:T(32,128)(4,1)}, u32[]{:S(2)}) copy-start(pred[160,512]{1,0:T(32,128)(4,1)} %copy.23) | copy-start | bytes 245764
  129.9 13.8 %copy-start.8 = (pred[160,512]{1,0:T(32,128)(4,1)S(1)}, pred[160,512]{1,0:T(32,128)(4,1)}, u32[]{:S(2)}) copy-start(pred[160,512]{1,0:T(32,128)(4,1)} %copy.27) | copy-start | bytes 245764
  129.9 13.8 %copy-start.11 = (pred[160,512]{1,0:T(32,128)(4,1)S(1)}, pred[160,512]{1,0:T(32,128)(4,1)}, u32[]{:S(2)}) copy-start(pred[160,512]{1,0:T(32,128)(4,1)} %copy.21) | copy-start | bytes 245764
  129.9 13.8 %copy-start.14 = (pred[160,512]{1,0:T(32,128)(4,1)S(1)}, pred[160,512]{1,0:T(32,128)(4,1)}, u32[]{:S(2)}) copy-start(pred[160,512]{1,0:T(32,128)(4,1)} %copy-done.13) | copy-start | bytes 245764
  129.9 13.8 %copy-start.24 = (s32[512]{0:T(512)S(1)}, s32[512]{0:T(512)}, u32[]{:S(2)}) copy-start(s32[512]{0:T(512)} %copy-done.23) | copy-start | bytes 6148
  152.1 13.8 %copy-start.6 = (pred[160,512]{1,0:T(32,128)(4,1)S(1)}, pred[160,512]{1,0:T(32,128)(4,1)}, u32[]{:S(2)}) copy-start(pred[160,512]{1,0:T(32,128)(4,1)} %copy.23) | copy-start | bytes 245764
  152.1 13.8 %copy-start.9 = (pred[160,512]{1,0:T(32,128)(4,1)S(1)}, pred[160,512]{1,0:T(32,128)(4,1)}, u32[]{:S(2)}) copy-start(pred[160,512]{1,0:T(32,128)(4,1)} %copy.27) | copy-start | bytes 245764
  152.1 13.8 %copy-start.12 = (pred[160,512]{1,0:T(32,128)(4,1)S(1)}, pred[160,512]{1,0:T(32,128)(4,1)}, u32[]{:S(2)}) copy-start(pred[160,512]{1,0:T(32,128)(4,1)} %copy.21) | copy-start | bytes 245764
  152.1 13.8 %copy-start.15 = (pred[160,512]{1,0:T(32,128)(4,1)S(1)}, pred[160,512]{1,0:T(32,128)(4,1)}, u32[]{:S(2)}) copy-start(pred[160,512]{1,0:T(32,128)(4,1)} %copy-done.13) | copy-start | bytes 245764
  152.1 13.8 %copy-start.25 = (s32[512]{0:T(512)S(1)}, s32[512]{0:T(512)}, u32[]{:S(2)}) copy-start(s32[512]{0:T(512)} %copy-done.23) | copy-start | bytes 6148
  165.8 3.4 %copy-start.26 = (f32[256]{0:T(256)S(1)}, f32[256]{0:T(256)}, u32[]{:S(2)}) copy-start(f32[256]{0:T(256)} %reduce_sum.46) | copy-start | bytes 3076
  165.9 3.4 %copy-start.27 = (f32[256]{0:T(256)S(1)}, f32[256]{0:T(256)}, u32[]{:S(2)}) copy-start(f32[256]{0:T(256)} %reduce_sum.62) | copy-start | bytes 3076
  165.9 3.4 %copy-start.29 = (s32[256]{0:T(256)S(1)}, s32[256]{0:T(256)}, u32[]{:S(2)}) copy-start(s32[256]{0:T(256)} %add.354) | copy-start | bytes 3076
where the time goes:
time: 187 us; the launch traced here: 186 us
  local copies, waits for them, and re-layouts  41.6 us (22%)
  Pallas kernels  40.5 us (22%)
  waiting for transfers between devices  33.2 us (18%)
  starting transfers between devices  16.9 us (9%)
  other arithmetic  16.5 us (9%)
  blocking collectives  14.8 us (8%)
  matrix products  11.3 us (6%)
  between operations  10.8 us (6%)
    pallas_call x3, Pallas kernels, run(): pl.pallas_call(kernel, out_shape=(block, block), in_specs=in_specs, out_s...  40.5 us
    ppermute x1, waiting for transfers between devices, with_halo(): lax.ppermute(lax.slice_in_dim(block, 0, width, axis=dim), axis, backward)  25.3 us
    broadcast_in_dim x16, local copies, waits for them, and re-layouts, per_device(): term = jnp.where(cells == row[None, :, None], weights[None, :, :], 0.0)  22.6 us
    all_to_all x1, blocking collectives, per_device(): lax.all_to_all(spread.reshape(SCALES, groups, HOWN), 'gy', split_axis=1,...  14.8 us
    ppermute x3, starting transfers between devices, z_neighbours(): lax.ppermute(lax.slice_in_dim(block, 0, width, axis=0), 'gz', backward)  13.2 us
    dot_general x3, matrix products, per_device(): jnp.dot(feature, pick_x, precision=lax.Precision.HIGHEST, preferred_eleme...  10.4 us
    ppermute x3, waiting for transfers between devices, z_neighbours(): lax.ppermute(lax.slice_in_dim(block, 0, width, axis=0), 'gz', backward)  7.84 us
    add x1, other arithmetic, smooth_padded(): running = summand if running is None else running + summand  5.92 us
  transfers between devices with their start and end apart: 8, of which 2 were waited for; matrix products, arithmetic and copies ran while one was open for 28% of the time, Pallas kernels for 14%

commit v1 on v0

--- a/solution.py
+++ b/solution.py
@@ -249,22 +249,24 @@
     pick_x = (
         jnp.arange(row_length, dtype=jnp.int32)[:, None] == target_x[None, :]
     ).astype(jnp.float32)
-    cells = jnp.arange(slab_depth * band_rows, dtype=jnp.int32)[:, None, None]
+    cells = jnp.arange(slab_depth * band_rows, dtype=jnp.int32)[:, None]
     weight_grid = None
     for step_z in (0, 1):
         for step_y in (0, 1):
-            row = (z_index + step_z) * band_rows + y_index + step_y
+            row = jnp.repeat((z_index + step_z) * band_rows + y_index + step_y, 2)
             corner = 4 * step_z + 2 * step_y
-            weights = jnp.stack([corner_weights[corner], corner_weights[corner + 1]], axis=1)
-            term = jnp.where(cells == row[None, :, None], weights[None, :, :], 0.0)
+            weights = jnp.stack(
+                [corner_weights[corner], corner_weights[corner + 1]], axis=1
+            ).reshape(-1)
+            term = jnp.where(cells == row[None, :], weights[None, :], 0.0)
             weight_grid = term if weight_grid is None else weight_grid + term
-    weight_grid = weight_grid.reshape(slab_depth * band_rows, entries * 2)
     partials = []
     for feature in features:
         picked = jnp.dot(
             feature, pick_x, precision=lax.Precision.HIGHEST, preferred_element_type=jnp.float32
         )
-        partials.append(jnp.sum((picked * weight_grid).reshape(-1, entries, 2), axis=(0, 2)))
+        per_column = jnp.sum(picked * weight_grid, axis=0)
+        partials.append(jnp.sum(per_column.reshape(entries, 2), axis=1))
     partial_value = jnp.stack(partials)
     owner_group = owner_rank[:, 0]
     groups = lax.axis_size("gy")

time: 187 us -> 189 us (1.011)
  waiting for transfers between devices: 33.2 us -> 43 us
  local copies, waits for them, and re-layouts: 41.6 us -> 36.7 us
  other arithmetic: 16.5 us -> 14 us
    broadcast_in_dim x16 -> x8, local copies, waits for them, and re-layouts: 22.6 us -> 10.9 us  [the longest x4 6.5 us: per_device(): term = jnp.where(cells == row[None, :], weights[None, :], 0.0)]
    ppermute x1, waiting for transfers between devices: 25.3 us -> 33.9 us  [with_halo(): lax.ppermute(lax.slice_in_dim(block, 0, width, axis=dim), axis, backward)]
    eq x0 -> x4, local copies, waits for them, and re-layouts: none -> 6.52 us  [per_device(): term = jnp.where(cells == row[None, :], weights[None, :], 0.0)]
    reduce_sum x3 -> x0, local copies, waits for them, and re-layouts: 3.08 us -> none  [per_device(): jnp.sum((picked * weight_grid).reshape(-1, entries, 2), axis=(0, 2))]
    reshape x0 -> x3, local copies, waits for them, and re-layouts: none -> 3.08 us  [per_device(): partials.append(jnp.sum(per_column.reshape(entries, 2), axis=1))]
  transfers between devices with their start and end apart: 8 -> 8, of which waited for: 2 -> 2; matrix products, arithmetic and copies ran while one was open for 28% -> 24% of each run, Pallas kernels for 14% -> 14%
where the time goes in v1:
time: 189 us; the launch traced here: 188 us
  waiting for transfers between devices  43 us (23%)
  Pallas kernels  40.3 us (21%)
  local copies, waits for them, and re-layouts  36.7 us (19%)
  starting transfers between devices  16.9 us (9%)
  blocking collectives  14.8 us (8%)
  other arithmetic  14 us (7%)
  matrix products  11.3 us (6%)
  between operations  10.9 us (6%)
    pallas_call x3, Pallas kernels, run(): pl.pallas_call(kernel, out_shape=(block, block), in_specs=in_specs, out_s...  40.3 us
    ppermute x1, waiting for transfers between devices, with_halo(): lax.ppermute(lax.slice_in_dim(block, 0, width, axis=dim), axis, backward)  33.9 us
    all_to_all x1, blocking collectives, per_device(): lax.all_to_all(spread.reshape(SCALES, groups, HOWN), 'gy', split_axis=1,...  14.8 us
    ppermute x3, starting transfers between devices, z_neighbours(): lax.ppermute(lax.slice_in_dim(block, 0, width, axis=0), 'gz', backward)  13.2 us
    dot_general x3, matrix products, per_device(): jnp.dot(feature, pick_x, precision=lax.Precision.HIGHEST, preferred_eleme...  10.5 us
    ppermute x3, waiting for transfers between devices, z_neighbours(): lax.ppermute(lax.slice_in_dim(block, 0, width, axis=0), 'gz', backward)  9.06 us
    eq x4, local copies, waits for them, and re-layouts, per_device(): term = jnp.where(cells == row[None, :], weights[None, :], 0.0)  6.52 us
    broadcast_in_dim x4, local copies, waits for them, and re-layouts, per_device(): term = jnp.where(cells == row[None, :], weights[None, :], 0.0)  6.5 us
  transfers between devices with their start and end apart: 8, of which 2 were waited for; matrix products, arithmetic and copies ran while one was open for 24% of the time, Pallas kernels for 14%

profile of v1, /device:TPU:2, one launch (start us, length us, event | category | flops | bytes accessed | tf_op | source)
XLA Modules:
  0.0 187.8 jit_solution(14035555493659978493)
XLA Ops:
  0.6 2.0 %fusion.24 = (f32[10,9,2048]{2,1,0:T(8,128)S(1)}, f32[10,9,2048]{2,1,0:T(8,128)S(1)}) fusion(f32[10,16,2048]{2,1,0:T(8,128)} %param.6), kind=kLoop, calls=%fused_computation.67 | loop fusion | bytes 2949120 | tf_op jit(solution)/shard_map/slice | solution.py:25
  3.1 3.2 %collective-permute-start.1 = (f32[10,9,2048]{2,0,1:T(8,128)S(1)}, f32[10,9,2048]{2,0,1:T(8,128)S(1)}, u32[]{:S(2)}, u32[]{:S(2)}) collective-permute-start(f32[10,9,2048]{2,0,1:T(8,128)S(1)} %copy.22), channel_id=1, source_target_pairs={{1,0},{2,1},{3,2},{4,3},{5,4},{6,5},{7,6},{0,7},{9,8},{10,9},{11,1... | collective-permute-start | bytes 2211848 | tf_op jit(solution)/shard_map/ppermute | solution.py:27
  7.2 0.6 fusion.25
  17.6 0.6 slice_bitcast_fusion.7
  18.2 0.8 copy.18
  19.0 1.6 broadcast_in_dim.64
  20.6 0.7 pad_maximum_fusion.1
  21.3 0.8 copy.16
  22.1 1.6 broadcast_in_dim.57
  23.7 33.9 %collective-permute-done.1 = f32[10,9,2048]{2,0,1:T(8,128)S(1)} collective-permute-done((f32[10,9,2048]{2,0,1:T(8,128)S(1)}, f32[10,9,2048]{2,0,1:T(8,128)S(1)}, u32[]{:S(2)}, u32[]{:S(2)}) %collective-permute-start.1) | collective-permute-done | bytes 737312 | tf_op jit(solution)/shard_map/ppermute | solution.py:27
  58.1 1.7 copy.14
  60.3 5.0 %multiply_add_fusion = (f32[10,18,2048]{2,1,0:T(8,128)S(1)}, f32[10,18,2048]{2,1,0:T(8,128)S(1)}, f32[10,18,2048]{2,1,0:T(8,128)S(1)}) fusion(f32[10,34,2048]{2,1,0:T(8,128)S(1)} %pad_maximum_fusion, s32[]{:T(128)S(6)} %select_n.89, s32[]{:T(128)S(6)} %select_n.88, s32[]{:T(128)S(6)} %select_n.87, s32[]{:T(128)S(6)} %select_n.86, s32[]{:T(128)S(6)} %select_n.85, ...), kind=kLoop, calls=%fused_computation.11 | loop fusion | flops 9216000 | bytes 23593008 | tf_op jit(solution)/shard_map/add | solution.py:39
  65.4 1.7 fusion.21
  67.2 5.4 %collective-permute-start.7 = (f32[9,18,2048]{2,1,0:T(8,128)S(1)}, f32[9,18,2048]{2,1,0:T(8,128)S(1)}, u32[]{:S(2)}, u32[]{:S(2)}) collective-permute-start(f32[9,18,2048]{2,1,0:T(8,128)S(1)} %get-tuple-element.23), channel_id=1, source_target_pairs={{8,0},{16,8},{24,16},{32,24},{40,32},{48,40},{56,48},{64,56},{72,6... | collective-permute-start | bytes 3981320 | tf_op jit(solution)/shard_map/ppermute | solution.py:173
  73.3 2.2 %fusion.22 = (f32[9,18,2048]{2,1,0:T(8,128)}, f32[9,18,2048]{2,1,0:T(8,128)}) fusion(f32[10,18,2048]{2,1,0:T(8,128)S(1)} %get-tuple-element.21.refs_2_), kind=kLoop, calls=%fused_computation.65 | loop fusion | bytes 5308416 | tf_op jit(solution)/shard_map/slice | solution.py:173
  75.4 3.9 %collective-permute-start.5 = (f32[9,18,2048]{2,1,0:T(8,128)}, f32[9,18,2048]{2,1,0:T(8,128)}, u32[]{:S(2)}, u32[]{:S(2)}) collective-permute-start(f32[9,18,2048]{2,1,0:T(8,128)} %get-tuple-element.25), channel_id=1, source_target_pairs={{8,0},{16,8},{24,16},{32,24},{40,32},{48,40},{56,48},{64,56},{72,6... | collective-permute-start | bytes 3981320 | tf_op jit(solution)/shard_map/ppermute | solution.py:173
  79.7 3.9 %collective-permute-start.3 = (f32[9,18,2048]{2,1,0:T(8,128)S(1)}, f32[9,18,2048]{2,1,0:T(8,128)}, u32[]{:S(2)}, u32[]{:S(2)}) collective-permute-start(f32[9,18,2048]{2,1,0:T(8,128)S(1)} %get-tuple-element.27), channel_id=1, source_target_pairs={{8,0},{16,8},{24,16},{32,24},{40,32},{48,40},{56,48},{64,56},{72,6... | collective-permute-start | bytes 3981320 | tf_op jit(solution)/shard_map/ppermute | solution.py:173
  83.7 9.1 %collective-permute-done.7.refs_3_ = f32[9,18,2048]{2,1,0:T(8,128)S(1)} collective-permute-done((f32[9,18,2048]{2,1,0:T(8,128)S(1)}, f32[9,18,2048]{2,1,0:T(8,128)S(1)}, u32[]{:S(2)}, u32[]{:S(2)}) %collective-permute-start.7) | collective-permute-done | bytes 1327136 | tf_op jit(solution)/shard_map/ppermute | solution.py:173
  92.7 1.2 copy-done.4
  94.5 0.8 broadcast_in_dim.66
  95.3 1.6 eq.107
  96.9 1.4 broadcast_in_dim.60
  98.3 1.6 eq.99
  100.0 0.8 copy.19
  100.8 1.6 broadcast_in_dim.67
  102.4 0.8 copy.17
  103.2 1.6 broadcast_in_dim.61
  104.8 1.4 broadcast_in_dim.63
  106.2 1.6 eq.103
  107.9 0.8 broadcast_in_dim.56
  108.6 1.6 eq.95
  110.2 0.8 iota_add_fusion
  111.0 1.0 add.341
  112.0 0.7 broadcast_multiply_fusion
  112.7 1.3 add.351
  114.1 12.9 %shard_map.77 = (f32[10,16,2048]{2,1,0:T(8,128)}, f32[10,16,2048]{2,1,0:T(8,128)}) custom-call(s32[3]{0:T(128)} %refs_0_.5, f32[9,18,2048]{2,1,0:T(8,128)} %collective-permute-done.6.refs_1_, f32[10,18,2048]{2,1,0:T(8,128)} %copy-done, f32[9,18,2048]{2,1,0:T(8,128)} %copy-done.4), custom_call_target="tpu_custom_call" | custom-call | tf_op jit(solution)/shard_map/pallas_call | solution.py:151
  127.1 3.7 %fusion.12 = f32[512]{0:T(512)} fusion(f32[160,2048]{1,0:T(8,128)} %bitcast.58, s32[512]{0:T(512)S(1)} %add_select_fusion, f32[512]{0:T(512)S(1)} %copy-done.11, s32[512]{0:T(512)S(1)} %copy-done.9, f32[512]{0:T(512)S(1)} %copy-done.7, s32[512]{0:T(512)S(1)} %copy-done.17, f32[512]{0:T(512)S(1)} %copy-done.14, s32[512]{0:T(512)S(1)} %copy-done.10, ...), kind=kOutput, calls=%fused_computation.19 | convolution fusion | flops 2015378944 | bytes 1331200 | tf_op jit(solution)/shard_map/dot_general | solution.py:265
  130.8 1.5 reshape.129
  132.3 13.7 %shard_map.78 = (f32[10,16,2048]{2,1,0:T(8,128)}, f32[10,16,2048]{2,1,0:T(8,128)}) custom-call(s32[3]{0:T(128)} %refs_0_.5, f32[9,18,2048]{2,1,0:T(8,128)} %collective-permute-done.4.refs_1_, f32[10,18,2048]{2,1,0:T(8,128)} %copy-done.2, f32[9,18,2048]{2,1,0:T(8,128)} %collective-permute-done.5.refs_3_, f32[10,16,2048]{2,1,0:T(8,128)} %get-tuple-element.8.refs_4_), custom_call_target="tpu_custom_call" | custom-call | tf_op jit(solution)/shard_map/pallas_call | solution.py:151
  146.1 3.7 %fusion.11 = f32[512]{0:T(512)} fusion(f32[160,2048]{1,0:T(8,128)} %bitcast.57, s32[512]{0:T(512)S(1)} %copy-done.24, f32[512]{0:T(512)S(1)} %copy-done.12, s32[512]{0:T(512)S(1)} %copy-done.9, f32[512]{0:T(512)S(1)} %copy-done.7, s32[512]{0:T(512)S(1)} %copy-done.18, f32[512]{0:T(512)S(1)} %copy-done.15, s32[512]{0:T(512)S(1)} %copy-done.10, ...), kind=kOutput, calls=%fused_computation.18 | convolution fusion | flops 2015378944 | bytes 1331200 | tf_op jit(solution)/shard_map/dot_general | solution.py:265
  149.8 1.5 reshape.131
  151.2 1.6 reduce_sum.64
  152.8 1.6 reduce_sum.66
  154.5 13.6 %shard_map.79 = (f32[10,16,2048]{2,1,0:T(8,128)}, f32[10,16,2048]{2,1,0:T(8,128)}) custom-call(s32[3]{0:T(128)} %refs_0_.5, f32[9,18,2048]{2,1,0:T(8,128)} %collective-permute-done.2.refs_1_, f32[10,18,2048]{2,1,0:T(8,128)} %copy-done.1, f32[9,18,2048]{2,1,0:T(8,128)} %collective-permute-done.3.refs_3_, f32[10,16,2048]{2,1,0:T(8,128)} %get-tuple-element.9.refs_4_), custom_call_target="tpu_custom_call" | custom-call | tf_op jit(solution)/shard_map/pallas_call | solution.py:151
  168.2 3.1 %fusion.10 = f32[512]{0:T(512)S(1)} fusion(f32[160,2048]{1,0:T(8,128)} %bitcast.56, s32[512]{0:T(512)S(1)} %copy-done.25, f32[512]{0:T(512)S(1)} %copy-done.13, s32[512]{0:T(512)S(1)} %copy-done.9, f32[512]{0:T(512)S(1)} %copy-done.7, s32[512]{0:T(512)S(1)} %copy-done.19, f32[512]{0:T(512)S(1)} %copy-done.16, s32[512]{0:T(512)S(1)} %copy-done.10, ...), kind=kOutput, calls=%fused_computation.17 | convolution fusion | flops 2015378944 | bytes 1331200 | tf_op jit(solution)/shard_map/dot_general | solution.py:265
  171.6 0.8 fusion.6
  172.4 14.8 %all_to_all.5 = f32[3,8,256]{2,0,1:T(4,128)S(1)} all-to-all(f32[3,8,256]{2,0,1:T(4,128)S(1)} %bitcast.51), channel_id=1, replica_groups=mesh['gz'=32,'gy'=8] {'gy'}, dimensions={1} | all-to-all | bytes 49152 | tf_op jit(solution)/shard_map/all_to_all | solution.py:280
  187.2 0.6 reduce_sum.69
  (80 shorter events, 4.3 us)
Async XLA Ops:
  2.6 4.6 %copy-start.5 = (s32[3]{0:T(128)S(1)}, s32[3]{0:T(128)}, u32[]{:S(2)}) copy-start(s32[3]{0:T(128)} %refs_0_.5) | copy-start | bytes 40
  2.6 14.9 %copy-start.6 = (f32[8,256]{1,0:T(8,128)S(1)}, f32[8,256]{1,0:T(8,128)}, u32[]{:S(2)}) copy-start(f32[8,256]{1,0:T(8,128)} %param.11) | copy-start | bytes 24580
  3.1 54.6 %collective-permute-start.1 = (f32[10,9,2048]{2,0,1:T(8,128)S(1)}, f32[10,9,2048]{2,0,1:T(8,128)S(1)}, u32[]{:S(2)}, u32[]{:S(2)}) collective-permute-start(f32[10,9,2048]{2,0,1:T(8,128)S(1)} %copy.22), channel_id=1, source_target_pairs={{1,0},{2,1},{3,2},{4,3},{5,4},{6,5},{7,6},{0,7},{9,8},{10,9},{11,1... | collective-permute-start | bytes 2211848 | tf_op jit(solution)/shard_map/ppermute | solution.py:27
  6.8 51.3 %collective-permute-start = (f32[10,9,2048]{2,0,1:T(8,128)S(1)}, f32[10,9,2048]{2,0,1:T(8,128)}, u32[]{:S(2)}, u32[]{:S(2)}) collective-permute-start(f32[10,9,2048]{2,0,1:T(8,128)S(1)} %copy.21), channel_id=1, source_target_pairs={{0,1},{1,2},{2,3},{3,4},{4,5},{5,6},{6,7},{7,0},{8,9},{9,10},{10,1... | collective-permute-start | bytes 2211848 | tf_op jit(solution)/shard_map/ppermute | solution.py:24
  23.7 36.1 %copy-start.3 = (f32[10,16,2048]{2,1,0:T(8,128)S(1)}, f32[10,16,2048]{2,1,0:T(8,128)}, u32[]{:S(2)}) copy-start(f32[10,16,2048]{2,1,0:T(8,128)} %param.6) | copy-start | bytes 3932164
  65.4 1.9 copy-start
  65.4 7.9 %copy-start.2 = (f32[10,18,2048]{2,1,0:T(8,128)}, f32[10,18,2048]{2,1,0:T(8,128)S(1)}, u32[]{:S(2)}) copy-start(f32[10,18,2048]{2,1,0:T(8,128)S(1)} %get-tuple-element.21.refs_2_) | copy-start | bytes 4423684
  65.4 13.9 %copy-start.1 = (f32[10,18,2048]{2,1,0:T(8,128)}, f32[10,18,2048]{2,1,0:T(8,128)S(1)}, u32[]{:S(2)}) copy-start(f32[10,18,2048]{2,1,0:T(8,128)S(1)} %get-tuple-element.22.refs_2_) | copy-start | bytes 4423684
  65.4 7.3 %copy-start.29 = (s32[256]{0:T(256)S(1)}, s32[256]{0:T(256)}, u32[]{:S(2)}) copy-start(s32[256]{0:T(256)} %param.10) | copy-start | bytes 3076
  67.2 25.5 %collective-permute-start.7 = (f32[9,18,2048]{2,1,0:T(8,128)S(1)}, f32[9,18,2048]{2,1,0:T(8,128)S(1)}, u32[]{:S(2)}, u32[]{:S(2)}) collective-permute-start(f32[9,18,2048]{2,1,0:T(8,128)S(1)} %get-tuple-element.23), channel_id=1, source_target_pairs={{8,0},{16,8},{24,16},{32,24},{40,32},{48,40},{56,48},{64,56},{72,6... | collective-permute-start | bytes 3981320 | tf_op jit(solution)/shard_map/ppermute | solution.py:173
  73.2 40.8 %collective-permute-start.6 = (f32[9,18,2048]{2,1,0:T(8,128)}, f32[9,18,2048]{2,1,0:T(8,128)}, u32[]{:S(2)}, u32[]{:S(2)}) collective-permute-start(f32[9,18,2048]{2,1,0:T(8,128)} %get-tuple-element.24), channel_id=1, source_target_pairs={{0,8},{8,16},{16,24},{24,32},{32,40},{40,48},{48,56},{56,64},{64,7... | collective-permute-start | bytes 3981320 | tf_op jit(solution)/shard_map/ppermute | solution.py:172
  75.4 56.9 %collective-permute-start.5 = (f32[9,18,2048]{2,1,0:T(8,128)}, f32[9,18,2048]{2,1,0:T(8,128)}, u32[]{:S(2)}, u32[]{:S(2)}) collective-permute-start(f32[9,18,2048]{2,1,0:T(8,128)} %get-tuple-element.25), channel_id=1, source_target_pairs={{8,0},{16,8},{24,16},{32,24},{40,32},{48,40},{56,48},{64,56},{72,6... | collective-permute-start | bytes 3981320 | tf_op jit(solution)/shard_map/ppermute | solution.py:173
  79.3 53.0 %collective-permute-start.4 = (f32[9,18,2048]{2,1,0:T(8,128)}, f32[9,18,2048]{2,1,0:T(8,128)}, u32[]{:S(2)}, u32[]{:S(2)}) collective-permute-start(f32[9,18,2048]{2,1,0:T(8,128)} %get-tuple-element.26), channel_id=1, source_target_pairs={{0,8},{8,16},{16,24},{24,32},{32,40},{40,48},{48,56},{56,64},{64,7... | collective-permute-start | bytes 3981320 | tf_op jit(solution)/shard_map/ppermute | solution.py:172
  79.7 74.7 %collective-permute-start.3 = (f32[9,18,2048]{2,1,0:T(8,128)S(1)}, f32[9,18,2048]{2,1,0:T(8,128)}, u32[]{:S(2)}, u32[]{:S(2)}) collective-permute-start(f32[9,18,2048]{2,1,0:T(8,128)S(1)} %get-tuple-element.27), channel_id=1, source_target_pairs={{8,0},{16,8},{24,16},{32,24},{40,32},{48,40},{56,48},{64,56},{72,6... | collective-permute-start | bytes 3981320 | tf_op jit(solution)/shard_map/ppermute | solution.py:173
  92.7 1.2 copy-start.4
  92.7 61.7 %collective-permute-start.2 = (f32[9,18,2048]{2,1,0:T(8,128)S(1)}, f32[9,18,2048]{2,1,0:T(8,128)}, u32[]{:S(2)}, u32[]{:S(2)}) collective-permute-start(f32[9,18,2048]{2,1,0:T(8,128)S(1)} %get-tuple-element.28), channel_id=1, source_target_pairs={{0,8},{8,16},{16,24},{24,32},{32,40},{40,48},{48,56},{56,64},{64,7... | collective-permute-start | bytes 3981320 | tf_op jit(solution)/shard_map/ppermute | solution.py:172
  114.0 13.0 %copy-start.23 = (s32[512]{0:T(512)}, s32[512]{0:T(512)S(1)}, u32[]{:S(2)}) copy-start(s32[512]{0:T(512)S(1)} %add_select_fusion) | copy-start | bytes 6148
  114.0 13.0 %copy-start.7 = (f32[512]{0:T(512)S(1)}, f32[512]{0:T(512)}, u32[]{:S(2)}) copy-start(f32[512]{0:T(512)} %broadcast_in_dim.64) | copy-start | bytes 6148
  114.0 13.0 %copy-start.8 = (f32[512]{0:T(512)S(1)}, f32[512]{0:T(512)}, u32[]{:S(2)}) copy-start(f32[512]{0:T(512)} %broadcast_in_dim.57) | copy-start | bytes 6148
  114.0 13.0 %copy-start.9 = (s32[512]{0:T(512)S(1)}, s32[512]{0:T(512)}, u32[]{:S(2)}) copy-start(s32[512]{0:T(512)} %eq.107) | copy-start | bytes 6148
  114.0 13.0 %copy-start.10 = (s32[512]{0:T(512)S(1)}, s32[512]{0:T(512)}, u32[]{:S(2)}) copy-start(s32[512]{0:T(512)} %eq.99) | copy-start | bytes 6148
  114.0 13.0 %copy-start.11 = (f32[512]{0:T(512)S(1)}, f32[512]{0:T(512)}, u32[]{:S(2)}) copy-start(f32[512]{0:T(512)} %broadcast_in_dim.67) | copy-start | bytes 6148
  114.0 13.0 %copy-start.14 = (f32[512]{0:T(512)S(1)}, f32[512]{0:T(512)}, u32[]{:S(2)}) copy-start(f32[512]{0:T(512)} %broadcast_in_dim.61) | copy-start | bytes 6148
  114.1 13.0 %copy-start.17 = (s32[512]{0:T(512)S(1)}, s32[512]{0:T(512)}, u32[]{:S(2)}) copy-start(s32[512]{0:T(512)} %eq.103) | copy-start | bytes 6148
  114.1 13.0 %copy-start.20 = (s32[512]{0:T(512)S(1)}, s32[512]{0:T(512)}, u32[]{:S(2)}) copy-start(s32[512]{0:T(512)} %eq.95) | copy-start | bytes 6148
  132.3 13.7 %copy-start.12 = (f32[512]{0:T(512)S(1)}, f32[512]{0:T(512)}, u32[]{:S(2)}) copy-start(f32[512]{0:T(512)} %broadcast_in_dim.67) | copy-start | bytes 6148
  132.3 13.8 %copy-start.15 = (f32[512]{0:T(512)S(1)}, f32[512]{0:T(512)}, u32[]{:S(2)}) copy-start(f32[512]{0:T(512)} %broadcast_in_dim.61) | copy-start | bytes 6148
  132.3 13.8 %copy-start.18 = (s32[512]{0:T(512)S(1)}, s32[512]{0:T(512)}, u32[]{:S(2)}) copy-start(s32[512]{0:T(512)} %eq.103) | copy-start | bytes 6148
  132.3 13.8 %copy-start.21 = (s32[512]{0:T(512)S(1)}, s32[512]{0:T(512)}, u32[]{:S(2)}) copy-start(s32[512]{0:T(512)} %eq.95) | copy-start | bytes 6148
  132.3 13.8 %copy-start.24 = (s32[512]{0:T(512)S(1)}, s32[512]{0:T(512)}, u32[]{:S(2)}) copy-start(s32[512]{0:T(512)} %copy-done.23) | copy-start | bytes 6148
  154.4 13.7 %copy-start.13 = (f32[512]{0:T(512)S(1)}, f32[512]{0:T(512)}, u32[]{:S(2)}) copy-start(f32[512]{0:T(512)} %broadcast_in_dim.67) | copy-start | bytes 6148
  154.4 13.7 %copy-start.16 = (f32[512]{0:T(512)S(1)}, f32[512]{0:T(512)}, u32[]{:S(2)}) copy-start(f32[512]{0:T(512)} %broadcast_in_dim.61) | copy-start | bytes 6148
  154.4 13.7 %copy-start.19 = (s32[512]{0:T(512)S(1)}, s32[512]{0:T(512)}, u32[]{:S(2)}) copy-start(s32[512]{0:T(512)} %eq.103) | copy-start | bytes 6148
  154.5 13.7 %copy-start.22 = (s32[512]{0:T(512)S(1)}, s32[512]{0:T(512)}, u32[]{:S(2)}) copy-start(s32[512]{0:T(512)} %eq.95) | copy-start | bytes 6148
  154.5 13.7 %copy-start.25 = (s32[512]{0:T(512)S(1)}, s32[512]{0:T(512)}, u32[]{:S(2)}) copy-start(s32[512]{0:T(512)} %copy-done.23) | copy-start | bytes 6148
  168.1 3.4 %copy-start.26 = (f32[256]{0:T(256)S(1)}, f32[256]{0:T(256)}, u32[]{:S(2)}) copy-start(f32[256]{0:T(256)} %reduce_sum.64) | copy-start | bytes 3076
  168.1 3.4 %copy-start.27 = (f32[256]{0:T(256)S(1)}, f32[256]{0:T(256)}, u32[]{:S(2)}) copy-start(f32[256]{0:T(256)} %reduce_sum.66) | copy-start | bytes 3076
  168.1 3.4 %copy-start.28 = (s32[256]{0:T(256)S(1)}, s32[256]{0:T(256)}, u32[]{:S(2)}) copy-start(s32[256]{0:T(256)} %add.351) | copy-start | bytes 3076

commit v2 on v1

--- a/solution.py
+++ b/solution.py
@@ -244,8 +244,7 @@
     y_index = remainder // row_length
     x_index = remainder % row_length
     entries = base_cell.shape[0]
-    steps = jnp.arange(2, dtype=jnp.int32)
-    target_x = ((x_index[:, None] + steps[None, :]) % row_length).reshape(-1)
+    target_x = jnp.concatenate([x_index, (x_index + 1) % row_length])
     pick_x = (
         jnp.arange(row_length, dtype=jnp.int32)[:, None] == target_x[None, :]
     ).astype(jnp.float32)
@@ -253,12 +252,10 @@
     weight_grid = None
     for step_z in (0, 1):
         for step_y in (0, 1):
-            row = jnp.repeat((z_index + step_z) * band_rows + y_index + step_y, 2)
+            row = (z_index + step_z) * band_rows + y_index + step_y
             corner = 4 * step_z + 2 * step_y
-            weights = jnp.stack(
-                [corner_weights[corner], corner_weights[corner + 1]], axis=1
-            ).reshape(-1)
-            term = jnp.where(cells == row[None, :], weights[None, :], 0.0)
+            weights = jnp.concatenate([corner_weights[corner], corner_weights[corner + 1]])
+            term = jnp.where(cells == jnp.concatenate([row, row])[None, :], weights[None, :], 0.0)
             weight_grid = term if weight_grid is None else weight_grid + term
     partials = []
     for feature in features:
@@ -266,7 +263,7 @@
             feature, pick_x, precision=lax.Precision.HIGHEST, preferred_element_type=jnp.float32
         )
         per_column = jnp.sum(picked * weight_grid, axis=0)
-        partials.append(jnp.sum(per_column.reshape(entries, 2), axis=1))
+        partials.append(per_column[:entries] + per_column[entries:])
     partial_value = jnp.stack(partials)
     owner_group = owner_rank[:, 0]
     groups = lax.axis_size("gy")

time: 189 us -> 168 us (0.89)
  local copies, waits for them, and re-layouts: 36.7 us -> 10.4 us
  waiting for transfers between devices: 43 us -> 60.5 us
  other arithmetic: 14 us -> 6.04 us
  matrix products: 11.3 us -> 7.47 us
    broadcast_in_dim x8 -> x0, local copies, waits for them, and re-layouts: 10.9 us -> none  [the longest x4 6.5 us: per_device(): term = jnp.where(cells == row[None, :], weights[None, :], 0.0)]
    ppermute x3, waiting for transfers between devices: 0.01 us -> 8.58 us  [z_neighbours(): lax.ppermute(lax.slice_in_dim(block, block.shape[0] - width, None, axis=0...]
    eq x4 -> x0, local copies, waits for them, and re-layouts: 6.52 us -> none  [per_device(): term = jnp.where(cells == row[None, :], weights[None, :], 0.0)]
    ppermute x1, waiting for transfers between devices: 33.9 us -> 40 us  [with_halo(): lax.ppermute(lax.slice_in_dim(block, 0, width, axis=dim), axis, backward)]
    dot_general x3, matrix products: 10.5 us -> 6.64 us  [per_device(): jnp.dot(feature, pick_x, precision=lax.Precision.HIGHEST, preferred_eleme...]
    another operation x5 -> x0, local copies, waits for them, and re-layouts: 3.79 us -> none  [per_device(): jnp.stack([corner_weights[corner], corner_weights[corner + 1]], axis=1)]
    reduce_sum x3 -> x0, other arithmetic: 3.31 us -> none  [per_device(): partials.append(jnp.sum(per_column.reshape(entries, 2), axis=1))]
    reshape x3 -> x0, local copies, waits for them, and re-layouts: 3.08 us -> none  [per_device(): partials.append(jnp.sum(per_column.reshape(entries, 2), axis=1))]
  transfers between devices with their start and end apart: 8 -> 8, of which waited for: 2 -> 6; matrix products, arithmetic and copies ran while one was open for 24% -> 4% of each run, Pallas kernels for 14% -> 16%
where the time goes in v2:
time: 168 us; the launch traced here: 167 us
  waiting for transfers between devices  60.5 us (36%)
  Pallas kernels  40.5 us (24%)
  starting transfers between devices  16.9 us (10%)
  blocking collectives  14.8 us (9%)
  between operations  10.7 us (6%)
  local copies, waits for them, and re-layouts  10.4 us (6%)
  matrix products  7.47 us (4%)
  other arithmetic  6.04 us (4%)
    pallas_call x3, Pallas kernels, run(): pl.pallas_call(kernel, out_shape=(block, block), in_specs=in_specs, out_s...  40.5 us
    ppermute x1, waiting for transfers between devices, with_halo(): lax.ppermute(lax.slice_in_dim(block, 0, width, axis=dim), axis, backward)  40 us
    all_to_all x1, blocking collectives, per_device(): lax.all_to_all(spread.reshape(SCALES, groups, HOWN), 'gy', split_axis=1,...  14.8 us
    ppermute x3, starting transfers between devices, z_neighbours(): lax.ppermute(lax.slice_in_dim(block, 0, width, axis=0), 'gz', backward)  13.2 us
    ppermute x3, waiting for transfers between devices, z_neighbours(): lax.ppermute(lax.slice_in_dim(block, 0, width, axis=0), 'gz', backward)  11.9 us
    ppermute x3, waiting for transfers between devices, z_neighbours(): lax.ppermute(lax.slice_in_dim(block, block.shape[0] - width, None, axis=0...  8.58 us
    dot_general x3, matrix products, per_device(): jnp.dot(feature, pick_x, precision=lax.Precision.HIGHEST, preferred_eleme...  6.64 us
    add x1, other arithmetic, smooth_padded(): running = summand if running is None else running + summand  4.9 us
  transfers between devices with their start and end apart: 8, of which 6 were waited for; matrix products, arithmetic and copies ran while one was open for 4% of the time, Pallas kernels for 16%

profile of v2, /device:TPU:2, one launch (start us, length us, event | category | flops | bytes accessed | tf_op | source)
XLA Modules:
  0.0 167.3 jit_solution(12169767133561396979)
XLA Ops:
  0.6 2.0 %fusion.24 = (f32[10,9,2048]{2,1,0:T(8,128)S(1)}, f32[10,9,2048]{2,1,0:T(8,128)S(1)}) fusion(f32[10,16,2048]{2,1,0:T(8,128)} %param.6), kind=kLoop, calls=%fused_computation.66 | loop fusion | bytes 2949120 | tf_op jit(solution)/shard_map/slice | solution.py:25
  2.7 0.0 copy-start.6
  2.7 0.0 copy-start.10
  2.7 0.0 copy-start.8
  2.7 0.0 copy-start.9
  2.7 0.4 copy.14
  3.2 3.2 %collective-permute-start.1 = (f32[10,9,2048]{2,0,1:T(8,128)S(1)}, f32[10,9,2048]{2,0,1:T(8,128)S(1)}, u32[]{:S(2)}, u32[]{:S(2)}) collective-permute-start(f32[10,9,2048]{2,0,1:T(8,128)S(1)} %copy.14), channel_id=1, source_target_pairs={{1,0},{2,1},{3,2},{4,3},{5,4},{6,5},{7,6},{0,7},{9,8},{10,9},{11,1... | collective-permute-start | bytes 2211848 | tf_op jit(solution)/shard_map/ppermute | solution.py:27
  6.4 0.4 copy.13
  6.9 0.4 collective-permute-start
  7.3 0.6 fusion.26
  17.6 0.0 copy-done.8
  17.7 0.0 copy-start.3
  17.7 40.0 %collective-permute-done.1 = f32[10,9,2048]{2,0,1:T(8,128)S(1)} collective-permute-done((f32[10,9,2048]{2,0,1:T(8,128)S(1)}, f32[10,9,2048]{2,0,1:T(8,128)S(1)}, u32[]{:S(2)}, u32[]{:S(2)}) %collective-permute-start.1) | collective-permute-done | bytes 737312 | tf_op jit(solution)/shard_map/ppermute | solution.py:27
  57.7 0.5 copy.11
  58.2 0.0 collective-permute-done
  58.2 1.7 %copy.10 = f32[10,9,2048]{2,1,0:T(8,128)S(1)} copy(f32[10,9,2048]{2,0,1:T(8,128)} %collective-permute-done) | data formatting | bytes 1474560 | tf_op jit(solution)/shard_map/ppermute | solution.py:24
  60.0 0.4 pad_maximum_fusion
  60.4 4.9 %multiply_add_fusion = (f32[10,18,2048]{2,1,0:T(8,128)S(1)}, f32[10,18,2048]{2,1,0:T(8,128)S(1)}, f32[10,18,2048]{2,1,0:T(8,128)S(1)}) fusion(f32[10,34,2048]{2,1,0:T(8,128)S(1)} %pad_maximum_fusion, s32[]{:T(128)S(6)} %select_n.83, s32[]{:T(128)S(6)} %select_n.82, s32[]{:T(128)S(6)} %select_n.81, s32[]{:T(128)S(6)} %select_n.80, s32[]{:T(128)S(6)} %select_n.79, ...), kind=kLoop, calls=%fused_computation.11 | loop fusion | flops 9216000 | bytes 23593008 | tf_op jit(solution)/shard_map/add | solution.py:39
  65.3 0.0 copy-start
  65.3 0.0 copy-start.2
  65.3 0.0 copy-start.1
  65.3 0.4 fusion.21
  65.8 0.8 copy-done
  66.6 5.4 %collective-permute-start.7 = (f32[9,18,2048]{2,1,0:T(8,128)S(1)}, f32[9,18,2048]{2,1,0:T(8,128)S(1)}, u32[]{:S(2)}, u32[]{:S(2)}) collective-permute-start(f32[9,18,2048]{2,1,0:T(8,128)S(1)} %get-tuple-element.25), channel_id=1, source_target_pairs={{8,0},{16,8},{24,16},{32,24},{40,32},{48,40},{56,48},{64,56},{72,6... | collective-permute-start | bytes 3981320 | tf_op jit(solution)/shard_map/ppermute | solution.py:173
  72.0 0.0 collective-permute-start.6
  72.0 0.4 fusion.22
  72.5 3.9 %collective-permute-start.5 = (f32[9,18,2048]{2,1,0:T(8,128)S(1)}, f32[9,18,2048]{2,1,0:T(8,128)}, u32[]{:S(2)}, u32[]{:S(2)}) collective-permute-start(f32[9,18,2048]{2,1,0:T(8,128)S(1)} %get-tuple-element.27), channel_id=1, source_target_pairs={{8,0},{16,8},{24,16},{32,24},{40,32},{48,40},{56,48},{64,56},{72,6... | collective-permute-start | bytes 3981320 | tf_op jit(solution)/shard_map/ppermute | solution.py:173
  76.4 0.0 collective-permute-start.4
  76.4 0.0 copy-start.7
  76.5 1.8 %fusion.23 = (f32[9,18,2048]{2,1,0:T(8,128)}, f32[9,18,2048]{2,1,0:T(8,128)S(1)}) fusion(f32[10,18,2048]{2,1,0:T(8,128)S(1)} %get-tuple-element.24.refs_2_), kind=kLoop, calls=%fused_computation.65 | loop fusion | bytes 5308416 | tf_op jit(solution)/shard_map/slice | solution.py:173
  78.2 3.8 %collective-permute-start.3 = (f32[9,18,2048]{2,1,0:T(8,128)}, f32[9,18,2048]{2,1,0:T(8,128)S(1)}, u32[]{:S(2)}, u32[]{:S(2)}) collective-permute-start(f32[9,18,2048]{2,1,0:T(8,128)} %get-tuple-element.29), channel_id=1, source_target_pairs={{8,0},{16,8},{24,16},{32,24},{40,32},{48,40},{56,48},{64,56},{72,6... | collective-permute-start | bytes 3981320 | tf_op jit(solution)/shard_map/ppermute | solution.py:173
  82.1 10.0 %collective-permute-done.7.refs_3_ = f32[9,18,2048]{2,1,0:T(8,128)S(1)} collective-permute-done((f32[9,18,2048]{2,1,0:T(8,128)S(1)}, f32[9,18,2048]{2,1,0:T(8,128)S(1)}, u32[]{:S(2)}, u32[]{:S(2)}) %collective-permute-start.7) | collective-permute-done | bytes 1327136 | tf_op jit(solution)/shard_map/ppermute | solution.py:173
  92.1 0.0 collective-permute-start.2
  92.1 1.2 copy-done.5
  93.3 2.9 %collective-permute-done.6.refs_1_ = f32[9,18,2048]{2,1,0:T(8,128)} collective-permute-done((f32[9,18,2048]{2,1,0:T(8,128)S(1)}, f32[9,18,2048]{2,1,0:T(8,128)}, u32[]{:S(2)}, u32[]{:S(2)}) %collective-permute-start.6) | collective-permute-done | bytes 1327136 | tf_op jit(solution)/shard_map/ppermute | solution.py:172
  96.2 13.0 %shard_map.77 = (f32[10,16,2048]{2,1,0:T(8,128)}, f32[10,16,2048]{2,1,0:T(8,128)}) custom-call(s32[3]{0:T(128)} %refs_0_.5, f32[9,18,2048]{2,1,0:T(8,128)} %collective-permute-done.6.refs_1_, f32[10,18,2048]{2,1,0:T(8,128)} %copy-done, f32[9,18,2048]{2,1,0:T(8,128)} %copy-done.5), custom_call_target="tpu_custom_call" | custom-call | tf_op jit(solution)/shard_map/pallas_call | solution.py:151
  109.1 1.9 %collective-permute-done.5.refs_3_ = f32[9,18,2048]{2,1,0:T(8,128)} collective-permute-done((f32[9,18,2048]{2,1,0:T(8,128)S(1)}, f32[9,18,2048]{2,1,0:T(8,128)}, u32[]{:S(2)}, u32[]{:S(2)}) %collective-permute-start.5) | collective-permute-done | bytes 1327136 | tf_op jit(solution)/shard_map/ppermute | solution.py:173
  111.0 4.1 %collective-permute-done.4.refs_1_ = f32[9,18,2048]{2,1,0:T(8,128)} collective-permute-done((f32[9,18,2048]{2,1,0:T(8,128)S(1)}, f32[9,18,2048]{2,1,0:T(8,128)}, u32[]{:S(2)}, u32[]{:S(2)}) %collective-permute-start.4) | collective-permute-done | bytes 1327136 | tf_op jit(solution)/shard_map/ppermute | solution.py:172
  115.1 13.7 %shard_map.78 = (f32[10,16,2048]{2,1,0:T(8,128)}, f32[10,16,2048]{2,1,0:T(8,128)}) custom-call(s32[3]{0:T(128)} %refs_0_.5, f32[9,18,2048]{2,1,0:T(8,128)} %collective-permute-done.4.refs_1_, f32[10,18,2048]{2,1,0:T(8,128)} %copy-done.2, f32[9,18,2048]{2,1,0:T(8,128)} %collective-permute-done.5.refs_3_, f32[10,16,2048]{2,1,0:T(8,128)} %get-tuple-element.8.refs_4_), custom_call_target="tpu_custom_call" | custom-call | tf_op jit(solution)/shard_map/pallas_call | solution.py:151
  128.9 1.8 %fusion.12 = f32[512]{0:T(512)S(1)} fusion(f32[160,2048]{1,0:T(8,128)S(1)} %bitcast.56, s32[512]{0:T(512)S(1)} %get-tuple-element.46, f32[512]{0:T(512)S(1)} %get-tuple-element.53, s32[512]{0:T(512)S(1)} %pad_add_fusion.4, f32[512]{0:T(512)S(1)} %get-tuple-element.52, s32[512]{0:T(512)S(1)} %get-tuple-element.49, f32[512]{0:T(512)S(1)} %get-tuple-element.51, ...), kind=kOutput, calls=%fused_computation.19 | convolution fusion | flops 2015378944 | bytes 1331200 | tf_op jit(solution)/shard_map/dot_general | solution.py:262
  130.7 1.8 %fusion.11 = f32[512]{0:T(512)S(1)} fusion(f32[160,2048]{1,0:T(8,128)S(1)} %bitcast.57, s32[512]{0:T(512)S(1)} %get-tuple-element.46, f32[512]{0:T(512)S(1)} %get-tuple-element.53, s32[512]{0:T(512)S(1)} %pad_add_fusion.4, f32[512]{0:T(512)S(1)} %get-tuple-element.52, s32[512]{0:T(512)S(1)} %get-tuple-element.49, f32[512]{0:T(512)S(1)} %get-tuple-element.51, ...), kind=kOutput, calls=%fused_computation.18 | convolution fusion | flops 2015378944 | bytes 1331200 | tf_op jit(solution)/shard_map/dot_general | solution.py:262
  132.5 0.0 collective-permute-done.3.refs_3_
  132.5 1.6 collective-permute-done.2.refs_1_
  134.1 13.9 %shard_map.79 = (f32[10,16,2048]{2,1,0:T(8,128)}, f32[10,16,2048]{2,1,0:T(8,128)}) custom-call(s32[3]{0:T(128)} %refs_0_.5, f32[9,18,2048]{2,1,0:T(8,128)} %collective-permute-done.2.refs_1_, f32[10,18,2048]{2,1,0:T(8,128)} %copy-done.1, f32[9,18,2048]{2,1,0:T(8,128)} %copy-done.4, f32[10,16,2048]{2,1,0:T(8,128)} %get-tuple-element.9.refs_4_), custom_call_target="tpu_custom_call" | custom-call | tf_op jit(solution)/shard_map/pallas_call | solution.py:151
  148.0 3.1 %fusion.10 = f32[512]{0:T(512)S(1)} fusion(f32[160,2048]{1,0:T(8,128)} %bitcast.58, s32[512]{0:T(512)S(1)} %get-tuple-element.46, f32[512]{0:T(512)S(1)} %get-tuple-element.53, s32[512]{0:T(512)S(1)} %pad_add_fusion.4, f32[512]{0:T(512)S(1)} %get-tuple-element.52, s32[512]{0:T(512)S(1)} %get-tuple-element.49, f32[512]{0:T(512)S(1)} %get-tuple-element.51, ...), kind=kOutput, calls=%fused_computation.17 | convolution fusion | flops 2015378944 | bytes 1331200 | tf_op jit(solution)/shard_map/dot_general | solution.py:262
  151.1 0.8 fusion.6
  151.9 14.8 %all_to_all.5 = f32[3,8,256]{2,0,1:T(4,128)S(1)} all-to-all(f32[3,8,256]{2,0,1:T(4,128)S(1)} %bitcast.43), channel_id=1, replica_groups=mesh['gz'=32,'gy'=8] {'gy'}, dimensions={1} | all-to-all | bytes 49152 | tf_op jit(solution)/shard_map/all_to_all | solution.py:277
  166.7 0.6 reduce_sum.39
  (27 shorter events, 0.1 us)
Async XLA Ops:
  2.7 4.6 %copy-start.6 = (s32[3]{0:T(128)S(1)}, s32[3]{0:T(128)}, u32[]{:S(2)}) copy-start(s32[3]{0:T(128)} %refs_0_.5) | copy-start | bytes 40
  2.7 14.9 %copy-start.10 = (s32[256,1]{0,1:T(1,128)S(1)}, s32[256,1]{0,1:T(1,128)}, u32[]{:S(2)}) copy-start(s32[256,1]{0,1:T(1,128)} %param.8) | copy-start | bytes 3076
  2.7 14.9 %copy-start.8 = (s32[256]{0:T(256)S(1)}, s32[256]{0:T(256)}, u32[]{:S(2)}) copy-start(s32[256]{0:T(256)} %param.9) | copy-start | bytes 3076
  2.7 15.0 %copy-start.9 = (s32[256]{0:T(256)S(1)}, s32[256]{0:T(256)}, u32[]{:S(2)}) copy-start(s32[256]{0:T(256)} %param.10) | copy-start | bytes 3076
  3.2 54.6 %collective-permute-start.1 = (f32[10,9,2048]{2,0,1:T(8,128)S(1)}, f32[10,9,2048]{2,0,1:T(8,128)S(1)}, u32[]{:S(2)}, u32[]{:S(2)}) collective-permute-start(f32[10,9,2048]{2,0,1:T(8,128)S(1)} %copy.14), channel_id=1, source_target_pairs={{1,0},{2,1},{3,2},{4,3},{5,4},{6,5},{7,6},{0,7},{9,8},{10,9},{11,1... | collective-permute-start | bytes 2211848 | tf_op jit(solution)/shard_map/ppermute | solution.py:27
  6.9 51.3 %collective-permute-start = (f32[10,9,2048]{2,0,1:T(8,128)S(1)}, f32[10,9,2048]{2,0,1:T(8,128)}, u32[]{:S(2)}, u32[]{:S(2)}) collective-permute-start(f32[10,9,2048]{2,0,1:T(8,128)S(1)} %copy.13), channel_id=1, source_target_pairs={{0,1},{1,2},{2,3},{3,4},{4,5},{5,6},{6,7},{7,0},{8,9},{9,10},{10,1... | collective-permute-start | bytes 2211848 | tf_op jit(solution)/shard_map/ppermute | solution.py:24
  17.7 42.2 %copy-start.3 = (f32[10,16,2048]{2,1,0:T(8,128)S(1)}, f32[10,16,2048]{2,1,0:T(8,128)}, u32[]{:S(2)}) copy-start(f32[10,16,2048]{2,1,0:T(8,128)} %param.6) | copy-start | bytes 3932164
  65.3 1.3 copy-start
  65.3 6.7 %copy-start.2 = (f32[10,18,2048]{2,1,0:T(8,128)}, f32[10,18,2048]{2,1,0:T(8,128)S(1)}, u32[]{:S(2)}) copy-start(f32[10,18,2048]{2,1,0:T(8,128)S(1)} %get-tuple-element.23.refs_2_) | copy-start | bytes 4423684
  65.3 11.1 %copy-start.1 = (f32[10,18,2048]{2,1,0:T(8,128)}, f32[10,18,2048]{2,1,0:T(8,128)S(1)}, u32[]{:S(2)}) copy-start(f32[10,18,2048]{2,1,0:T(8,128)S(1)} %get-tuple-element.24.refs_2_) | copy-start | bytes 4423684
  66.6 25.5 %collective-permute-start.7 = (f32[9,18,2048]{2,1,0:T(8,128)S(1)}, f32[9,18,2048]{2,1,0:T(8,128)S(1)}, u32[]{:S(2)}, u32[]{:S(2)}) collective-permute-start(f32[9,18,2048]{2,1,0:T(8,128)S(1)} %get-tuple-element.25), channel_id=1, source_target_pairs={{8,0},{16,8},{24,16},{32,24},{40,32},{48,40},{56,48},{64,56},{72,6... | collective-permute-start | bytes 3981320 | tf_op jit(solution)/shard_map/ppermute | solution.py:173
  72.0 24.2 %collective-permute-start.6 = (f32[9,18,2048]{2,1,0:T(8,128)S(1)}, f32[9,18,2048]{2,1,0:T(8,128)}, u32[]{:S(2)}, u32[]{:S(2)}) collective-permute-start(f32[9,18,2048]{2,1,0:T(8,128)S(1)} %get-tuple-element.26), channel_id=1, source_target_pairs={{0,8},{8,16},{16,24},{24,32},{32,40},{40,48},{48,56},{56,64},{64,7... | collective-permute-start | bytes 3981320 | tf_op jit(solution)/shard_map/ppermute | solution.py:172
  72.5 38.6 %collective-permute-start.5 = (f32[9,18,2048]{2,1,0:T(8,128)S(1)}, f32[9,18,2048]{2,1,0:T(8,128)}, u32[]{:S(2)}, u32[]{:S(2)}) collective-permute-start(f32[9,18,2048]{2,1,0:T(8,128)S(1)} %get-tuple-element.27), channel_id=1, source_target_pairs={{8,0},{16,8},{24,16},{32,24},{40,32},{48,40},{56,48},{64,56},{72,6... | collective-permute-start | bytes 3981320 | tf_op jit(solution)/shard_map/ppermute | solution.py:173
  76.4 38.8 %collective-permute-start.4 = (f32[9,18,2048]{2,1,0:T(8,128)S(1)}, f32[9,18,2048]{2,1,0:T(8,128)}, u32[]{:S(2)}, u32[]{:S(2)}) collective-permute-start(f32[9,18,2048]{2,1,0:T(8,128)S(1)} %get-tuple-element.28), channel_id=1, source_target_pairs={{0,8},{8,16},{16,24},{24,32},{32,40},{40,48},{48,56},{56,64},{64,7... | collective-permute-start | bytes 3981320 | tf_op jit(solution)/shard_map/ppermute | solution.py:172
  76.4 16.8 %copy-start.7 = (f32[8,256]{1,0:T(8,128)S(1)}, f32[8,256]{1,0:T(8,128)}, u32[]{:S(2)}) copy-start(f32[8,256]{1,0:T(8,128)} %param.11) | copy-start | bytes 24580
  78.2 54.3 %collective-permute-start.3 = (f32[9,18,2048]{2,1,0:T(8,128)}, f32[9,18,2048]{2,1,0:T(8,128)S(1)}, u32[]{:S(2)}, u32[]{:S(2)}) collective-permute-start(f32[9,18,2048]{2,1,0:T(8,128)} %get-tuple-element.29), channel_id=1, source_target_pairs={{8,0},{16,8},{24,16},{32,24},{40,32},{48,40},{56,48},{64,56},{72,6... | collective-permute-start | bytes 3981320 | tf_op jit(solution)/shard_map/ppermute | solution.py:173
  92.1 1.2 copy-start.5
  92.1 42.0 %collective-permute-start.2 = (f32[9,18,2048]{2,1,0:T(8,128)S(1)}, f32[9,18,2048]{2,1,0:T(8,128)}, u32[]{:S(2)}, u32[]{:S(2)}) collective-permute-start(f32[9,18,2048]{2,1,0:T(8,128)S(1)} %get-tuple-element.30), channel_id=1, source_target_pairs={{0,8},{8,16},{16,24},{24,32},{32,40},{40,48},{48,56},{56,64},{64,7... | collective-permute-start | bytes 3981320 | tf_op jit(solution)/shard_map/ppermute | solution.py:172
  115.1 13.8 %copy-start.11 = (f32[10,16,2048]{2,1,0:T(8,128)S(1)}, f32[10,16,2048]{2,1,0:T(8,128)}, u32[]{:S(2)}) copy-start(f32[10,16,2048]{2,1,0:T(8,128)} %get-tuple-element.11) | copy-start | bytes 3932164
  128.9 1.8 %copy-start.12 = (f32[10,16,2048]{2,1,0:T(8,128)S(1)}, f32[10,16,2048]{2,1,0:T(8,128)}, u32[]{:S(2)}) copy-start(f32[10,16,2048]{2,1,0:T(8,128)} %get-tuple-element.12) | copy-start | bytes 3932164
  132.5 1.6 copy-start.4

commit v3 on v2

--- a/solution.py
+++ b/solution.py
@@ -106,7 +106,7 @@
                     - curve_zx * curve_zx
                     - curve_yx * curve_yx
                 )
-                value = (trace_sum * trace_sum / 3.0 - minor_sum) * (1.0 / (1.0 + jnp.exp(trace_sum)))
+                value = (trace_sum * trace_sum * (1.0 / 3.0) - minor_sum) / (1.0 + jnp.exp(trace_sum))
                 feature_ref[z, pl.ds(y0, 8), :] = value
                 if first:
                     best_ref[z, pl.ds(y0, 8), :] = value
@@ -265,19 +265,20 @@
         per_column = jnp.sum(picked * weight_grid, axis=0)
         partials.append(per_column[:entries] + per_column[entries:])
     partial_value = jnp.stack(partials)
-    owner_group = owner_rank[:, 0]
     groups = lax.axis_size("gy")
-    column = owner_group * HOWN + owner_slot
+    me = lax.axis_index("gy")
+    column = ((owner_rank[:, 0] - me) % groups) * HOWN + owner_slot
     onehot = (column[:, None] == jnp.arange(groups * HOWN, dtype=jnp.int32)[None, :]).astype(
         jnp.float32
     )
     spread = jnp.dot(
         partial_value, onehot, precision=lax.Precision.HIGHEST, preferred_element_type=jnp.float32
     )
-    exchanged = lax.all_to_all(
-        spread.reshape(SCALES, groups, HOWN), "gy", split_axis=1, concat_axis=1, tiled=True
-    )
-    catalogue = jnp.sum(exchanged, axis=1)
+    catalogue = spread[:, :HOWN]
+    for shift in range(1, groups):
+        chunk = spread[:, shift * HOWN:(shift + 1) * HOWN]
+        pairs = [(i, (i + shift) % groups) for i in range(groups)]
+        catalogue = catalogue + lax.ppermute(chunk, "gy", pairs)
     return (response, catalogue)
 
 

time: 168 us -> 173 us (1.030)
  blocking collectives: 14.8 us -> 0 us
  starting transfers between devices: 16.9 us -> 31.6 us
  other arithmetic: 6.04 us -> 10.2 us
    all_to_all x1 -> x0, blocking collectives: 14.8 us -> none  [per_device(): lax.all_to_all(spread.reshape(SCALES, groups, HOWN), 'gy', split_axis=1,...]
    ppermute x0 -> x7, starting transfers between devices: none -> 14.7 us  [per_device(): catalogue = catalogue + lax.ppermute(chunk, 'gy', pairs)]
    ppermute x0 -> x7, waiting for transfers between devices: none -> 4.4 us  [per_device(): catalogue = catalogue + lax.ppermute(chunk, 'gy', pairs)]
    ppermute x1, waiting for transfers between devices: 40 us -> 36.9 us  [with_halo(): lax.ppermute(lax.slice_in_dim(block, 0, width, axis=dim), axis, backward)]
  transfers between devices with their start and end apart: 8 -> 15, of which waited for: 6 -> 8; matrix products, arithmetic and copies ran while one was open for 4% -> 7% of each run, Pallas kernels for 16% -> 16%
where the time goes in v3:
time: 173 us; the launch traced here: 172 us
  waiting for transfers between devices  61.7 us (36%)
  Pallas kernels  40.5 us (23%)
  starting transfers between devices  31.6 us (18%)
  local copies, waits for them, and re-layouts  10.5 us (6%)
  other arithmetic  10.2 us (6%)
  between operations  9.99 us (6%)
  matrix products  7.46 us (4%)
    pallas_call x3, Pallas kernels, run(): pl.pallas_call(kernel, out_shape=(block, block), in_specs=in_specs, out_s...  40.5 us
    ppermute x1, waiting for transfers between devices, with_halo(): lax.ppermute(lax.slice_in_dim(block, 0, width, axis=dim), axis, backward)  36.9 us
    ppermute x7, starting transfers between devices, per_device(): catalogue = catalogue + lax.ppermute(chunk, 'gy', pairs)  14.7 us
    ppermute x3, starting transfers between devices, z_neighbours(): lax.ppermute(lax.slice_in_dim(block, 0, width, axis=0), 'gz', backward)  13.2 us
    ppermute x3, waiting for transfers between devices, z_neighbours(): lax.ppermute(lax.slice_in_dim(block, 0, width, axis=0), 'gz', backward)  11.9 us
    ppermute x3, waiting for transfers between devices, z_neighbours(): lax.ppermute(lax.slice_in_dim(block, block.shape[0] - width, None, axis=0...  8.51 us
    dot_general x3, matrix products, per_device(): jnp.dot(feature, pick_x, precision=lax.Precision.HIGHEST, preferred_eleme...  6.63 us
    add x1, other arithmetic, smooth_padded(): running = summand if running is None else running + summand  5.18 us
  transfers between devices with their start and end apart: 15, of which 8 were waited for; matrix products, arithmetic and copies ran while one was open for 7% of the time, Pallas kernels for 16%

profile of v3, /device:TPU:2, one launch (start us, length us, event | category | flops | bytes accessed | tf_op | source)
XLA Modules:
  0.0 171.9 jit_solution(10754982561382838675)
XLA Ops:
  0.6 2.0 %fusion.33 = (f32[10,9,2048]{2,1,0:T(8,128)S(1)}, f32[10,9,2048]{2,1,0:T(8,128)S(1)}) fusion(f32[10,16,2048]{2,1,0:T(8,128)} %param.6), kind=kLoop, calls=%fused_computation.79 | loop fusion | bytes 2949120 | tf_op jit(solution)/shard_map/slice | solution.py:25
  2.7 0.0 copy-start.6
  2.7 0.4 copy.13
  3.2 3.2 %collective-permute-start.1 = (f32[10,9,2048]{2,0,1:T(8,128)S(1)}, f32[10,9,2048]{2,0,1:T(8,128)S(1)}, u32[]{:S(2)}, u32[]{:S(2)}) collective-permute-start(f32[10,9,2048]{2,0,1:T(8,128)S(1)} %copy.13), channel_id=1, source_target_pairs={{1,0},{2,1},{3,2},{4,3},{5,4},{6,5},{7,6},{0,7},{9,8},{10,9},{11,1... | collective-permute-start | bytes 2211848 | tf_op jit(solution)/shard_map/ppermute | solution.py:27
  6.4 0.4 copy.12
  6.9 0.4 collective-permute-start
  7.3 0.6 broadcast_add_fusion.1
  7.9 0.6 fusion.36
  17.5 0.7 broadcast_add_fusion
  18.2 1.4 pad_add_fusion.2
  19.6 1.3 pad_add_fusion
  20.8 0.0 copy-start.3
  20.9 36.9 %collective-permute-done.1 = f32[10,9,2048]{2,0,1:T(8,128)S(1)} collective-permute-done((f32[10,9,2048]{2,0,1:T(8,128)S(1)}, f32[10,9,2048]{2,0,1:T(8,128)S(1)}, u32[]{:S(2)}, u32[]{:S(2)}) %collective-permute-start.1) | collective-permute-done | bytes 737312 | tf_op jit(solution)/shard_map/ppermute | solution.py:27
  57.7 0.5 copy.11
  58.2 1.7 %copy.10 = f32[10,9,2048]{2,1,0:T(8,128)S(1)} copy(f32[10,9,2048]{2,0,1:T(8,128)} %collective-permute-done) | data formatting | bytes 1474560 | tf_op jit(solution)/shard_map/ppermute | solution.py:24
  60.0 0.4 pad_maximum_fusion
  60.4 5.2 %multiply_add_fusion = (f32[10,18,2048]{2,1,0:T(8,128)S(1)}, f32[10,18,2048]{2,1,0:T(8,128)S(1)}, f32[10,18,2048]{2,1,0:T(8,128)S(1)}) fusion(f32[10,34,2048]{2,1,0:T(8,128)S(1)} %pad_maximum_fusion, s32[]{:T(128)S(6)} %select_n.87, s32[]{:T(128)S(6)} %select_n.86, s32[]{:T(128)S(6)} %select_n.85, s32[]{:T(128)S(6)} %select_n.84, s32[]{:T(128)S(6)} %select_n.83, ...), kind=kLoop, calls=%fused_computation.11 | loop fusion | flops 9216000 | bytes 23593008 | tf_op jit(solution)/shard_map/add | solution.py:39
  65.6 0.4 fusion.30
  66.0 0.9 copy-done
  66.9 5.4 %collective-permute-start.7 = (f32[9,18,2048]{2,1,0:T(8,128)S(1)}, f32[9,18,2048]{2,1,0:T(8,128)S(1)}, u32[]{:S(2)}, u32[]{:S(2)}) collective-permute-start(f32[9,18,2048]{2,1,0:T(8,128)S(1)} %get-tuple-element.25), channel_id=1, source_target_pairs={{8,0},{16,8},{24,16},{32,24},{40,32},{48,40},{56,48},{64,56},{72,6... | collective-permute-start | bytes 3981320 | tf_op jit(solution)/shard_map/ppermute | solution.py:173
  72.3 0.4 fusion.31
  72.8 3.9 %collective-permute-start.5 = (f32[9,18,2048]{2,1,0:T(8,128)S(1)}, f32[9,18,2048]{2,1,0:T(8,128)}, u32[]{:S(2)}, u32[]{:S(2)}) collective-permute-start(f32[9,18,2048]{2,1,0:T(8,128)S(1)} %get-tuple-element.27), channel_id=1, source_target_pairs={{8,0},{16,8},{24,16},{32,24},{40,32},{48,40},{56,48},{64,56},{72,6... | collective-permute-start | bytes 3981320 | tf_op jit(solution)/shard_map/ppermute | solution.py:173
  76.8 0.0 copy-start.14
  76.8 1.7 %fusion.32 = (f32[9,18,2048]{2,1,0:T(8,128)}, f32[9,18,2048]{2,1,0:T(8,128)S(1)}) fusion(f32[10,18,2048]{2,1,0:T(8,128)S(1)} %get-tuple-element.24.refs_2_), kind=kLoop, calls=%fused_computation.78 | loop fusion | bytes 5308416 | tf_op jit(solution)/shard_map/slice | solution.py:173
  78.5 3.8 %collective-permute-start.3 = (f32[9,18,2048]{2,1,0:T(8,128)}, f32[9,18,2048]{2,1,0:T(8,128)S(1)}, u32[]{:S(2)}, u32[]{:S(2)}) collective-permute-start(f32[9,18,2048]{2,1,0:T(8,128)} %get-tuple-element.29), channel_id=1, source_target_pairs={{8,0},{16,8},{24,16},{32,24},{40,32},{48,40},{56,48},{64,56},{72,6... | collective-permute-start | bytes 3981320 | tf_op jit(solution)/shard_map/ppermute | solution.py:173
  82.4 10.0 %collective-permute-done.7.refs_3_ = f32[9,18,2048]{2,1,0:T(8,128)S(1)} collective-permute-done((f32[9,18,2048]{2,1,0:T(8,128)S(1)}, f32[9,18,2048]{2,1,0:T(8,128)S(1)}, u32[]{:S(2)}, u32[]{:S(2)}) %collective-permute-start.7) | collective-permute-done | bytes 1327136 | tf_op jit(solution)/shard_map/ppermute | solution.py:173
  92.4 1.2 copy-done.4
  93.6 2.9 %collective-permute-done.6.refs_1_ = f32[9,18,2048]{2,1,0:T(8,128)} collective-permute-done((f32[9,18,2048]{2,1,0:T(8,128)S(1)}, f32[9,18,2048]{2,1,0:T(8,128)}, u32[]{:S(2)}, u32[]{:S(2)}) %collective-permute-start.6) | collective-permute-done | bytes 1327136 | tf_op jit(solution)/shard_map/ppermute | solution.py:172
  96.5 12.9 %shard_map.77 = (f32[10,16,2048]{2,1,0:T(8,128)}, f32[10,16,2048]{2,1,0:T(8,128)}) custom-call(s32[3]{0:T(128)} %refs_0_.5, f32[9,18,2048]{2,1,0:T(8,128)} %collective-permute-done.6.refs_1_, f32[10,18,2048]{2,1,0:T(8,128)} %copy-done, f32[9,18,2048]{2,1,0:T(8,128)} %copy-done.4), custom_call_target="tpu_custom_call" | custom-call | tf_op jit(solution)/shard_map/pallas_call | solution.py:151
  109.4 1.9 %collective-permute-done.5.refs_3_ = f32[9,18,2048]{2,1,0:T(8,128)} collective-permute-done((f32[9,18,2048]{2,1,0:T(8,128)S(1)}, f32[9,18,2048]{2,1,0:T(8,128)}, u32[]{:S(2)}, u32[]{:S(2)}) %collective-permute-start.5) | collective-permute-done | bytes 1327136 | tf_op jit(solution)/shard_map/ppermute | solution.py:173
  111.3 4.1 %collective-permute-done.4.refs_1_ = f32[9,18,2048]{2,1,0:T(8,128)} collective-permute-done((f32[9,18,2048]{2,1,0:T(8,128)S(1)}, f32[9,18,2048]{2,1,0:T(8,128)}, u32[]{:S(2)}, u32[]{:S(2)}) %collective-permute-start.4) | collective-permute-done | bytes 1327136 | tf_op jit(solution)/shard_map/ppermute | solution.py:172
  115.5 13.7 %shard_map.78 = (f32[10,16,2048]{2,1,0:T(8,128)}, f32[10,16,2048]{2,1,0:T(8,128)}) custom-call(s32[3]{0:T(128)} %refs_0_.5, f32[9,18,2048]{2,1,0:T(8,128)} %collective-permute-done.4.refs_1_, f32[10,18,2048]{2,1,0:T(8,128)} %copy-done.2, f32[9,18,2048]{2,1,0:T(8,128)} %collective-permute-done.5.refs_3_, f32[10,16,2048]{2,1,0:T(8,128)} %get-tuple-element.8.refs_4_), custom_call_target="tpu_custom_call" | custom-call | tf_op jit(solution)/shard_map/pallas_call | solution.py:151
  129.3 1.8 %fusion.12 = f32[512]{0:T(512)S(1)} fusion(f32[160,2048]{1,0:T(8,128)S(1)} %bitcast.54, s32[512]{0:T(512)S(1)} %copy-done.10, f32[512]{0:T(512)S(1)} %get-tuple-element.60, s32[512]{0:T(512)S(1)} %pad_add_fusion.4, f32[512]{0:T(512)S(1)} %get-tuple-element.59, s32[512]{0:T(512)S(1)} %copy-done.9, f32[512]{0:T(512)S(1)} %get-tuple-element.58, ...), kind=kOutput, calls=%fused_computation.19 | convolution fusion | flops 2015378944 | bytes 1331200 | tf_op jit(solution)/shard_map/dot_general | solution.py:262
  131.1 1.8 %fusion.11 = f32[512]{0:T(512)S(1)} fusion(f32[160,2048]{1,0:T(8,128)S(1)} %bitcast.55, s32[512]{0:T(512)S(1)} %copy-done.10, f32[512]{0:T(512)S(1)} %get-tuple-element.60, s32[512]{0:T(512)S(1)} %pad_add_fusion.4, f32[512]{0:T(512)S(1)} %get-tuple-element.59, s32[512]{0:T(512)S(1)} %copy-done.9, f32[512]{0:T(512)S(1)} %get-tuple-element.58, ...), kind=kOutput, calls=%fused_computation.18 | convolution fusion | flops 2015378944 | bytes 1331200 | tf_op jit(solution)/shard_map/dot_general | solution.py:262
  132.9 1.5 collective-permute-done.2.refs_1_
  134.4 13.9 %shard_map.79 = (f32[10,16,2048]{2,1,0:T(8,128)}, f32[10,16,2048]{2,1,0:T(8,128)}) custom-call(s32[3]{0:T(128)} %refs_0_.5, f32[9,18,2048]{2,1,0:T(8,128)} %collective-permute-done.2.refs_1_, f32[10,18,2048]{2,1,0:T(8,128)} %copy-done.1, f32[9,18,2048]{2,1,0:T(8,128)} %copy-done.5, f32[10,16,2048]{2,1,0:T(8,128)} %get-tuple-element.9.refs_4_), custom_call_target="tpu_custom_call" | custom-call | tf_op jit(solution)/shard_map/pallas_call | solution.py:151
  148.3 3.1 %fusion.10 = f32[512]{0:T(512)S(1)} fusion(f32[160,2048]{1,0:T(8,128)} %bitcast.56, s32[512]{0:T(512)S(1)} %copy-done.10, f32[512]{0:T(512)S(1)} %get-tuple-element.60, s32[512]{0:T(512)S(1)} %pad_add_fusion.4, f32[512]{0:T(512)S(1)} %get-tuple-element.59, s32[512]{0:T(512)S(1)} %copy-done.9, f32[512]{0:T(512)S(1)} %get-tuple-element.58, ...), kind=kOutput, calls=%fused_computation.17 | convolution fusion | flops 2015378944 | bytes 1331200 | tf_op jit(solution)/shard_map/dot_general | solution.py:262
  151.4 0.8 fusion.6
  152.2 4.6 %collective-permute-start.8 = (f32[3,256]{1,0:T(4,128)S(1)}, f32[3,256]{1,0:T(4,128)S(1)}, u32[]{:S(2)}, u32[]{:S(2)}) collective-permute-start(f32[3,256]{1,0:T(4,128)S(1)} %get-tuple-element.33), channel_id=1, source_target_pairs={{0,1},{1,2},{2,3},{3,4},{4,5},{5,6},{6,7},{7,0},{8,9},{9,10},{10,1... | collective-permute-start | bytes 9224 | tf_op jit(solution)/shard_map/ppermute | solution.py:281
  156.8 0.1 collective-permute-start.14
  156.8 2.7 %collective-permute-start.13 = (f32[3,256]{1,0:T(4,128)S(1)}, f32[3,256]{1,0:T(4,128)S(1)}, u32[]{:S(2)}, u32[]{:S(2)}) collective-permute-start(f32[3,256]{1,0:T(4,128)S(1)} %get-tuple-element.35), channel_id=1, source_target_pairs={{0,6},{1,7},{2,0},{3,1},{4,2},{5,3},{6,4},{7,5},{8,14},{9,15},{10,... | collective-permute-start | bytes 9224 | tf_op jit(solution)/shard_map/ppermute | solution.py:281
  159.5 3.2 %collective-permute-start.12 = (f32[3,256]{1,0:T(4,128)S(1)}, f32[3,256]{1,0:T(4,128)S(1)}, u32[]{:S(2)}, u32[]{:S(2)}) collective-permute-start(f32[3,256]{1,0:T(4,128)S(1)} %get-tuple-element.36), channel_id=1, source_target_pairs={{0,5},{1,6},{2,7},{3,0},{4,1},{5,2},{6,3},{7,4},{8,13},{9,14},{10,... | collective-permute-start | bytes 9224 | tf_op jit(solution)/shard_map/ppermute | solution.py:281
  162.7 1.1 collective-permute-start.11
  163.8 1.0 collective-permute-start.10
  164.8 2.1 %collective-permute-start.9 = (f32[3,256]{1,0:T(4,128)S(1)}, f32[3,256]{1,0:T(4,128)S(1)}, u32[]{:S(2)}, u32[]{:S(2)}) collective-permute-start(f32[3,256]{1,0:T(4,128)S(1)} %get-tuple-element.39), channel_id=1, source_target_pairs={{0,2},{1,3},{2,4},{3,5},{4,6},{5,7},{6,0},{7,1},{8,10},{9,11},{10,... | collective-permute-start | bytes 9224 | tf_op jit(solution)/shard_map/ppermute | solution.py:281
  166.9 0.9 collective-permute-done.11
  167.8 3.5 %collective-permute-done.10 = f32[3,256]{1,0:T(4,128)S(1)} collective-permute-done((f32[3,256]{1,0:T(4,128)S(1)}, f32[3,256]{1,0:T(4,128)S(1)}, u32[]{:S(2)}, u32[]{:S(2)}) %collective-permute-start.10) | collective-permute-done | bytes 3104 | tf_op jit(solution)/shard_map/ppermute | solution.py:281
  171.3 0.6 fusion.19
  (49 shorter events, 0.2 us)
Async XLA Ops:
  2.7 4.6 %copy-start.12 = (s32[256]{0:T(256)S(1)}, s32[256]{0:T(256)}, u32[]{:S(2)}) copy-start(s32[256]{0:T(256)} %param.10) | copy-start | bytes 3076
  2.7 5.2 %copy-start.6 = (s32[3]{0:T(128)S(1)}, s32[3]{0:T(128)}, u32[]{:S(2)}) copy-start(s32[3]{0:T(128)} %refs_0_.5) | copy-start | bytes 40
  3.1 17.7 %copy-start.7 = (f32[8,256]{1,0:T(8,128)S(1)}, f32[8,256]{1,0:T(8,128)}, u32[]{:S(2)}) copy-start(f32[8,256]{1,0:T(8,128)} %param.11) | copy-start | bytes 24580
  3.2 54.6 %collective-permute-start.1 = (f32[10,9,2048]{2,0,1:T(8,128)S(1)}, f32[10,9,2048]{2,0,1:T(8,128)S(1)}, u32[]{:S(2)}, u32[]{:S(2)}) collective-permute-start(f32[10,9,2048]{2,0,1:T(8,128)S(1)} %copy.13), channel_id=1, source_target_pairs={{1,0},{2,1},{3,2},{4,3},{5,4},{6,5},{7,6},{0,7},{9,8},{10,9},{11,1... | collective-permute-start | bytes 2211848 | tf_op jit(solution)/shard_map/ppermute | solution.py:27
  6.9 51.3 %collective-permute-start = (f32[10,9,2048]{2,0,1:T(8,128)S(1)}, f32[10,9,2048]{2,0,1:T(8,128)}, u32[]{:S(2)}, u32[]{:S(2)}) collective-permute-start(f32[10,9,2048]{2,0,1:T(8,128)S(1)} %copy.12), channel_id=1, source_target_pairs={{0,1},{1,2},{2,3},{3,4},{4,5},{5,6},{6,7},{7,0},{8,9},{9,10},{10,1... | collective-permute-start | bytes 2211848 | tf_op jit(solution)/shard_map/ppermute | solution.py:24
  20.8 39.1 %copy-start.3 = (f32[10,16,2048]{2,1,0:T(8,128)S(1)}, f32[10,16,2048]{2,1,0:T(8,128)}, u32[]{:S(2)}) copy-start(f32[10,16,2048]{2,1,0:T(8,128)} %param.6) | copy-start | bytes 3932164
  65.6 1.3 copy-start
  65.6 6.7 %copy-start.2 = (f32[10,18,2048]{2,1,0:T(8,128)}, f32[10,18,2048]{2,1,0:T(8,128)S(1)}, u32[]{:S(2)}) copy-start(f32[10,18,2048]{2,1,0:T(8,128)S(1)} %get-tuple-element.23.refs_2_) | copy-start | bytes 4423684
  65.6 11.2 %copy-start.1 = (f32[10,18,2048]{2,1,0:T(8,128)}, f32[10,18,2048]{2,1,0:T(8,128)S(1)}, u32[]{:S(2)}) copy-start(f32[10,18,2048]{2,1,0:T(8,128)S(1)} %get-tuple-element.24.refs_2_) | copy-start | bytes 4423684
  66.9 25.5 %collective-permute-start.7 = (f32[9,18,2048]{2,1,0:T(8,128)S(1)}, f32[9,18,2048]{2,1,0:T(8,128)S(1)}, u32[]{:S(2)}, u32[]{:S(2)}) collective-permute-start(f32[9,18,2048]{2,1,0:T(8,128)S(1)} %get-tuple-element.25), channel_id=1, source_target_pairs={{8,0},{16,8},{24,16},{32,24},{40,32},{48,40},{56,48},{64,56},{72,6... | collective-permute-start | bytes 3981320 | tf_op jit(solution)/shard_map/ppermute | solution.py:173
  72.3 24.2 %collective-permute-start.6 = (f32[9,18,2048]{2,1,0:T(8,128)S(1)}, f32[9,18,2048]{2,1,0:T(8,128)}, u32[]{:S(2)}, u32[]{:S(2)}) collective-permute-start(f32[9,18,2048]{2,1,0:T(8,128)S(1)} %get-tuple-element.26), channel_id=1, source_target_pairs={{0,8},{8,16},{16,24},{24,32},{32,40},{40,48},{48,56},{56,64},{64,7... | collective-permute-start | bytes 3981320 | tf_op jit(solution)/shard_map/ppermute | solution.py:172
  72.8 38.5 %collective-permute-start.5 = (f32[9,18,2048]{2,1,0:T(8,128)S(1)}, f32[9,18,2048]{2,1,0:T(8,128)}, u32[]{:S(2)}, u32[]{:S(2)}) collective-permute-start(f32[9,18,2048]{2,1,0:T(8,128)S(1)} %get-tuple-element.27), channel_id=1, source_target_pairs={{8,0},{16,8},{24,16},{32,24},{40,32},{48,40},{56,48},{64,56},{72,6... | collective-permute-start | bytes 3981320 | tf_op jit(solution)/shard_map/ppermute | solution.py:173
  76.7 38.7 %collective-permute-start.4 = (f32[9,18,2048]{2,1,0:T(8,128)S(1)}, f32[9,18,2048]{2,1,0:T(8,128)}, u32[]{:S(2)}, u32[]{:S(2)}) collective-permute-start(f32[9,18,2048]{2,1,0:T(8,128)S(1)} %get-tuple-element.28), channel_id=1, source_target_pairs={{0,8},{8,16},{16,24},{24,32},{32,40},{40,48},{48,56},{56,64},{64,7... | collective-permute-start | bytes 3981320 | tf_op jit(solution)/shard_map/ppermute | solution.py:172
  76.8 16.8 %copy-start.14 = (s32[256,1]{0,1:T(1,128)S(1)}, s32[256,1]{0,1:T(1,128)}, u32[]{:S(2)}) copy-start(s32[256,1]{0,1:T(1,128)} %param.8) | copy-start | bytes 3076
  76.8 16.8 %copy-start.13 = (s32[256]{0:T(256)S(1)}, s32[256]{0:T(256)}, u32[]{:S(2)}) copy-start(s32[256]{0:T(256)} %param.9) | copy-start | bytes 3076
  78.5 54.3 %collective-permute-start.3 = (f32[9,18,2048]{2,1,0:T(8,128)}, f32[9,18,2048]{2,1,0:T(8,128)S(1)}, u32[]{:S(2)}, u32[]{:S(2)}) collective-permute-start(f32[9,18,2048]{2,1,0:T(8,128)} %get-tuple-element.29), channel_id=1, source_target_pairs={{8,0},{16,8},{24,16},{32,24},{40,32},{48,40},{56,48},{64,56},{72,6... | collective-permute-start | bytes 3981320 | tf_op jit(solution)/shard_map/ppermute | solution.py:173
  92.4 1.2 copy-start.4
  92.4 42.0 %collective-permute-start.2 = (f32[9,18,2048]{2,1,0:T(8,128)S(1)}, f32[9,18,2048]{2,1,0:T(8,128)}, u32[]{:S(2)}, u32[]{:S(2)}) collective-permute-start(f32[9,18,2048]{2,1,0:T(8,128)S(1)} %get-tuple-element.30), channel_id=1, source_target_pairs={{0,8},{8,16},{16,24},{24,32},{32,40},{40,48},{48,56},{56,64},{64,7... | collective-permute-start | bytes 3981320 | tf_op jit(solution)/shard_map/ppermute | solution.py:172
  115.5 13.8 %copy-start.8 = (s32[512]{0:T(512)S(1)}, s32[512]{0:T(512)}, u32[]{:S(2)}) copy-start(s32[512]{0:T(512)} %get-tuple-element.55) | copy-start | bytes 6148
  115.5 13.8 %copy-start.9 = (s32[512]{0:T(512)S(1)}, s32[512]{0:T(512)}, u32[]{:S(2)}) copy-start(s32[512]{0:T(512)} %get-tuple-element.56) | copy-start | bytes 6148
  115.5 13.8 %copy-start.10 = (s32[512]{0:T(512)S(1)}, s32[512]{0:T(512)}, u32[]{:S(2)}) copy-start(s32[512]{0:T(512)} %get-tuple-element.53) | copy-start | bytes 6148
  115.5 13.8 %copy-start.11 = (s32[512]{0:T(512)S(1)}, s32[512]{0:T(512)}, u32[]{:S(2)}) copy-start(s32[512]{0:T(512)} %get-tuple-element.54) | copy-start | bytes 6148
  115.5 13.8 %copy-start.15 = (f32[10,16,2048]{2,1,0:T(8,128)S(1)}, f32[10,16,2048]{2,1,0:T(8,128)}, u32[]{:S(2)}) copy-start(f32[10,16,2048]{2,1,0:T(8,128)} %get-tuple-element.11) | copy-start | bytes 3932164
  129.2 1.9 %copy-start.16 = (f32[10,16,2048]{2,1,0:T(8,128)S(1)}, f32[10,16,2048]{2,1,0:T(8,128)}, u32[]{:S(2)}) copy-start(f32[10,16,2048]{2,1,0:T(8,128)} %get-tuple-element.12) | copy-start | bytes 3932164
  132.9 1.5 copy-start.5
  152.2 11.6 %collective-permute-start.8 = (f32[3,256]{1,0:T(4,128)S(1)}, f32[3,256]{1,0:T(4,128)S(1)}, u32[]{:S(2)}, u32[]{:S(2)}) collective-permute-start(f32[3,256]{1,0:T(4,128)S(1)} %get-tuple-element.33), channel_id=1, source_target_pairs={{0,1},{1,2},{2,3},{3,4},{4,5},{5,6},{6,7},{7,0},{8,9},{9,10},{10,1... | collective-permute-start | bytes 9224 | tf_op jit(solution)/shard_map/ppermute | solution.py:281
  156.8 8.1 %collective-permute-start.14 = (f32[3,256]{1,0:T(4,128)S(1)}, f32[3,256]{1,0:T(4,128)S(1)}, u32[]{:S(2)}, u32[]{:S(2)}) collective-permute-start(f32[3,256]{1,0:T(4,128)S(1)} %get-tuple-element.34), channel_id=1, source_target_pairs={{0,7},{1,0},{2,1},{3,2},{4,3},{5,4},{6,5},{7,6},{8,15},{9,8},{10,9... | collective-permute-start | bytes 9224 | tf_op jit(solution)/shard_map/ppermute | solution.py:281
  156.8 10.1 %collective-permute-start.13 = (f32[3,256]{1,0:T(4,128)S(1)}, f32[3,256]{1,0:T(4,128)S(1)}, u32[]{:S(2)}, u32[]{:S(2)}) collective-permute-start(f32[3,256]{1,0:T(4,128)S(1)} %get-tuple-element.35), channel_id=1, source_target_pairs={{0,6},{1,7},{2,0},{3,1},{4,2},{5,3},{6,4},{7,5},{8,14},{9,15},{10,... | collective-permute-start | bytes 9224 | tf_op jit(solution)/shard_map/ppermute | solution.py:281
  159.5 7.4 %collective-permute-start.12 = (f32[3,256]{1,0:T(4,128)S(1)}, f32[3,256]{1,0:T(4,128)S(1)}, u32[]{:S(2)}, u32[]{:S(2)}) collective-permute-start(f32[3,256]{1,0:T(4,128)S(1)} %get-tuple-element.36), channel_id=1, source_target_pairs={{0,5},{1,6},{2,7},{3,0},{4,1},{5,2},{6,3},{7,4},{8,13},{9,14},{10,... | collective-permute-start | bytes 9224 | tf_op jit(solution)/shard_map/ppermute | solution.py:281
  162.7 5.1 %collective-permute-start.11 = (f32[3,256]{1,0:T(4,128)S(1)}, f32[3,256]{1,0:T(4,128)S(1)}, u32[]{:S(2)}, u32[]{:S(2)}) collective-permute-start(f32[3,256]{1,0:T(4,128)S(1)} %get-tuple-element.37), channel_id=1, source_target_pairs={{0,4},{1,5},{2,6},{3,7},{4,0},{5,1},{6,2},{7,3},{8,12},{9,13},{10,... | collective-permute-start | bytes 9224 | tf_op jit(solution)/shard_map/ppermute | solution.py:281
  163.8 7.5 %collective-permute-start.10 = (f32[3,256]{1,0:T(4,128)S(1)}, f32[3,256]{1,0:T(4,128)S(1)}, u32[]{:S(2)}, u32[]{:S(2)}) collective-permute-start(f32[3,256]{1,0:T(4,128)S(1)} %get-tuple-element.38), channel_id=1, source_target_pairs={{0,3},{1,4},{2,5},{3,6},{4,7},{5,0},{6,1},{7,2},{8,11},{9,12},{10,... | collective-permute-start | bytes 9224 | tf_op jit(solution)/shard_map/ppermute | solution.py:281
  164.8 6.5 %collective-permute-start.9 = (f32[3,256]{1,0:T(4,128)S(1)}, f32[3,256]{1,0:T(4,128)S(1)}, u32[]{:S(2)}, u32[]{:S(2)}) collective-permute-start(f32[3,256]{1,0:T(4,128)S(1)} %get-tuple-element.39), channel_id=1, source_target_pairs={{0,2},{1,3},{2,4},{3,5},{4,6},{5,7},{6,0},{7,1},{8,10},{9,11},{10,... | collective-permute-start | bytes 9224 | tf_op jit(solution)/shard_map/ppermute | solution.py:281

commit v4 on v2

--- a/solution.py
+++ b/solution.py
@@ -91,12 +91,10 @@
                 curve_yy = hessian_scale * (above_y - 2.0 * centre + below_y)
                 curve_xx = hessian_scale * (left(centre) - 2.0 * centre + right(centre))
                 curve_zy = (hessian_scale * 0.25) * (at(1, 1) - at(1, -1) - at(-1, 1) + at(-1, -1))
-                curve_zx = (hessian_scale * 0.25) * (
-                    left(above_z) - right(above_z) - left(below_z) + right(below_z)
-                )
-                curve_yx = (hessian_scale * 0.25) * (
-                    left(above_y) - right(above_y) - left(below_y) + right(below_y)
-                )
+                across_z = above_z - below_z
+                across_y = above_y - below_y
+                curve_zx = (hessian_scale * 0.25) * (left(across_z) - right(across_z))
+                curve_yx = (hessian_scale * 0.25) * (left(across_y) - right(across_y))
                 trace_sum = curve_xx + curve_yy + curve_zz
                 minor_sum = (
                     curve_xx * curve_yy
@@ -231,13 +229,30 @@
     banded = with_halo(density, (("gy", 1),), HALO)
     response = None
     features = []
-    for level_index in range(SCALES):
-        dilation = dilations[level_index]
-        along_y = smooth_padded(banded, dilation, 1, band_rows)
-        low, high = z_neighbours(along_y, HALO)
+    pending = None
+
+    def finish(pending, response):
+        level_index, low, along_y, high = pending
         run = level_kernel(level_index, level_index == 0, slab_depth, band_rows, row_length)
         feature, response = run(dilations, low, along_y, high, response)
         features.append(feature.reshape(slab_depth * band_rows, row_length))
+        return response
+
+    for level_index in range(SCALES):
+        along_y = smooth_padded(banded, dilations[level_index], 1, band_rows)
+        if pending is not None:
+            held = (along_y, pending[1], pending[3])
+            if response is not None:
+                held = held + (response,)
+            held = lax.optimization_barrier(held)
+            along_y, pending[1], pending[3] = held[:3]
+            if response is not None:
+                response = held[3]
+        low, high = z_neighbours(along_y, HALO)
+        if pending is not None:
+            response = finish(pending, response)
+        pending = [level_index, low, along_y, high]
+    response = finish(pending, response)
     plane = (band_rows - 1) * row_length
     z_index = base_cell // plane
     remainder = base_cell % plane

time: 168 us -> 183 us (1.089)
  waiting for transfers between devices: 60.5 us -> 81.3 us
  starting transfers between devices: 16.9 us -> 11.6 us
    ppermute x3, waiting for transfers between devices: 11.9 us -> 29.1 us  [z_neighbours(): lax.ppermute(lax.slice_in_dim(block, 0, width, axis=0), 'gz', backward)]
    ppermute x3, starting transfers between devices: 13.2 us -> 7.93 us  [z_neighbours(): lax.ppermute(lax.slice_in_dim(block, 0, width, axis=0), 'gz', backward)]
    ppermute x3, waiting for transfers between devices: 8.58 us -> 12.1 us  [z_neighbours(): lax.ppermute(lax.slice_in_dim(block, block.shape[0] - width, None, axis=0...]
    unnamed x28 -> x32, local copies, waits for them, and re-layouts: 2.99 us -> 4.27 us
  transfers between devices with their start and end apart: 8 -> 8, of which waited for: 6 -> 7; matrix products, arithmetic and copies ran while one was open for 4% -> 4% of each run, Pallas kernels for 16% -> 14%
where the time goes in v4:
time: 183 us
  waiting for transfers between devices  81.3 us (44%)
  Pallas kernels  39.3 us (21%)
  blocking collectives  14.8 us (8%)
  starting transfers between devices  11.6 us (6%)
  between operations  10.6 us (6%)
  local copies, waits for them, and re-layouts  10.3 us (6%)
  matrix products  8.78 us (5%)
  other arithmetic  6.24 us (3%)
    ppermute x1, waiting for transfers between devices, with_halo(): lax.ppermute(lax.slice_in_dim(block, 0, width, axis=dim), axis, backward)  40.1 us
    pallas_call x3, Pallas kernels, run(): pl.pallas_call(kernel, out_shape=(block, block), in_specs=in_specs, out_s...  39.3 us
    ppermute x3, waiting for transfers between devices, z_neighbours(): lax.ppermute(lax.slice_in_dim(block, 0, width, axis=0), 'gz', backward)  29.1 us
    all_to_all x1, blocking collectives, per_device(): lax.all_to_all(spread.reshape(SCALES, groups, HOWN), 'gy', split_axis=1,...  14.8 us
    ppermute x3, waiting for transfers between devices, z_neighbours(): lax.ppermute(lax.slice_in_dim(block, block.shape[0] - width, None, axis=0...  12.1 us
    dot_general x3, matrix products, per_device(): jnp.dot(feature, pick_x, precision=lax.Precision.HIGHEST, preferred_eleme...  7.96 us
    ppermute x3, starting transfers between devices, z_neighbours(): lax.ppermute(lax.slice_in_dim(block, 0, width, axis=0), 'gz', backward)  7.93 us
    add x1, other arithmetic, smooth_padded(): running = summand if running is None else running + summand  5.1 us
  transfers between devices with their start and end apart: 8, of which 7 were waited for; matrix products, arithmetic and copies ran while one was open for 4% of the time, Pallas kernels for 14%

profile of v4, /device:TPU:2, one launch (start us, length us, event | category | flops | bytes accessed | tf_op | source)
XLA Modules:
  0.0 183.0 jit_solution(1173343063168643206)
XLA Ops:
  0.6 2.0 %fusion.24 = (f32[10,9,2048]{2,1,0:T(8,128)S(1)}, f32[10,9,2048]{2,1,0:T(8,128)S(1)}) fusion(f32[10,16,2048]{2,1,0:T(8,128)} %param.6), kind=kLoop, calls=%fused_computation.66 | loop fusion | bytes 2949120 | tf_op jit(solution)/shard_map/slice | solution.py:25
  2.6 0.0 copy-start.9
  2.6 0.4 copy.14
  3.1 3.2 %collective-permute-start.1 = (f32[10,9,2048]{2,0,1:T(8,128)S(1)}, f32[10,9,2048]{2,0,1:T(8,128)S(1)}, u32[]{:S(2)}, u32[]{:S(2)}) collective-permute-start(f32[10,9,2048]{2,0,1:T(8,128)S(1)} %copy.14), channel_id=1, source_target_pairs={{1,0},{2,1},{3,2},{4,3},{5,4},{6,5},{7,6},{0,7},{9,8},{10,9},{11,1... | collective-permute-start | bytes 2211848 | tf_op jit(solution)/shard_map/ppermute | solution.py:27
  6.3 0.4 copy.13
  6.8 0.4 collective-permute-start
  7.2 0.0 copy-done.9
  7.2 0.6 fusion.26
  17.6 0.0 copy-start.3
  17.6 40.1 %collective-permute-done.1 = f32[10,9,2048]{2,0,1:T(8,128)S(1)} collective-permute-done((f32[10,9,2048]{2,0,1:T(8,128)S(1)}, f32[10,9,2048]{2,0,1:T(8,128)S(1)}, u32[]{:S(2)}, u32[]{:S(2)}) %collective-permute-start.1) | collective-permute-done | bytes 737312 | tf_op jit(solution)/shard_map/ppermute | solution.py:27
  57.6 0.5 copy.11
  58.1 0.0 collective-permute-done
  58.1 1.7 copy.10
  59.9 0.0 copy-done.3
  59.9 0.4 pad_maximum_fusion
  60.3 5.1 %multiply_add_fusion = (f32[10,18,2048]{2,1,0:T(8,128)S(1)}, f32[10,18,2048]{2,1,0:T(8,128)S(1)}, f32[10,18,2048]{2,1,0:T(8,128)S(1)}) fusion(f32[10,34,2048]{2,1,0:T(8,128)S(1)} %pad_maximum_fusion, s32[]{:T(128)S(6)} %select_n.83, s32[]{:T(128)S(6)} %select_n.82, s32[]{:T(128)S(6)} %select_n.81, s32[]{:T(128)S(6)} %select_n.80, s32[]{:T(128)S(6)} %select_n.79, ...), kind=kLoop, calls=%fused_computation.11 | loop fusion | flops 9216000 | bytes 23593008 | tf_op jit(solution)/shard_map/add | solution.py:39
  65.4 0.0 copy-start
  65.4 0.4 fusion.23
  65.9 0.8 copy-done
  66.7 5.4 %collective-permute-start.3 = (f32[9,18,2048]{2,1,0:T(8,128)S(1)}, f32[9,18,2048]{2,1,0:T(8,128)S(1)}, u32[]{:S(2)}, u32[]{:S(2)}) collective-permute-start(f32[9,18,2048]{2,1,0:T(8,128)S(1)} %get-tuple-element.43), channel_id=1, source_target_pairs={{8,0},{16,8},{24,16},{32,24},{40,32},{48,40},{56,48},{64,56},{72,6... | collective-permute-start | bytes 3981320 | tf_op jit(solution)/shard_map/ppermute | solution.py:171
  72.1 0.0 collective-permute-start.2
  72.1 20.0 %collective-permute-done.3.refs_3_ = f32[9,18,2048]{2,1,0:T(8,128)S(1)} collective-permute-done((f32[9,18,2048]{2,1,0:T(8,128)S(1)}, f32[9,18,2048]{2,1,0:T(8,128)S(1)}, u32[]{:S(2)}, u32[]{:S(2)}) %collective-permute-start.3) | collective-permute-done | bytes 1327136 | tf_op jit(solution)/shard_map/ppermute | solution.py:171
  92.2 4.0 %collective-permute-done.2.refs_1_ = f32[9,18,2048]{2,1,0:T(8,128)S(1)} collective-permute-done((f32[9,18,2048]{2,1,0:T(8,128)S(1)}, f32[9,18,2048]{2,1,0:T(8,128)S(1)}, u32[]{:S(2)}, u32[]{:S(2)}) %collective-permute-start.2) | collective-permute-done | bytes 1327136 | tf_op jit(solution)/shard_map/ppermute | solution.py:170
  96.2 0.0 copy-done.6
  96.2 1.3 copy-done.8
  97.5 0.4 fusion.22
  97.9 1.3 collective-permute-start.5
  99.2 0.0 collective-permute-start.4
  99.2 0.0 copy-done.13
  99.3 0.0 copy-done.12
  99.4 12.7 %shard_map.77 = (f32[10,16,2048]{2,1,0:T(8,128)}, f32[10,16,2048]{2,1,0:T(8,128)}) custom-call(s32[3]{0:T(128)} %refs_0_.5, f32[9,18,2048]{2,1,0:T(8,128)} %copy-done.8, f32[10,18,2048]{2,1,0:T(8,128)} %copy-done, f32[9,18,2048]{2,1,0:T(8,128)} %copy-done.6), custom_call_target="tpu_custom_call" | custom-call | tf_op jit(solution)/shard_map/pallas_call | solution.py:149
  112.0 7.2 %collective-permute-done.5.refs_3_ = f32[9,18,2048]{2,1,0:T(8,128)S(1)} collective-permute-done((f32[9,18,2048]{2,1,0:T(8,128)S(1)}, f32[9,18,2048]{2,1,0:T(8,128)S(1)}, u32[]{:S(2)}, u32[]{:S(2)}) %collective-permute-start.5) | collective-permute-done | bytes 1327136 | tf_op jit(solution)/shard_map/ppermute | solution.py:171
  119.3 4.1 %collective-permute-done.4.refs_1_ = f32[9,18,2048]{2,1,0:T(8,128)} collective-permute-done((f32[9,18,2048]{2,1,0:T(8,128)S(1)}, f32[9,18,2048]{2,1,0:T(8,128)}, u32[]{:S(2)}, u32[]{:S(2)}) %collective-permute-start.4) | collective-permute-done | bytes 1327136 | tf_op jit(solution)/shard_map/ppermute | solution.py:170
  123.4 0.4 fusion.21
  123.8 1.2 collective-permute-start.7
  125.0 0.0 collective-permute-start.6
  125.1 0.0 copy-done.14
  125.1 1.8 fusion.12
  126.9 13.2 %shard_map.78 = (f32[10,16,2048]{2,1,0:T(8,128)}, f32[10,16,2048]{2,1,0:T(8,128)}) custom-call(s32[3]{0:T(128)} %refs_0_.5, f32[9,18,2048]{2,1,0:T(8,128)} %collective-permute-done.4.refs_1_, f32[10,18,2048]{2,1,0:T(8,128)} %copy-done.2, f32[9,18,2048]{2,1,0:T(8,128)} %copy-done.4, f32[10,16,2048]{2,1,0:T(8,128)} %get-tuple-element.22.refs_4_), custom_call_target="tpu_custom_call" | custom-call | tf_op jit(solution)/shard_map/pallas_call | solution.py:149
  140.1 3.1 %fusion.11 = f32[512]{0:T(512)S(1)} fusion(f32[160,2048]{1,0:T(8,128)} %bitcast.58, s32[512]{0:T(512)S(1)} %get-tuple-element.60, f32[512]{0:T(512)S(1)} %get-tuple-element.67, s32[512]{0:T(512)S(1)} %pad_add_fusion.4, f32[512]{0:T(512)S(1)} %get-tuple-element.66, s32[512]{0:T(512)S(1)} %get-tuple-element.63, f32[512]{0:T(512)S(1)} %get-tuple-element.65, ...), kind=kOutput, calls=%fused_computation.18 | convolution fusion | flops 2015378944 | bytes 1331200 | tf_op jit(solution)/shard_map/dot_general | solution.py:277
  143.2 1.8 %collective-permute-done.7.refs_3_ = f32[9,18,2048]{2,1,0:T(8,128)S(1)} collective-permute-done((f32[9,18,2048]{2,1,0:T(8,128)S(1)}, f32[9,18,2048]{2,1,0:T(8,128)S(1)}, u32[]{:S(2)}, u32[]{:S(2)}) %collective-permute-start.7) | collective-permute-done | bytes 1327136 | tf_op jit(solution)/shard_map/ppermute | solution.py:171
  145.1 4.0 %collective-permute-done.6.refs_1_ = f32[9,18,2048]{2,1,0:T(8,128)S(1)} collective-permute-done((f32[9,18,2048]{2,1,0:T(8,128)S(1)}, f32[9,18,2048]{2,1,0:T(8,128)S(1)}, u32[]{:S(2)}, u32[]{:S(2)}) %collective-permute-start.6) | collective-permute-done | bytes 1327136 | tf_op jit(solution)/shard_map/ppermute | solution.py:170
  149.1 1.2 copy-done.7
  150.3 13.4 %shard_map.79 = (f32[10,16,2048]{2,1,0:T(8,128)}, f32[10,16,2048]{2,1,0:T(8,128)}) custom-call(s32[3]{0:T(128)} %refs_0_.5, f32[9,18,2048]{2,1,0:T(8,128)} %copy-done.7, f32[10,18,2048]{2,1,0:T(8,128)} %copy-done.1, f32[9,18,2048]{2,1,0:T(8,128)} %copy-done.5, f32[10,16,2048]{2,1,0:T(8,128)} %get-tuple-element.23.refs_4_), custom_call_target="tpu_custom_call" | custom-call | tf_op jit(solution)/shard_map/pallas_call | solution.py:149
  163.7 3.1 %fusion.10 = f32[512]{0:T(512)S(1)} fusion(f32[160,2048]{1,0:T(8,128)} %bitcast.57, s32[512]{0:T(512)S(1)} %get-tuple-element.60, f32[512]{0:T(512)S(1)} %get-tuple-element.67, s32[512]{0:T(512)S(1)} %pad_add_fusion.4, f32[512]{0:T(512)S(1)} %get-tuple-element.66, s32[512]{0:T(512)S(1)} %get-tuple-element.63, f32[512]{0:T(512)S(1)} %get-tuple-element.65, ...), kind=kOutput, calls=%fused_computation.17 | convolution fusion | flops 2015378944 | bytes 1331200 | tf_op jit(solution)/shard_map/dot_general | solution.py:277
  166.8 0.8 fusion.6
  167.6 14.8 %all_to_all.5 = f32[3,8,256]{2,0,1:T(4,128)S(1)} all-to-all(f32[3,8,256]{2,0,1:T(4,128)S(1)} %bitcast.43), channel_id=1, replica_groups=mesh['gz'=32,'gy'=8] {'gy'}, dimensions={1} | all-to-all | bytes 49152 | tf_op jit(solution)/shard_map/all_to_all | solution.py:292
  182.4 0.6 reduce_sum.39
  (31 shorter events, 0.1 us)
Async XLA Ops:
  2.6 4.6 %copy-start.9 = (s32[3]{0:T(128)S(1)}, s32[3]{0:T(128)}, u32[]{:S(2)}) copy-start(s32[3]{0:T(128)} %refs_0_.5) | copy-start | bytes 40
  3.1 54.6 %collective-permute-start.1 = (f32[10,9,2048]{2,0,1:T(8,128)S(1)}, f32[10,9,2048]{2,0,1:T(8,128)S(1)}, u32[]{:S(2)}, u32[]{:S(2)}) collective-permute-start(f32[10,9,2048]{2,0,1:T(8,128)S(1)} %copy.14), channel_id=1, source_target_pairs={{1,0},{2,1},{3,2},{4,3},{5,4},{6,5},{7,6},{0,7},{9,8},{10,9},{11,1... | collective-permute-start | bytes 2211848 | tf_op jit(solution)/shard_map/ppermute | solution.py:27
  6.8 51.3 %collective-permute-start = (f32[10,9,2048]{2,0,1:T(8,128)S(1)}, f32[10,9,2048]{2,0,1:T(8,128)}, u32[]{:S(2)}, u32[]{:S(2)}) collective-permute-start(f32[10,9,2048]{2,0,1:T(8,128)S(1)} %copy.13), channel_id=1, source_target_pairs={{0,1},{1,2},{2,3},{3,4},{4,5},{5,6},{6,7},{7,0},{8,9},{9,10},{10,1... | collective-permute-start | bytes 2211848 | tf_op jit(solution)/shard_map/ppermute | solution.py:24
  17.6 42.3 %copy-start.3 = (f32[10,16,2048]{2,1,0:T(8,128)S(1)}, f32[10,16,2048]{2,1,0:T(8,128)}, u32[]{:S(2)}) copy-start(f32[10,16,2048]{2,1,0:T(8,128)} %param.6) | copy-start | bytes 3932164
  65.4 1.3 copy-start
  65.4 32.1 %copy-start.2 = (f32[10,18,2048]{2,1,0:T(8,128)}, f32[10,18,2048]{2,1,0:T(8,128)S(1)}, u32[]{:S(2)}) copy-start(f32[10,18,2048]{2,1,0:T(8,128)S(1)} %get-tuple-element.15.refs_2_) | copy-start | bytes 4423684
  65.4 58.0 %copy-start.1 = (f32[10,18,2048]{2,1,0:T(8,128)}, f32[10,18,2048]{2,1,0:T(8,128)S(1)}, u32[]{:S(2)}) copy-start(f32[10,18,2048]{2,1,0:T(8,128)S(1)} %get-tuple-element.19.refs_2_) | copy-start | bytes 4423684
  66.7 25.5 %collective-permute-start.3 = (f32[9,18,2048]{2,1,0:T(8,128)S(1)}, f32[9,18,2048]{2,1,0:T(8,128)S(1)}, u32[]{:S(2)}, u32[]{:S(2)}) collective-permute-start(f32[9,18,2048]{2,1,0:T(8,128)S(1)} %get-tuple-element.43), channel_id=1, source_target_pairs={{8,0},{16,8},{24,16},{32,24},{40,32},{48,40},{56,48},{64,56},{72,6... | collective-permute-start | bytes 3981320 | tf_op jit(solution)/shard_map/ppermute | solution.py:171
  72.1 24.1 %collective-permute-start.2 = (f32[9,18,2048]{2,1,0:T(8,128)S(1)}, f32[9,18,2048]{2,1,0:T(8,128)S(1)}, u32[]{:S(2)}, u32[]{:S(2)}) collective-permute-start(f32[9,18,2048]{2,1,0:T(8,128)S(1)} %get-tuple-element.44), channel_id=1, source_target_pairs={{0,8},{8,16},{16,24},{24,32},{32,40},{40,48},{48,56},{56,64},{64,7... | collective-permute-start | bytes 3981320 | tf_op jit(solution)/shard_map/ppermute | solution.py:170
  92.1 4.0 %copy-start.6 = (f32[9,18,2048]{2,1,0:T(8,128)}, f32[9,18,2048]{2,1,0:T(8,128)S(1)}, u32[]{:S(2)}) copy-start(f32[9,18,2048]{2,1,0:T(8,128)S(1)} %collective-permute-done.3.refs_3_) | copy-start | bytes 3981316
  96.2 1.3 copy-start.8
  97.5 1.7 copy-start.13
  97.5 1.7 copy-start.11
  97.5 1.8 copy-start.12
  97.9 21.3 %collective-permute-start.5 = (f32[9,18,2048]{2,1,0:T(8,128)S(1)}, f32[9,18,2048]{2,1,0:T(8,128)S(1)}, u32[]{:S(2)}, u32[]{:S(2)}) collective-permute-start(f32[9,18,2048]{2,1,0:T(8,128)S(1)} %get-tuple-element.41), channel_id=1, source_target_pairs={{8,0},{16,8},{24,16},{32,24},{40,32},{48,40},{56,48},{64,56},{72,6... | collective-permute-start | bytes 3981320 | tf_op jit(solution)/shard_map/ppermute | solution.py:171
  99.2 24.2 %collective-permute-start.4 = (f32[9,18,2048]{2,1,0:T(8,128)S(1)}, f32[9,18,2048]{2,1,0:T(8,128)}, u32[]{:S(2)}, u32[]{:S(2)}) collective-permute-start(f32[9,18,2048]{2,1,0:T(8,128)S(1)} %get-tuple-element.42), channel_id=1, source_target_pairs={{0,8},{8,16},{16,24},{24,32},{32,40},{40,48},{48,56},{56,64},{64,7... | collective-permute-start | bytes 3981320 | tf_op jit(solution)/shard_map/ppermute | solution.py:170
  119.3 4.1 %copy-start.4 = (f32[9,18,2048]{2,1,0:T(8,128)}, f32[9,18,2048]{2,1,0:T(8,128)S(1)}, u32[]{:S(2)}) copy-start(f32[9,18,2048]{2,1,0:T(8,128)S(1)} %collective-permute-done.5.refs_3_) | copy-start | bytes 3981316
  123.4 1.6 copy-start.10
  123.4 1.7 copy-start.14
  123.8 21.2 %collective-permute-start.7 = (f32[9,18,2048]{2,1,0:T(8,128)S(1)}, f32[9,18,2048]{2,1,0:T(8,128)S(1)}, u32[]{:S(2)}, u32[]{:S(2)}) collective-permute-start(f32[9,18,2048]{2,1,0:T(8,128)S(1)} %get-tuple-element.39), channel_id=1, source_target_pairs={{8,0},{16,8},{24,16},{32,24},{40,32},{48,40},{56,48},{64,56},{72,6... | collective-permute-start | bytes 3981320 | tf_op jit(solution)/shard_map/ppermute | solution.py:171
  125.0 24.1 %collective-permute-start.6 = (f32[9,18,2048]{2,1,0:T(8,128)S(1)}, f32[9,18,2048]{2,1,0:T(8,128)S(1)}, u32[]{:S(2)}, u32[]{:S(2)}) collective-permute-start(f32[9,18,2048]{2,1,0:T(8,128)S(1)} %get-tuple-element.40), channel_id=1, source_target_pairs={{0,8},{8,16},{16,24},{24,32},{32,40},{40,48},{48,56},{56,64},{64,7... | collective-permute-start | bytes 3981320 | tf_op jit(solution)/shard_map/ppermute | solution.py:170
  145.1 4.0 %copy-start.5 = (f32[9,18,2048]{2,1,0:T(8,128)}, f32[9,18,2048]{2,1,0:T(8,128)S(1)}, u32[]{:S(2)}) copy-start(f32[9,18,2048]{2,1,0:T(8,128)S(1)} %collective-permute-done.7.refs_3_) | copy-start | bytes 3981316
  149.1 1.2 copy-start.7

commit v5 on v2

--- a/solution.py
+++ b/solution.py
@@ -15,16 +15,26 @@
 hessian_scale = 4.0
 
 
+def split_ppermute(part, axis, pairs, pieces):
+    size = part.shape[0]
+    bounds = [size * i // pieces for i in range(pieces + 1)]
+    moved = [
+        lax.ppermute(lax.slice_in_dim(part, bounds[i], bounds[i + 1], axis=0), axis, pairs)
+        for i in range(pieces)
+    ]
+    return jnp.concatenate(moved, axis=0)
+
+
 def with_halo(block, sides, width):
     for axis, dim in sides:
         count = lax.axis_size(axis)
         forward = [(i, i + 1) for i in range(count - 1)]
         forward.append((count - 1, 0))
         backward = [(target, source) for source, target in forward]
-        low = lax.ppermute(
-            lax.slice_in_dim(block, block.shape[dim] - width, None, axis=dim), axis, forward
-        )
-        high = lax.ppermute(lax.slice_in_dim(block, 0, width, axis=dim), axis, backward)
+        low = split_ppermute(
+            lax.slice_in_dim(block, block.shape[dim] - width, None, axis=dim), axis, forward, 5
+        )
+        high = split_ppermute(lax.slice_in_dim(block, 0, width, axis=dim), axis, backward, 5)
         block = jnp.concatenate([low, block, high], axis=dim)
     return block
 

time: 168 us -> 184 us (1.095)
  starting transfers between devices: 16.9 us -> 40.2 us
  waiting for transfers between devices: 60.5 us -> 54.4 us
  local copies, waits for them, and re-layouts: 10.4 us -> 8.37 us
    ppermute x2 -> x10, starting transfers between devices: 3.68 us -> 27.7 us  [split_ppermute(): lax.ppermute(lax.slice_in_dim(part, bounds[i], bounds[i + 1], axis=0), ax...]
    ppermute x2 -> x10, waiting for transfers between devices: 40 us -> 35.5 us  [split_ppermute(): lax.ppermute(lax.slice_in_dim(part, bounds[i], bounds[i + 1], axis=0), ax...]
    ppermute x3, waiting for transfers between devices: 11.9 us -> 7.81 us  [z_neighbours(): lax.ppermute(lax.slice_in_dim(block, 0, width, axis=0), 'gz', backward)]
    ppermute x3, starting transfers between devices: 13.2 us -> 9.36 us  [z_neighbours(): lax.ppermute(lax.slice_in_dim(block, 0, width, axis=0), 'gz', backward)]
    ppermute x3, starting transfers between devices: 0.01 us -> 3.1 us  [z_neighbours(): lax.ppermute(lax.slice_in_dim(block, block.shape[0] - width, None, axis=0...]
    ppermute x3, waiting for transfers between devices: 8.58 us -> 11.1 us  [z_neighbours(): lax.ppermute(lax.slice_in_dim(block, block.shape[0] - width, None, axis=0...]
    ppermute x2 -> x0, local copies, waits for them, and re-layouts: 2.19 us -> none  [the longest x1 1.73 us: with_halo(): lax.ppermute(lax.slice_in_dim(block, block.shape[dim] - width, None, axis...]
  transfers between devices with their start and end apart: 8 -> 16, of which waited for: 6 -> 10; matrix products, arithmetic and copies ran while one was open for 4% -> 5% of each run, Pallas kernels for 16% -> 15%
where the time goes in v5:
time: 184 us; the launch traced here: 183 us
  waiting for transfers between devices  54.4 us (30%)
  Pallas kernels  40.6 us (22%)
  starting transfers between devices  40.2 us (22%)
  blocking collectives  15.5 us (8%)
  between operations  10.7 us (6%)
  local copies, waits for them, and re-layouts  8.37 us (5%)
  matrix products  7.46 us (4%)
  other arithmetic  6.03 us (3%)
    pallas_call x3, Pallas kernels, run(): pl.pallas_call(kernel, out_shape=(block, block), in_specs=in_specs, out_s...  40.6 us
    ppermute x10, waiting for transfers between devices, split_ppermute(): lax.ppermute(lax.slice_in_dim(part, bounds[i], bounds[i + 1], axis=0), ax...  35.5 us
    ppermute x10, starting transfers between devices, split_ppermute(): lax.ppermute(lax.slice_in_dim(part, bounds[i], bounds[i + 1], axis=0), ax...  27.7 us
    all_to_all x1, blocking collectives, per_device(): lax.all_to_all(spread.reshape(SCALES, groups, HOWN), 'gy', split_axis=1,...  15.5 us
    ppermute x3, waiting for transfers between devices, z_neighbours(): lax.ppermute(lax.slice_in_dim(block, block.shape[0] - width, None, axis=0...  11.1 us
    ppermute x3, starting transfers between devices, z_neighbours(): lax.ppermute(lax.slice_in_dim(block, 0, width, axis=0), 'gz', backward)  9.36 us
    ppermute x3, waiting for transfers between devices, z_neighbours(): lax.ppermute(lax.slice_in_dim(block, 0, width, axis=0), 'gz', backward)  7.81 us
    dot_general x3, matrix products, per_device(): jnp.dot(feature, pick_x, precision=lax.Precision.HIGHEST, preferred_eleme...  6.64 us
  transfers between devices with their start and end apart: 16, of which 10 were waited for; matrix products, arithmetic and copies ran while one was open for 5% of the time, Pallas kernels for 15%

profile of v5, /device:TPU:2, one launch (start us, length us, event | category | flops | bytes accessed | tf_op | source)
XLA Modules:
  0.0 183.3 jit_solution(6251650864874975528)
XLA Ops:
  0.6 0.0 copy-start.6
  0.7 2.0 %fusion.24 = (f32[2,9,2048]{2,1,0:T(8,128)S(1)}, f32[2,9,2048]{2,1,0:T(8,128)S(1)}, f32[2,9,2048]{2,1,0:T(8,128)S(1)}, f32[2,9,2048]{2,1,0:T(8,128)S(1)}, f32[2,...) fusion(f32[10,16,2048]{2,1,0:T(8,128)} %param.6), kind=kLoop, calls=%fused_computation.76 | loop fusion | bytes 2949120 | tf_op jit(solution)/shard_map/slice | solution.py:22
  2.7 3.3 %collective-permute-start.4 = (f32[2,9,2048]{2,1,0:T(8,128)S(1)}, f32[2,9,2048]{2,1,0:T(8,128)S(1)}, u32[]{:S(2)}, u32[]{:S(2)}) collective-permute-start(f32[2,9,2048]{2,1,0:T(8,128)S(1)} %get-tuple-element.31), channel_id=1, source_target_pairs={{0,1},{1,2},{2,3},{3,4},{4,5},{5,6},{6,7},{7,0},{8,9},{9,10},{10,1... | collective-permute-start | bytes 442376 | tf_op jit(solution)/shard_map/ppermute | solution.py:22
  6.0 1.2 collective-permute-start.8
  7.2 2.3 %collective-permute-start.7 = (f32[2,9,2048]{2,1,0:T(8,128)S(1)}, f32[2,9,2048]{2,1,0:T(8,128)S(1)}, u32[]{:S(2)}, u32[]{:S(2)}) collective-permute-start(f32[2,9,2048]{2,1,0:T(8,128)S(1)} %get-tuple-element.33), channel_id=1, source_target_pairs={{1,0},{2,1},{3,2},{4,3},{5,4},{6,5},{7,6},{0,7},{9,8},{10,9},{11,1... | collective-permute-start | bytes 442376 | tf_op jit(solution)/shard_map/ppermute | solution.py:22
  9.5 4.2 %collective-permute-start.6 = (f32[2,9,2048]{2,1,0:T(8,128)S(1)}, f32[2,9,2048]{2,1,0:T(8,128)}, u32[]{:S(2)}, u32[]{:S(2)}) collective-permute-start(f32[2,9,2048]{2,1,0:T(8,128)S(1)} %get-tuple-element.34), channel_id=1, source_target_pairs={{1,0},{2,1},{3,2},{4,3},{5,4},{6,5},{7,6},{0,7},{9,8},{10,9},{11,1... | collective-permute-start | bytes 442376 | tf_op jit(solution)/shard_map/ppermute | solution.py:22
  13.7 0.6 fusion.26
  24.1 9.9 %collective-permute-done = f32[2,9,2048]{2,1,0:T(8,128)} collective-permute-done((f32[2,9,2048]{2,1,0:T(8,128)S(1)}, f32[2,9,2048]{2,1,0:T(8,128)}, u32[]{:S(2)}, u32[]{:S(2)}) %collective-permute-start) | collective-permute-done | bytes 147488 | tf_op jit(solution)/shard_map/ppermute | solution.py:22
  34.0 4.1 %collective-permute-start.5 = (f32[2,9,2048]{2,1,0:T(8,128)S(1)}, f32[2,9,2048]{2,1,0:T(8,128)S(1)}, u32[]{:S(2)}, u32[]{:S(2)}) collective-permute-start(f32[2,9,2048]{2,1,0:T(8,128)S(1)} %get-tuple-element.35), channel_id=1, source_target_pairs={{1,0},{2,1},{3,2},{4,3},{5,4},{6,5},{7,6},{0,7},{9,8},{10,9},{11,1... | collective-permute-start | bytes 442376 | tf_op jit(solution)/shard_map/ppermute | solution.py:22
  38.1 1.0 constant_dynamic-update-slice_fusion.4
  39.1 4.5 %collective-permute-done.5 = f32[2,9,2048]{2,1,0:T(8,128)S(1)} collective-permute-done((f32[2,9,2048]{2,1,0:T(8,128)S(1)}, f32[2,9,2048]{2,1,0:T(8,128)S(1)}, u32[]{:S(2)}, u32[]{:S(2)}) %collective-permute-start.5) | collective-permute-done | bytes 147488 | tf_op jit(solution)/shard_map/ppermute | solution.py:22
  43.5 4.1 %collective-permute-start.1 = (f32[2,9,2048]{2,1,0:T(8,128)S(1)}, f32[2,9,2048]{2,1,0:T(8,128)S(1)}, u32[]{:S(2)}, u32[]{:S(2)}) collective-permute-start(f32[2,9,2048]{2,1,0:T(8,128)S(1)} %get-tuple-element.38), channel_id=1, source_target_pairs={{0,1},{1,2},{2,3},{3,4},{4,5},{5,6},{6,7},{7,0},{8,9},{9,10},{10,1... | collective-permute-start | bytes 442376 | tf_op jit(solution)/shard_map/ppermute | solution.py:22
  47.7 4.8 %collective-permute-done.1 = f32[2,9,2048]{2,1,0:T(8,128)S(1)} collective-permute-done((f32[2,9,2048]{2,1,0:T(8,128)S(1)}, f32[2,9,2048]{2,1,0:T(8,128)S(1)}, u32[]{:S(2)}, u32[]{:S(2)}) %collective-permute-start.1) | collective-permute-done | bytes 147488 | tf_op jit(solution)/shard_map/ppermute | solution.py:22
  52.5 3.1 %collective-permute-start.2 = (f32[2,9,2048]{2,1,0:T(8,128)S(1)}, f32[2,9,2048]{2,1,0:T(8,128)S(1)}, u32[]{:S(2)}, u32[]{:S(2)}) collective-permute-start(f32[2,9,2048]{2,1,0:T(8,128)S(1)} %get-tuple-element.37), channel_id=1, source_target_pairs={{0,1},{1,2},{2,3},{3,4},{4,5},{5,6},{6,7},{7,0},{8,9},{9,10},{10,1... | collective-permute-start | bytes 442376 | tf_op jit(solution)/shard_map/ppermute | solution.py:22
  55.6 5.7 %collective-permute-done.2 = f32[2,9,2048]{2,1,0:T(8,128)S(1)} collective-permute-done((f32[2,9,2048]{2,1,0:T(8,128)S(1)}, f32[2,9,2048]{2,1,0:T(8,128)S(1)}, u32[]{:S(2)}, u32[]{:S(2)}) %collective-permute-start.2) | collective-permute-done | bytes 147488 | tf_op jit(solution)/shard_map/ppermute | solution.py:22
  61.3 2.3 %collective-permute-start.3 = (f32[2,9,2048]{2,1,0:T(8,128)S(1)}, f32[2,9,2048]{2,1,0:T(8,128)S(1)}, u32[]{:S(2)}, u32[]{:S(2)}) collective-permute-start(f32[2,9,2048]{2,1,0:T(8,128)S(1)} %get-tuple-element.36), channel_id=1, source_target_pairs={{0,1},{1,2},{2,3},{3,4},{4,5},{5,6},{6,7},{7,0},{8,9},{9,10},{10,1... | collective-permute-start | bytes 442376 | tf_op jit(solution)/shard_map/ppermute | solution.py:22
  63.6 6.7 %collective-permute-done.3 = f32[2,9,2048]{2,1,0:T(8,128)S(1)} collective-permute-done((f32[2,9,2048]{2,1,0:T(8,128)S(1)}, f32[2,9,2048]{2,1,0:T(8,128)S(1)}, u32[]{:S(2)}, u32[]{:S(2)}) %collective-permute-start.3) | collective-permute-done | bytes 147488 | tf_op jit(solution)/shard_map/ppermute | solution.py:22
  70.3 3.2 %collective-permute-start.9 = (f32[2,9,2048]{2,1,0:T(8,128)S(1)}, f32[2,9,2048]{2,1,0:T(8,128)S(1)}, u32[]{:S(2)}, u32[]{:S(2)}) collective-permute-start(f32[2,9,2048]{2,1,0:T(8,128)S(1)} %get-tuple-element.40), channel_id=1, source_target_pairs={{1,0},{2,1},{3,2},{4,3},{5,4},{6,5},{7,6},{0,7},{9,8},{10,9},{11,1... | collective-permute-start | bytes 442376 | tf_op jit(solution)/shard_map/ppermute | solution.py:22
  73.5 0.0 collective-permute-done.6
  73.5 1.0 constant_dynamic-update-slice_fusion.8
  74.6 4.0 %collective-permute-done.9 = f32[2,9,2048]{2,1,0:T(8,128)S(1)} collective-permute-done((f32[2,9,2048]{2,1,0:T(8,128)S(1)}, f32[2,9,2048]{2,1,0:T(8,128)S(1)}, u32[]{:S(2)}, u32[]{:S(2)}) %collective-permute-start.9) | collective-permute-done | bytes 147488 | tf_op jit(solution)/shard_map/ppermute | solution.py:22
  78.6 0.4 pad_maximum_fusion
  79.0 4.9 %multiply_add_fusion = (f32[10,18,2048]{2,1,0:T(8,128)S(1)}, f32[10,18,2048]{2,1,0:T(8,128)S(1)}, f32[10,18,2048]{2,1,0:T(8,128)S(1)}) fusion(f32[10,34,2048]{2,1,0:T(8,128)S(1)} %pad_maximum_fusion, s32[]{:T(128)S(6)} %select_n.83, s32[]{:T(128)S(6)} %select_n.82, s32[]{:T(128)S(6)} %select_n.81, s32[]{:T(128)S(6)} %select_n.80, s32[]{:T(128)S(6)} %select_n.79, ...), kind=kLoop, calls=%fused_computation.11 | loop fusion | flops 9216000 | bytes 23593008 | tf_op jit(solution)/shard_map/add | solution.py:49
  84.0 0.4 fusion.21
  84.4 0.8 copy-done
  85.2 0.0 collective-permute-start.15
  85.2 0.5 collective-permute-start.14
  85.7 0.1 copy-done.2
  85.9 0.4 fusion.22
  86.3 5.5 %collective-permute-start.13 = (f32[9,18,2048]{2,1,0:T(8,128)S(1)}, f32[9,18,2048]{2,1,0:T(8,128)}, u32[]{:S(2)}, u32[]{:S(2)}) collective-permute-start(f32[9,18,2048]{2,1,0:T(8,128)S(1)} %get-tuple-element.27), channel_id=1, source_target_pairs={{8,0},{16,8},{24,16},{32,24},{40,32},{48,40},{56,48},{64,56},{72,6... | collective-permute-start | bytes 3981320 | tf_op jit(solution)/shard_map/ppermute | solution.py:183
  91.8 0.0 collective-permute-start.12
  91.9 0.0 copy-start.7
  91.9 1.7 fusion.23
  93.6 3.8 %collective-permute-start.11 = (f32[9,18,2048]{2,1,0:T(8,128)}, f32[9,18,2048]{2,1,0:T(8,128)S(1)}, u32[]{:S(2)}, u32[]{:S(2)}) collective-permute-start(f32[9,18,2048]{2,1,0:T(8,128)} %get-tuple-element.29), channel_id=1, source_target_pairs={{8,0},{16,8},{24,16},{32,24},{40,32},{48,40},{56,48},{64,56},{72,6... | collective-permute-start | bytes 3981320 | tf_op jit(solution)/shard_map/ppermute | solution.py:183
  97.5 7.8 %collective-permute-done.15.refs_3_ = f32[9,18,2048]{2,1,0:T(8,128)S(1)} collective-permute-done((f32[9,18,2048]{2,1,0:T(8,128)S(1)}, f32[9,18,2048]{2,1,0:T(8,128)S(1)}, u32[]{:S(2)}, u32[]{:S(2)}) %collective-permute-start.15) | collective-permute-done | bytes 1327136 | tf_op jit(solution)/shard_map/ppermute | solution.py:183
  105.3 2.6 %collective-permute-start.10 = (f32[9,18,2048]{2,1,0:T(8,128)S(1)}, f32[9,18,2048]{2,1,0:T(8,128)}, u32[]{:S(2)}, u32[]{:S(2)}) collective-permute-start(f32[9,18,2048]{2,1,0:T(8,128)S(1)} %get-tuple-element.30), channel_id=1, source_target_pairs={{0,8},{8,16},{16,24},{24,32},{32,40},{40,48},{48,56},{56,64},{64,7... | collective-permute-start | bytes 3981320 | tf_op jit(solution)/shard_map/ppermute | solution.py:182
  107.9 3.7 %collective-permute-done.14.refs_1_ = f32[9,18,2048]{2,1,0:T(8,128)} collective-permute-done((f32[9,18,2048]{2,1,0:T(8,128)S(1)}, f32[9,18,2048]{2,1,0:T(8,128)}, u32[]{:S(2)}, u32[]{:S(2)}) %collective-permute-start.14) | collective-permute-done | bytes 1327136 | tf_op jit(solution)/shard_map/ppermute | solution.py:182
  111.6 12.9 %shard_map.77 = (f32[10,16,2048]{2,1,0:T(8,128)}, f32[10,16,2048]{2,1,0:T(8,128)}) custom-call(s32[3]{0:T(128)} %refs_0_.5, f32[9,18,2048]{2,1,0:T(8,128)} %collective-permute-done.14.refs_1_, f32[10,18,2048]{2,1,0:T(8,128)} %copy-done, f32[9,18,2048]{2,1,0:T(8,128)} %copy-done.5), custom_call_target="tpu_custom_call" | custom-call | tf_op jit(solution)/shard_map/pallas_call | solution.py:161
  124.6 6.0 %collective-permute-done.12.refs_1_ = f32[9,18,2048]{2,1,0:T(8,128)} collective-permute-done((f32[9,18,2048]{2,1,0:T(8,128)S(1)}, f32[9,18,2048]{2,1,0:T(8,128)}, u32[]{:S(2)}, u32[]{:S(2)}) %collective-permute-start.12) | collective-permute-done | bytes 1327136 | tf_op jit(solution)/shard_map/ppermute | solution.py:182
  130.6 14.0 %shard_map.78 = (f32[10,16,2048]{2,1,0:T(8,128)}, f32[10,16,2048]{2,1,0:T(8,128)}) custom-call(s32[3]{0:T(128)} %refs_0_.5, f32[9,18,2048]{2,1,0:T(8,128)} %collective-permute-done.12.refs_1_, f32[10,18,2048]{2,1,0:T(8,128)} %copy-done.2, f32[9,18,2048]{2,1,0:T(8,128)} %collective-permute-done.13.refs_3_, f32[10,16,2048]{2,1,0:T(8,128)} %get-tuple-element.8.refs_4_), custom_call_target="tpu_custom_call" | custom-call | tf_op jit(solution)/shard_map/pallas_call | solution.py:161
  144.6 1.8 fusion.12
  146.4 1.8 fusion.11
  148.2 1.3 collective-permute-done.10.refs_1_
  149.5 13.6 %shard_map.79 = (f32[10,16,2048]{2,1,0:T(8,128)}, f32[10,16,2048]{2,1,0:T(8,128)}) custom-call(s32[3]{0:T(128)} %refs_0_.5, f32[9,18,2048]{2,1,0:T(8,128)} %collective-permute-done.10.refs_1_, f32[10,18,2048]{2,1,0:T(8,128)} %copy-done.1, f32[9,18,2048]{2,1,0:T(8,128)} %copy-done.4, f32[10,16,2048]{2,1,0:T(8,128)} %get-tuple-element.9.refs_4_), custom_call_target="tpu_custom_call" | custom-call | tf_op jit(solution)/shard_map/pallas_call | solution.py:161
  163.2 3.1 %fusion.10 = f32[512]{0:T(512)S(1)} fusion(f32[160,2048]{1,0:T(8,128)} %bitcast.58, s32[512]{0:T(512)S(1)} %get-tuple-element.54, f32[512]{0:T(512)S(1)} %get-tuple-element.61, s32[512]{0:T(512)S(1)} %pad_add_fusion.4, f32[512]{0:T(512)S(1)} %get-tuple-element.60, s32[512]{0:T(512)S(1)} %get-tuple-element.57, f32[512]{0:T(512)S(1)} %get-tuple-element.59, ...), kind=kOutput, calls=%fused_computation.17 | convolution fusion | flops 2015378944 | bytes 1331200 | tf_op jit(solution)/shard_map/dot_general | solution.py:272
  166.3 0.8 fusion.6
  167.1 15.5 %all_to_all.5 = f32[3,8,256]{2,0,1:T(4,128)S(1)} all-to-all(f32[3,8,256]{2,0,1:T(4,128)S(1)} %bitcast.43), channel_id=1, replica_groups=mesh['gz'=32,'gy'=8] {'gy'}, dimensions={1} | all-to-all | bytes 49152 | tf_op jit(solution)/shard_map/all_to_all | solution.py:287
  182.7 0.6 reduce_sum.39
  (49 shorter events, 0.3 us)
Async XLA Ops:
  0.6 13.0 %copy-start.6 = (s32[3]{0:T(128)S(1)}, s32[3]{0:T(128)}, u32[]{:S(2)}) copy-start(s32[3]{0:T(128)} %refs_0_.5) | copy-start | bytes 40
  0.6 23.3 %copy-start.10 = (s32[256,1]{0,1:T(1,128)S(1)}, s32[256,1]{0,1:T(1,128)}, u32[]{:S(2)}) copy-start(s32[256,1]{0,1:T(1,128)} %param.8) | copy-start | bytes 3076
  0.7 23.3 %copy-start.8 = (s32[256]{0:T(256)S(1)}, s32[256]{0:T(256)}, u32[]{:S(2)}) copy-start(s32[256]{0:T(256)} %param.10) | copy-start | bytes 3076
  0.7 23.4 %copy-start.9 = (s32[256]{0:T(256)S(1)}, s32[256]{0:T(256)}, u32[]{:S(2)}) copy-start(s32[256]{0:T(256)} %param.9) | copy-start | bytes 3076
  2.7 70.8 %collective-permute-start.4 = (f32[2,9,2048]{2,1,0:T(8,128)S(1)}, f32[2,9,2048]{2,1,0:T(8,128)S(1)}, u32[]{:S(2)}, u32[]{:S(2)}) collective-permute-start(f32[2,9,2048]{2,1,0:T(8,128)S(1)} %get-tuple-element.31), channel_id=1, source_target_pairs={{0,1},{1,2},{2,3},{3,4},{4,5},{5,6},{6,7},{7,0},{8,9},{9,10},{10,1... | collective-permute-start | bytes 442376 | tf_op jit(solution)/shard_map/ppermute | solution.py:22
  6.0 68.5 %collective-permute-start.8 = (f32[2,9,2048]{2,1,0:T(8,128)S(1)}, f32[2,9,2048]{2,1,0:T(8,128)S(1)}, u32[]{:S(2)}, u32[]{:S(2)}) collective-permute-start(f32[2,9,2048]{2,1,0:T(8,128)S(1)} %get-tuple-element.32), channel_id=1, source_target_pairs={{1,0},{2,1},{3,2},{4,3},{5,4},{6,5},{7,6},{0,7},{9,8},{10,9},{11,1... | collective-permute-start | bytes 442376 | tf_op jit(solution)/shard_map/ppermute | solution.py:22
  7.2 67.3 %collective-permute-start.7 = (f32[2,9,2048]{2,1,0:T(8,128)S(1)}, f32[2,9,2048]{2,1,0:T(8,128)S(1)}, u32[]{:S(2)}, u32[]{:S(2)}) collective-permute-start(f32[2,9,2048]{2,1,0:T(8,128)S(1)} %get-tuple-element.33), channel_id=1, source_target_pairs={{1,0},{2,1},{3,2},{4,3},{5,4},{6,5},{7,6},{0,7},{9,8},{10,9},{11,1... | collective-permute-start | bytes 442376 | tf_op jit(solution)/shard_map/ppermute | solution.py:22
  9.5 64.0 %collective-permute-start.6 = (f32[2,9,2048]{2,1,0:T(8,128)S(1)}, f32[2,9,2048]{2,1,0:T(8,128)}, u32[]{:S(2)}, u32[]{:S(2)}) collective-permute-start(f32[2,9,2048]{2,1,0:T(8,128)S(1)} %get-tuple-element.34), channel_id=1, source_target_pairs={{1,0},{2,1},{3,2},{4,3},{5,4},{6,5},{7,6},{0,7},{9,8},{10,9},{11,1... | collective-permute-start | bytes 442376 | tf_op jit(solution)/shard_map/ppermute | solution.py:22
  13.7 20.4 %collective-permute-start = (f32[2,9,2048]{2,1,0:T(8,128)S(1)}, f32[2,9,2048]{2,1,0:T(8,128)}, u32[]{:S(2)}, u32[]{:S(2)}) collective-permute-start(f32[2,9,2048]{2,1,0:T(8,128)S(1)} %get-tuple-element.39), channel_id=1, source_target_pairs={{0,1},{1,2},{2,3},{3,4},{4,5},{5,6},{6,7},{7,0},{8,9},{9,10},{10,1... | collective-permute-start | bytes 442376 | tf_op jit(solution)/shard_map/ppermute | solution.py:22
  34.0 9.5 %collective-permute-start.5 = (f32[2,9,2048]{2,1,0:T(8,128)S(1)}, f32[2,9,2048]{2,1,0:T(8,128)S(1)}, u32[]{:S(2)}, u32[]{:S(2)}) collective-permute-start(f32[2,9,2048]{2,1,0:T(8,128)S(1)} %get-tuple-element.35), channel_id=1, source_target_pairs={{1,0},{2,1},{3,2},{4,3},{5,4},{6,5},{7,6},{0,7},{9,8},{10,9},{11,1... | collective-permute-start | bytes 442376 | tf_op jit(solution)/shard_map/ppermute | solution.py:22
  43.5 8.9 %collective-permute-start.1 = (f32[2,9,2048]{2,1,0:T(8,128)S(1)}, f32[2,9,2048]{2,1,0:T(8,128)S(1)}, u32[]{:S(2)}, u32[]{:S(2)}) collective-permute-start(f32[2,9,2048]{2,1,0:T(8,128)S(1)} %get-tuple-element.38), channel_id=1, source_target_pairs={{0,1},{1,2},{2,3},{3,4},{4,5},{5,6},{6,7},{7,0},{8,9},{9,10},{10,1... | collective-permute-start | bytes 442376 | tf_op jit(solution)/shard_map/ppermute | solution.py:22
  52.5 8.8 %collective-permute-start.2 = (f32[2,9,2048]{2,1,0:T(8,128)S(1)}, f32[2,9,2048]{2,1,0:T(8,128)S(1)}, u32[]{:S(2)}, u32[]{:S(2)}) collective-permute-start(f32[2,9,2048]{2,1,0:T(8,128)S(1)} %get-tuple-element.37), channel_id=1, source_target_pairs={{0,1},{1,2},{2,3},{3,4},{4,5},{5,6},{6,7},{7,0},{8,9},{9,10},{10,1... | collective-permute-start | bytes 442376 | tf_op jit(solution)/shard_map/ppermute | solution.py:22
  61.3 17.3 %copy-start.3 = (f32[10,16,2048]{2,1,0:T(8,128)S(1)}, f32[10,16,2048]{2,1,0:T(8,128)}, u32[]{:S(2)}) copy-start(f32[10,16,2048]{2,1,0:T(8,128)} %param.6) | copy-start | bytes 3932164
  61.3 9.0 %collective-permute-start.3 = (f32[2,9,2048]{2,1,0:T(8,128)S(1)}, f32[2,9,2048]{2,1,0:T(8,128)S(1)}, u32[]{:S(2)}, u32[]{:S(2)}) collective-permute-start(f32[2,9,2048]{2,1,0:T(8,128)S(1)} %get-tuple-element.36), channel_id=1, source_target_pairs={{0,1},{1,2},{2,3},{3,4},{4,5},{5,6},{6,7},{7,0},{8,9},{9,10},{10,1... | collective-permute-start | bytes 442376 | tf_op jit(solution)/shard_map/ppermute | solution.py:22
  70.3 8.3 %collective-permute-start.9 = (f32[2,9,2048]{2,1,0:T(8,128)S(1)}, f32[2,9,2048]{2,1,0:T(8,128)S(1)}, u32[]{:S(2)}, u32[]{:S(2)}) collective-permute-start(f32[2,9,2048]{2,1,0:T(8,128)S(1)} %get-tuple-element.40), channel_id=1, source_target_pairs={{1,0},{2,1},{3,2},{4,3},{5,4},{6,5},{7,6},{0,7},{9,8},{10,9},{11,1... | collective-permute-start | bytes 442376 | tf_op jit(solution)/shard_map/ppermute | solution.py:22
  83.9 1.3 copy-start
  83.9 1.9 %copy-start.2 = (f32[10,18,2048]{2,1,0:T(8,128)}, f32[10,18,2048]{2,1,0:T(8,128)S(1)}, u32[]{:S(2)}) copy-start(f32[10,18,2048]{2,1,0:T(8,128)S(1)} %get-tuple-element.23.refs_2_) | copy-start | bytes 4423684
  84.0 7.9 %copy-start.1 = (f32[10,18,2048]{2,1,0:T(8,128)}, f32[10,18,2048]{2,1,0:T(8,128)S(1)}, u32[]{:S(2)}) copy-start(f32[10,18,2048]{2,1,0:T(8,128)S(1)} %get-tuple-element.24.refs_2_) | copy-start | bytes 4423684
  85.2 20.0 %collective-permute-start.15 = (f32[9,18,2048]{2,1,0:T(8,128)S(1)}, f32[9,18,2048]{2,1,0:T(8,128)S(1)}, u32[]{:S(2)}, u32[]{:S(2)}) collective-permute-start(f32[9,18,2048]{2,1,0:T(8,128)S(1)} %get-tuple-element.25), channel_id=1, source_target_pairs={{8,0},{16,8},{24,16},{32,24},{40,32},{48,40},{56,48},{64,56},{72,6... | collective-permute-start | bytes 3981320 | tf_op jit(solution)/shard_map/ppermute | solution.py:183
  85.2 26.4 %collective-permute-start.14 = (f32[9,18,2048]{2,1,0:T(8,128)S(1)}, f32[9,18,2048]{2,1,0:T(8,128)}, u32[]{:S(2)}, u32[]{:S(2)}) collective-permute-start(f32[9,18,2048]{2,1,0:T(8,128)S(1)} %get-tuple-element.26), channel_id=1, source_target_pairs={{0,8},{8,16},{16,24},{24,32},{32,40},{40,48},{48,56},{56,64},{64,7... | collective-permute-start | bytes 3981320 | tf_op jit(solution)/shard_map/ppermute | solution.py:182
  86.3 38.3 %collective-permute-start.13 = (f32[9,18,2048]{2,1,0:T(8,128)S(1)}, f32[9,18,2048]{2,1,0:T(8,128)}, u32[]{:S(2)}, u32[]{:S(2)}) collective-permute-start(f32[9,18,2048]{2,1,0:T(8,128)S(1)} %get-tuple-element.27), channel_id=1, source_target_pairs={{8,0},{16,8},{24,16},{32,24},{40,32},{48,40},{56,48},{64,56},{72,6... | collective-permute-start | bytes 3981320 | tf_op jit(solution)/shard_map/ppermute | solution.py:183
  91.8 38.8 %collective-permute-start.12 = (f32[9,18,2048]{2,1,0:T(8,128)S(1)}, f32[9,18,2048]{2,1,0:T(8,128)}, u32[]{:S(2)}, u32[]{:S(2)}) collective-permute-start(f32[9,18,2048]{2,1,0:T(8,128)S(1)} %get-tuple-element.28), channel_id=1, source_target_pairs={{0,8},{8,16},{16,24},{24,32},{32,40},{40,48},{48,56},{56,64},{64,7... | collective-permute-start | bytes 3981320 | tf_op jit(solution)/shard_map/ppermute | solution.py:182
  91.9 16.0 %copy-start.7 = (f32[8,256]{1,0:T(8,128)S(1)}, f32[8,256]{1,0:T(8,128)}, u32[]{:S(2)}) copy-start(f32[8,256]{1,0:T(8,128)} %param.11) | copy-start | bytes 24580
  93.6 54.6 %collective-permute-start.11 = (f32[9,18,2048]{2,1,0:T(8,128)}, f32[9,18,2048]{2,1,0:T(8,128)S(1)}, u32[]{:S(2)}, u32[]{:S(2)}) collective-permute-start(f32[9,18,2048]{2,1,0:T(8,128)} %get-tuple-element.29), channel_id=1, source_target_pairs={{8,0},{16,8},{24,16},{32,24},{40,32},{48,40},{56,48},{64,56},{72,6... | collective-permute-start | bytes 3981320 | tf_op jit(solution)/shard_map/ppermute | solution.py:183
  105.3 2.6 %copy-start.5 = (f32[9,18,2048]{2,1,0:T(8,128)}, f32[9,18,2048]{2,1,0:T(8,128)S(1)}, u32[]{:S(2)}) copy-start(f32[9,18,2048]{2,1,0:T(8,128)S(1)} %collective-permute-done.15.refs_3_) | copy-start | bytes 3981316
  105.3 44.3 %collective-permute-start.10 = (f32[9,18,2048]{2,1,0:T(8,128)S(1)}, f32[9,18,2048]{2,1,0:T(8,128)}, u32[]{:S(2)}, u32[]{:S(2)}) collective-permute-start(f32[9,18,2048]{2,1,0:T(8,128)S(1)} %get-tuple-element.30), channel_id=1, source_target_pairs={{0,8},{8,16},{16,24},{24,32},{32,40},{40,48},{48,56},{56,64},{64,7... | collective-permute-start | bytes 3981320 | tf_op jit(solution)/shard_map/ppermute | solution.py:182
  130.6 14.0 %copy-start.11 = (f32[10,16,2048]{2,1,0:T(8,128)S(1)}, f32[10,16,2048]{2,1,0:T(8,128)}, u32[]{:S(2)}) copy-start(f32[10,16,2048]{2,1,0:T(8,128)} %get-tuple-element.11) | copy-start | bytes 3932164
  144.6 1.8 copy-start.12
  148.2 1.4 copy-start.4

commit v6 on v2

--- a/solution.py
+++ b/solution.py
@@ -53,17 +53,20 @@
 
     def compute(dilation, a_scr, s_scr, feature_ref, prev_ref, best_ref):
         def smooth_plane(plane, carry):
-            along_z = None
-            for offset in range(5):
-                summand = tap_weights[offset] * a_scr[HALO - 1 + plane + (offset - 2) * dilation]
-                along_z = summand if along_z is None else along_z + summand
-            running = None
-            for offset in range(5):
-                shift = (-(offset - 2) * dilation) % row_length
-                moved = along_z if shift == 0 else pltpu.roll(along_z, shift, 1)
-                summand = tap_weights[offset] * moved
-                running = summand if running is None else running + summand
-            s_scr[plane] = running
+            for first_row in range(0, band_rows + 2, 8):
+                rows = min(8, band_rows + 2 - first_row)
+                along_z = None
+                for offset in range(5):
+                    source = HALO - 1 + plane + (offset - 2) * dilation
+                    summand = tap_weights[offset] * a_scr[source, pl.ds(first_row, rows), :]
+                    along_z = summand if along_z is None else along_z + summand
+                running = None
+                for offset in range(5):
+                    shift = (-(offset - 2) * dilation) % row_length
+                    moved = along_z if shift == 0 else pltpu.roll(along_z, shift, 1)
+                    summand = tap_weights[offset] * moved
+                    running = summand if running is None else running + summand
+                s_scr[plane, pl.ds(first_row, rows), :] = running
             return carry
 
         lax.fori_loop(0, planes, smooth_plane, 0)
@@ -75,37 +78,29 @@
                 def at(dz, dy):
                     return s_scr[z + 1 + dz, pl.ds(1 + y0 + dy, 8), :]
 
+                def left(v):
+                    return pltpu.roll(v, row_length - 1, 1)
+
+                def right(v):
+                    return pltpu.roll(v, 1, 1)
+
                 centre = at(0, 0)
                 above_z = at(1, 0)
                 below_z = at(-1, 0)
+                curve_zz = hessian_scale * (above_z - 2.0 * centre + below_z)
+                across_z = above_z - below_z
+                curve_zx = (hessian_scale * 0.25) * (left(across_z) - right(across_z))
                 above_y = at(0, 1)
                 below_y = at(0, -1)
-
-                def left(v):
-                    return pltpu.roll(v, row_length - 1, 1)
-
-                def right(v):
-                    return pltpu.roll(v, 1, 1)
-
-                curve_zz = hessian_scale * (above_z - 2.0 * centre + below_z)
                 curve_yy = hessian_scale * (above_y - 2.0 * centre + below_y)
+                across_y = above_y - below_y
+                curve_yx = (hessian_scale * 0.25) * (left(across_y) - right(across_y))
                 curve_xx = hessian_scale * (left(centre) - 2.0 * centre + right(centre))
+                trace_sum = curve_xx + curve_yy + curve_zz
+                minor_sum = curve_xx * curve_yy + curve_xx * curve_zz + curve_yy * curve_zz
+                minor_sum = minor_sum - curve_zx * curve_zx - curve_yx * curve_yx
                 curve_zy = (hessian_scale * 0.25) * (at(1, 1) - at(1, -1) - at(-1, 1) + at(-1, -1))
-                curve_zx = (hessian_scale * 0.25) * (
-                    left(above_z) - right(above_z) - left(below_z) + right(below_z)
-                )
-                curve_yx = (hessian_scale * 0.25) * (
-                    left(above_y) - right(above_y) - left(below_y) + right(below_y)
-                )
-                trace_sum = curve_xx + curve_yy + curve_zz
-                minor_sum = (
-                    curve_xx * curve_yy
-                    + curve_xx * curve_zz
-                    + curve_yy * curve_zz
-                    - curve_zy * curve_zy
-                    - curve_zx * curve_zx
-                    - curve_yx * curve_yx
-                )
+                minor_sum = minor_sum - curve_zy * curve_zy
                 value = (trace_sum * trace_sum / 3.0 - minor_sum) * (1.0 / (1.0 + jnp.exp(trace_sum)))
                 feature_ref[z, pl.ds(y0, 8), :] = value
                 if first:

time: 168 us -> 167 us (level)
  transfers between devices with their start and end apart: 8 -> 8, of which waited for: 6 -> 6; matrix products, arithmetic and copies ran while one was open for 4% -> 4% of each run, Pallas kernels for 16% -> 15%
where the time goes in v6:
time: 167 us
  waiting for transfers between devices  61.4 us (37%)
  Pallas kernels  39.2 us (23%)
  starting transfers between devices  16.9 us (10%)
  blocking collectives  14.8 us (9%)
  between operations  10.7 us (6%)
  local copies, waits for them, and re-layouts  10.4 us (6%)
  matrix products  7.46 us (4%)
  other arithmetic  6.03 us (4%)
    ppermute x1, waiting for transfers between devices, with_halo(): lax.ppermute(lax.slice_in_dim(block, 0, width, axis=dim), axis, backward)  40 us
    pallas_call x3, Pallas kernels, run(): pl.pallas_call(kernel, out_shape=(block, block), in_specs=in_specs, out_s...  39.2 us
    all_to_all x1, blocking collectives, per_device(): lax.all_to_all(spread.reshape(SCALES, groups, HOWN), 'gy', split_axis=1,...  14.8 us
    ppermute x3, starting transfers between devices, z_neighbours(): lax.ppermute(lax.slice_in_dim(block, 0, width, axis=0), 'gz', backward)  13.2 us
    ppermute x3, waiting for transfers between devices, z_neighbours(): lax.ppermute(lax.slice_in_dim(block, 0, width, axis=0), 'gz', backward)  12.4 us
    ppermute x3, waiting for transfers between devices, z_neighbours(): lax.ppermute(lax.slice_in_dim(block, block.shape[0] - width, None, axis=0...  9.01 us
    dot_general x3, matrix products, per_device(): jnp.dot(feature, pick_x, precision=lax.Precision.HIGHEST, preferred_eleme...  6.64 us
    add x1, other arithmetic, smooth_padded(): running = summand if running is None else running + summand  4.89 us
  transfers between devices with their start and end apart: 8, of which 6 were waited for; matrix products, arithmetic and copies ran while one was open for 4% of the time, Pallas kernels for 15%

profile of v6, /device:TPU:2, one launch (start us, length us, event | category | flops | bytes accessed | tf_op | source)
XLA Modules:
  0.0 166.9 jit_solution(18026719296227403542)
XLA Ops:
  0.6 2.0 %fusion.24 = (f32[10,9,2048]{2,1,0:T(8,128)S(1)}, f32[10,9,2048]{2,1,0:T(8,128)S(1)}) fusion(f32[10,16,2048]{2,1,0:T(8,128)} %param.6), kind=kLoop, calls=%fused_computation.66 | loop fusion | bytes 2949120 | tf_op jit(solution)/shard_map/slice | solution.py:25
  2.7 0.0 copy-start.6
  2.7 0.0 copy-start.10
  2.7 0.0 copy-start.8
  2.7 0.0 copy-start.9
  2.7 0.4 copy.14
  3.2 3.2 %collective-permute-start.1 = (f32[10,9,2048]{2,0,1:T(8,128)S(1)}, f32[10,9,2048]{2,0,1:T(8,128)S(1)}, u32[]{:S(2)}, u32[]{:S(2)}) collective-permute-start(f32[10,9,2048]{2,0,1:T(8,128)S(1)} %copy.14), channel_id=1, source_target_pairs={{1,0},{2,1},{3,2},{4,3},{5,4},{6,5},{7,6},{0,7},{9,8},{10,9},{11,1... | collective-permute-start | bytes 2211848 | tf_op jit(solution)/shard_map/ppermute | solution.py:27
  6.4 0.4 copy.13
  6.9 0.4 collective-permute-start
  7.3 0.6 fusion.26
  17.6 0.0 copy-done.8
  17.7 0.0 copy-start.3
  17.7 40.0 %collective-permute-done.1 = f32[10,9,2048]{2,0,1:T(8,128)S(1)} collective-permute-done((f32[10,9,2048]{2,0,1:T(8,128)S(1)}, f32[10,9,2048]{2,0,1:T(8,128)S(1)}, u32[]{:S(2)}, u32[]{:S(2)}) %collective-permute-start.1) | collective-permute-done | bytes 737312 | tf_op jit(solution)/shard_map/ppermute | solution.py:27
  57.7 0.5 copy.11
  58.2 0.0 collective-permute-done
  58.2 1.7 %copy.10 = f32[10,9,2048]{2,1,0:T(8,128)S(1)} copy(f32[10,9,2048]{2,0,1:T(8,128)} %collective-permute-done) | data formatting | bytes 1474560 | tf_op jit(solution)/shard_map/ppermute | solution.py:24
  60.0 0.4 pad_maximum_fusion
  60.4 4.9 %multiply_add_fusion = (f32[10,18,2048]{2,1,0:T(8,128)S(1)}, f32[10,18,2048]{2,1,0:T(8,128)S(1)}, f32[10,18,2048]{2,1,0:T(8,128)S(1)}) fusion(f32[10,34,2048]{2,1,0:T(8,128)S(1)} %pad_maximum_fusion, s32[]{:T(128)S(6)} %select_n.83, s32[]{:T(128)S(6)} %select_n.82, s32[]{:T(128)S(6)} %select_n.81, s32[]{:T(128)S(6)} %select_n.80, s32[]{:T(128)S(6)} %select_n.79, ...), kind=kLoop, calls=%fused_computation.11 | loop fusion | flops 9216000 | bytes 23593008 | tf_op jit(solution)/shard_map/add | solution.py:39
  65.3 0.4 fusion.21
  65.7 0.8 copy-done
  66.6 5.4 %collective-permute-start.7 = (f32[9,18,2048]{2,1,0:T(8,128)S(1)}, f32[9,18,2048]{2,1,0:T(8,128)S(1)}, u32[]{:S(2)}, u32[]{:S(2)}) collective-permute-start(f32[9,18,2048]{2,1,0:T(8,128)S(1)} %get-tuple-element.25), channel_id=1, source_target_pairs={{8,0},{16,8},{24,16},{32,24},{40,32},{48,40},{56,48},{64,56},{72,6... | collective-permute-start | bytes 3981320 | tf_op jit(solution)/shard_map/ppermute | solution.py:168
  72.0 0.0 collective-permute-start.6
  72.0 0.0 copy-done.2
  72.0 0.4 fusion.22
  72.5 3.9 %collective-permute-start.5 = (f32[9,18,2048]{2,1,0:T(8,128)S(1)}, f32[9,18,2048]{2,1,0:T(8,128)}, u32[]{:S(2)}, u32[]{:S(2)}) collective-permute-start(f32[9,18,2048]{2,1,0:T(8,128)S(1)} %get-tuple-element.27), channel_id=1, source_target_pairs={{8,0},{16,8},{24,16},{32,24},{40,32},{48,40},{56,48},{64,56},{72,6... | collective-permute-start | bytes 3981320 | tf_op jit(solution)/shard_map/ppermute | solution.py:168
  76.4 0.0 collective-permute-start.4
  76.4 0.0 copy-start.7
  76.4 1.8 %fusion.23 = (f32[9,18,2048]{2,1,0:T(8,128)}, f32[9,18,2048]{2,1,0:T(8,128)S(1)}) fusion(f32[10,18,2048]{2,1,0:T(8,128)S(1)} %get-tuple-element.24.refs_2_), kind=kLoop, calls=%fused_computation.65 | loop fusion | bytes 5308416 | tf_op jit(solution)/shard_map/slice | solution.py:168
  78.2 3.8 %collective-permute-start.3 = (f32[9,18,2048]{2,1,0:T(8,128)}, f32[9,18,2048]{2,1,0:T(8,128)S(1)}, u32[]{:S(2)}, u32[]{:S(2)}) collective-permute-start(f32[9,18,2048]{2,1,0:T(8,128)} %get-tuple-element.29), channel_id=1, source_target_pairs={{8,0},{16,8},{24,16},{32,24},{40,32},{48,40},{56,48},{64,56},{72,6... | collective-permute-start | bytes 3981320 | tf_op jit(solution)/shard_map/ppermute | solution.py:168
  82.0 10.0 %collective-permute-done.7.refs_3_ = f32[9,18,2048]{2,1,0:T(8,128)S(1)} collective-permute-done((f32[9,18,2048]{2,1,0:T(8,128)S(1)}, f32[9,18,2048]{2,1,0:T(8,128)S(1)}, u32[]{:S(2)}, u32[]{:S(2)}) %collective-permute-start.7) | collective-permute-done | bytes 1327136 | tf_op jit(solution)/shard_map/ppermute | solution.py:168
  92.1 0.0 collective-permute-start.2
  92.1 1.2 copy-done.5
  93.3 2.9 %collective-permute-done.6.refs_1_ = f32[9,18,2048]{2,1,0:T(8,128)} collective-permute-done((f32[9,18,2048]{2,1,0:T(8,128)S(1)}, f32[9,18,2048]{2,1,0:T(8,128)}, u32[]{:S(2)}, u32[]{:S(2)}) %collective-permute-start.6) | collective-permute-done | bytes 1327136 | tf_op jit(solution)/shard_map/ppermute | solution.py:167
  96.2 12.5 %shard_map.77 = (f32[10,16,2048]{2,1,0:T(8,128)}, f32[10,16,2048]{2,1,0:T(8,128)}) custom-call(s32[3]{0:T(128)} %refs_0_.5, f32[9,18,2048]{2,1,0:T(8,128)} %collective-permute-done.6.refs_1_, f32[10,18,2048]{2,1,0:T(8,128)} %copy-done, f32[9,18,2048]{2,1,0:T(8,128)} %copy-done.5), custom_call_target="tpu_custom_call" | custom-call | tf_op jit(solution)/shard_map/pallas_call | solution.py:146
  108.7 2.3 %collective-permute-done.5.refs_3_ = f32[9,18,2048]{2,1,0:T(8,128)} collective-permute-done((f32[9,18,2048]{2,1,0:T(8,128)S(1)}, f32[9,18,2048]{2,1,0:T(8,128)}, u32[]{:S(2)}, u32[]{:S(2)}) %collective-permute-start.5) | collective-permute-done | bytes 1327136 | tf_op jit(solution)/shard_map/ppermute | solution.py:168
  111.0 4.1 %collective-permute-done.4.refs_1_ = f32[9,18,2048]{2,1,0:T(8,128)} collective-permute-done((f32[9,18,2048]{2,1,0:T(8,128)S(1)}, f32[9,18,2048]{2,1,0:T(8,128)}, u32[]{:S(2)}, u32[]{:S(2)}) %collective-permute-start.4) | collective-permute-done | bytes 1327136 | tf_op jit(solution)/shard_map/ppermute | solution.py:167
  115.1 13.3 %shard_map.78 = (f32[10,16,2048]{2,1,0:T(8,128)}, f32[10,16,2048]{2,1,0:T(8,128)}) custom-call(s32[3]{0:T(128)} %refs_0_.5, f32[9,18,2048]{2,1,0:T(8,128)} %collective-permute-done.4.refs_1_, f32[10,18,2048]{2,1,0:T(8,128)} %copy-done.2, f32[9,18,2048]{2,1,0:T(8,128)} %collective-permute-done.5.refs_3_, f32[10,16,2048]{2,1,0:T(8,128)} %get-tuple-element.8.refs_4_), custom_call_target="tpu_custom_call" | custom-call | tf_op jit(solution)/shard_map/pallas_call | solution.py:146
  128.5 0.0 copy-start.12
  128.5 0.0 copy-done.11
  128.5 1.8 %fusion.12 = f32[512]{0:T(512)S(1)} fusion(f32[160,2048]{1,0:T(8,128)S(1)} %bitcast.56, s32[512]{0:T(512)S(1)} %get-tuple-element.46, f32[512]{0:T(512)S(1)} %get-tuple-element.53, s32[512]{0:T(512)S(1)} %pad_add_fusion.4, f32[512]{0:T(512)S(1)} %get-tuple-element.52, s32[512]{0:T(512)S(1)} %get-tuple-element.49, f32[512]{0:T(512)S(1)} %get-tuple-element.51, ...), kind=kOutput, calls=%fused_computation.19 | convolution fusion | flops 2015378944 | bytes 1331200 | tf_op jit(solution)/shard_map/dot_general | solution.py:257
  130.3 1.8 %fusion.11 = f32[512]{0:T(512)S(1)} fusion(f32[160,2048]{1,0:T(8,128)S(1)} %bitcast.57, s32[512]{0:T(512)S(1)} %get-tuple-element.46, f32[512]{0:T(512)S(1)} %get-tuple-element.53, s32[512]{0:T(512)S(1)} %pad_add_fusion.4, f32[512]{0:T(512)S(1)} %get-tuple-element.52, s32[512]{0:T(512)S(1)} %get-tuple-element.49, f32[512]{0:T(512)S(1)} %get-tuple-element.51, ...), kind=kOutput, calls=%fused_computation.18 | convolution fusion | flops 2015378944 | bytes 1331200 | tf_op jit(solution)/shard_map/dot_general | solution.py:257
  132.1 0.0 collective-permute-done.3.refs_3_
  132.1 2.0 %collective-permute-done.2.refs_1_ = f32[9,18,2048]{2,1,0:T(8,128)} collective-permute-done((f32[9,18,2048]{2,1,0:T(8,128)S(1)}, f32[9,18,2048]{2,1,0:T(8,128)}, u32[]{:S(2)}, u32[]{:S(2)}) %collective-permute-start.2) | collective-permute-done | bytes 1327136 | tf_op jit(solution)/shard_map/ppermute | solution.py:167
  134.1 13.4 %shard_map.79 = (f32[10,16,2048]{2,1,0:T(8,128)}, f32[10,16,2048]{2,1,0:T(8,128)}) custom-call(s32[3]{0:T(128)} %refs_0_.5, f32[9,18,2048]{2,1,0:T(8,128)} %collective-permute-done.2.refs_1_, f32[10,18,2048]{2,1,0:T(8,128)} %copy-done.1, f32[9,18,2048]{2,1,0:T(8,128)} %copy-done.4, f32[10,16,2048]{2,1,0:T(8,128)} %get-tuple-element.9.refs_4_), custom_call_target="tpu_custom_call" | custom-call | tf_op jit(solution)/shard_map/pallas_call | solution.py:146
  147.5 3.1 %fusion.10 = f32[512]{0:T(512)S(1)} fusion(f32[160,2048]{1,0:T(8,128)} %bitcast.58, s32[512]{0:T(512)S(1)} %get-tuple-element.46, f32[512]{0:T(512)S(1)} %get-tuple-element.53, s32[512]{0:T(512)S(1)} %pad_add_fusion.4, f32[512]{0:T(512)S(1)} %get-tuple-element.52, s32[512]{0:T(512)S(1)} %get-tuple-element.49, f32[512]{0:T(512)S(1)} %get-tuple-element.51, ...), kind=kOutput, calls=%fused_computation.17 | convolution fusion | flops 2015378944 | bytes 1331200 | tf_op jit(solution)/shard_map/dot_general | solution.py:257
  150.6 0.8 fusion.6
  151.5 14.8 %all_to_all.5 = f32[3,8,256]{2,0,1:T(4,128)S(1)} all-to-all(f32[3,8,256]{2,0,1:T(4,128)S(1)} %bitcast.43), channel_id=1, replica_groups=mesh['gz'=32,'gy'=8] {'gy'}, dimensions={1} | all-to-all | bytes 49152 | tf_op jit(solution)/shard_map/all_to_all | solution.py:272
  166.3 0.6 reduce_sum.39
  (27 shorter events, 0.1 us)
Async XLA Ops:
  2.7 4.6 %copy-start.6 = (s32[3]{0:T(128)S(1)}, s32[3]{0:T(128)}, u32[]{:S(2)}) copy-start(s32[3]{0:T(128)} %refs_0_.5) | copy-start | bytes 40
  2.7 14.9 %copy-start.10 = (s32[256,1]{0,1:T(1,128)S(1)}, s32[256,1]{0,1:T(1,128)}, u32[]{:S(2)}) copy-start(s32[256,1]{0,1:T(1,128)} %param.8) | copy-start | bytes 3076
  2.7 14.9 %copy-start.8 = (s32[256]{0:T(256)S(1)}, s32[256]{0:T(256)}, u32[]{:S(2)}) copy-start(s32[256]{0:T(256)} %param.9) | copy-start | bytes 3076
  2.7 15.0 %copy-start.9 = (s32[256]{0:T(256)S(1)}, s32[256]{0:T(256)}, u32[]{:S(2)}) copy-start(s32[256]{0:T(256)} %param.10) | copy-start | bytes 3076
  3.2 54.6 %collective-permute-start.1 = (f32[10,9,2048]{2,0,1:T(8,128)S(1)}, f32[10,9,2048]{2,0,1:T(8,128)S(1)}, u32[]{:S(2)}, u32[]{:S(2)}) collective-permute-start(f32[10,9,2048]{2,0,1:T(8,128)S(1)} %copy.14), channel_id=1, source_target_pairs={{1,0},{2,1},{3,2},{4,3},{5,4},{6,5},{7,6},{0,7},{9,8},{10,9},{11,1... | collective-permute-start | bytes 2211848 | tf_op jit(solution)/shard_map/ppermute | solution.py:27
  6.9 51.3 %collective-permute-start = (f32[10,9,2048]{2,0,1:T(8,128)S(1)}, f32[10,9,2048]{2,0,1:T(8,128)}, u32[]{:S(2)}, u32[]{:S(2)}) collective-permute-start(f32[10,9,2048]{2,0,1:T(8,128)S(1)} %copy.13), channel_id=1, source_target_pairs={{0,1},{1,2},{2,3},{3,4},{4,5},{5,6},{6,7},{7,0},{8,9},{9,10},{10,1... | collective-permute-start | bytes 2211848 | tf_op jit(solution)/shard_map/ppermute | solution.py:24
  17.7 42.2 %copy-start.3 = (f32[10,16,2048]{2,1,0:T(8,128)S(1)}, f32[10,16,2048]{2,1,0:T(8,128)}, u32[]{:S(2)}) copy-start(f32[10,16,2048]{2,1,0:T(8,128)} %param.6) | copy-start | bytes 3932164
  65.3 1.3 copy-start
  65.3 6.7 %copy-start.2 = (f32[10,18,2048]{2,1,0:T(8,128)}, f32[10,18,2048]{2,1,0:T(8,128)S(1)}, u32[]{:S(2)}) copy-start(f32[10,18,2048]{2,1,0:T(8,128)S(1)} %get-tuple-element.23.refs_2_) | copy-start | bytes 4423684
  65.3 11.1 %copy-start.1 = (f32[10,18,2048]{2,1,0:T(8,128)}, f32[10,18,2048]{2,1,0:T(8,128)S(1)}, u32[]{:S(2)}) copy-start(f32[10,18,2048]{2,1,0:T(8,128)S(1)} %get-tuple-element.24.refs_2_) | copy-start | bytes 4423684
  66.6 25.5 %collective-permute-start.7 = (f32[9,18,2048]{2,1,0:T(8,128)S(1)}, f32[9,18,2048]{2,1,0:T(8,128)S(1)}, u32[]{:S(2)}, u32[]{:S(2)}) collective-permute-start(f32[9,18,2048]{2,1,0:T(8,128)S(1)} %get-tuple-element.25), channel_id=1, source_target_pairs={{8,0},{16,8},{24,16},{32,24},{40,32},{48,40},{56,48},{64,56},{72,6... | collective-permute-start | bytes 3981320 | tf_op jit(solution)/shard_map/ppermute | solution.py:168
  72.0 24.2 %collective-permute-start.6 = (f32[9,18,2048]{2,1,0:T(8,128)S(1)}, f32[9,18,2048]{2,1,0:T(8,128)}, u32[]{:S(2)}, u32[]{:S(2)}) collective-permute-start(f32[9,18,2048]{2,1,0:T(8,128)S(1)} %get-tuple-element.26), channel_id=1, source_target_pairs={{0,8},{8,16},{16,24},{24,32},{32,40},{40,48},{48,56},{56,64},{64,7... | collective-permute-start | bytes 3981320 | tf_op jit(solution)/shard_map/ppermute | solution.py:167
  72.5 38.6 %collective-permute-start.5 = (f32[9,18,2048]{2,1,0:T(8,128)S(1)}, f32[9,18,2048]{2,1,0:T(8,128)}, u32[]{:S(2)}, u32[]{:S(2)}) collective-permute-start(f32[9,18,2048]{2,1,0:T(8,128)S(1)} %get-tuple-element.27), channel_id=1, source_target_pairs={{8,0},{16,8},{24,16},{32,24},{40,32},{48,40},{56,48},{64,56},{72,6... | collective-permute-start | bytes 3981320 | tf_op jit(solution)/shard_map/ppermute | solution.py:168
  76.4 38.8 %collective-permute-start.4 = (f32[9,18,2048]{2,1,0:T(8,128)S(1)}, f32[9,18,2048]{2,1,0:T(8,128)}, u32[]{:S(2)}, u32[]{:S(2)}) collective-permute-start(f32[9,18,2048]{2,1,0:T(8,128)S(1)} %get-tuple-element.28), channel_id=1, source_target_pairs={{0,8},{8,16},{16,24},{24,32},{32,40},{40,48},{48,56},{56,64},{64,7... | collective-permute-start | bytes 3981320 | tf_op jit(solution)/shard_map/ppermute | solution.py:167
  76.4 16.8 %copy-start.7 = (f32[8,256]{1,0:T(8,128)S(1)}, f32[8,256]{1,0:T(8,128)}, u32[]{:S(2)}) copy-start(f32[8,256]{1,0:T(8,128)} %param.11) | copy-start | bytes 24580
  78.2 53.9 %collective-permute-start.3 = (f32[9,18,2048]{2,1,0:T(8,128)}, f32[9,18,2048]{2,1,0:T(8,128)S(1)}, u32[]{:S(2)}, u32[]{:S(2)}) collective-permute-start(f32[9,18,2048]{2,1,0:T(8,128)} %get-tuple-element.29), channel_id=1, source_target_pairs={{8,0},{16,8},{24,16},{32,24},{40,32},{48,40},{56,48},{64,56},{72,6... | collective-permute-start | bytes 3981320 | tf_op jit(solution)/shard_map/ppermute | solution.py:168
  92.1 1.2 copy-start.5
  92.1 42.0 %collective-permute-start.2 = (f32[9,18,2048]{2,1,0:T(8,128)S(1)}, f32[9,18,2048]{2,1,0:T(8,128)}, u32[]{:S(2)}, u32[]{:S(2)}) collective-permute-start(f32[9,18,2048]{2,1,0:T(8,128)S(1)} %get-tuple-element.30), channel_id=1, source_target_pairs={{0,8},{8,16},{16,24},{24,32},{32,40},{40,48},{48,56},{56,64},{64,7... | collective-permute-start | bytes 3981320 | tf_op jit(solution)/shard_map/ppermute | solution.py:167
  115.1 13.3 %copy-start.11 = (f32[10,16,2048]{2,1,0:T(8,128)S(1)}, f32[10,16,2048]{2,1,0:T(8,128)}, u32[]{:S(2)}) copy-start(f32[10,16,2048]{2,1,0:T(8,128)} %get-tuple-element.11) | copy-start | bytes 3932164
  128.5 1.8 %copy-start.12 = (f32[10,16,2048]{2,1,0:T(8,128)S(1)}, f32[10,16,2048]{2,1,0:T(8,128)}, u32[]{:S(2)}) copy-start(f32[10,16,2048]{2,1,0:T(8,128)} %get-tuple-element.12) | copy-start | bytes 3932164
  132.1 2.0 %copy-start.4 = (f32[9,18,2048]{2,1,0:T(8,128)}, f32[9,18,2048]{2,1,0:T(8,128)S(1)}, u32[]{:S(2)}) copy-start(f32[9,18,2048]{2,1,0:T(8,128)S(1)} %collective-permute-done.3.refs_3_) | copy-start | bytes 3981316

commit v7 on v6

--- a/solution.py
+++ b/solution.py
@@ -51,8 +51,13 @@
 def level_kernel(level_index, first, slab_depth, band_rows, row_length):
     planes = slab_depth + 2
 
-    def compute(dilation, a_scr, s_scr, feature_ref, prev_ref, best_ref):
+    def compute(dilation, a_scr, s_scr, feature_ref, prev_ref, best_ref, row_wait, prev_copy, out_copy):
+        reach = HALO - 1 + 2 * dilation
+        for row in range(reach):
+            row_wait(row)
+
         def smooth_plane(plane, carry):
+            row_wait(reach + plane)
             for first_row in range(0, band_rows + 2, 8):
                 rows = min(8, band_rows + 2 - first_row)
                 along_z = None
@@ -70,6 +75,10 @@
             return carry
 
         lax.fori_loop(0, planes, smooth_plane, 0)
+        for row in range(reach + planes, planes + 2 * HALO - 2):
+            row_wait(row)
+        if prev_copy is not None:
+            prev_copy.wait()
 
         def feature_plane(z, carry):
             for half in range(band_rows // 8):
@@ -107,51 +116,74 @@
                     best_ref[z, pl.ds(y0, 8), :] = value
                 else:
                     best_ref[z, pl.ds(y0, 8), :] = jnp.maximum(prev_ref[z, pl.ds(y0, 8), :], value)
+            for copy in out_copy(z):
+                copy.start()
             return carry
 
         lax.fori_loop(0, slab_depth, feature_plane, 0)
+        for z in range(slab_depth):
+            for copy in out_copy(z):
+                copy.wait()
 
     def kernel(*refs):
         if first:
-            dil_ref, lo_hbm, mid_hbm, hi_hbm, feature_ref, best_ref, a_scr, s_scr, sems = refs
-            prev_ref = None
+            (dil_ref, lo_hbm, mid_hbm, hi_hbm, feature_hbm, best_hbm,
+             a_scr, s_scr, f_scr, b_scr, p_scr, row_sems, out_sems, prev_sem) = refs
         else:
-            (dil_ref, lo_hbm, mid_hbm, hi_hbm, prev_ref, feature_ref, best_ref,
-             a_scr, s_scr, sems) = refs
-        copies = [
-            pltpu.make_async_copy(lo_hbm, a_scr.at[pl.ds(0, HALO)], sems.at[0]),
-            pltpu.make_async_copy(mid_hbm, a_scr.at[pl.ds(HALO, slab_depth)], sems.at[1]),
-            pltpu.make_async_copy(hi_hbm, a_scr.at[pl.ds(HALO + slab_depth, HALO)], sems.at[2]),
-        ]
-        for copy in copies:
-            copy.start()
-        for copy in copies:
-            copy.wait()
-        dilation = dil_ref[level_index]
-        for value in range(1, DMAX + 1):
-
-            @pl.when(dilation == value)
-            def _():
-                compute(value, a_scr, s_scr, feature_ref, prev_ref, best_ref)
+            (dil_ref, lo_hbm, mid_hbm, hi_hbm, prev_hbm, feature_hbm, best_hbm,
+             a_scr, s_scr, f_scr, b_scr, p_scr, row_sems, out_sems, prev_sem) = refs
+        pieces = [(lo_hbm, HALO), (mid_hbm, slab_depth), (hi_hbm, HALO)]
+        row = 0
+        for source, count in pieces:
+            for index in range(count):
+                pltpu.make_async_copy(source.at[index], a_scr.at[row], row_sems.at[row]).start()
+                row += 1
+        prev_copy = None
+        if not first:
+            prev_copy = pltpu.make_async_copy(prev_hbm, p_scr, prev_sem.at[0])
+            prev_copy.start()
+
+        def row_wait(row):
+            pltpu.make_async_copy(mid_hbm.at[0], a_scr.at[row], row_sems.at[row]).wait()
+
+        def out_copy(z):
+            return [
+                pltpu.make_async_copy(f_scr.at[z], feature_hbm.at[z], out_sems.at[0, z]),
+                pltpu.make_async_copy(b_scr.at[z], best_hbm.at[z], out_sems.at[1, z]),
+            ]
+
+        def branch(value):
+            def run_branch():
+                compute(value, a_scr, s_scr, f_scr, None if first else p_scr, b_scr,
+                        row_wait, prev_copy, out_copy)
+            return run_branch
+
+        pick = jnp.clip(dil_ref[level_index], 1, DMAX) - 1
+        lax.switch(pick, [branch(value) for value in range(1, DMAX + 1)])
 
     def run(dilations, low, middle, high, prev):
         block = jax.ShapeDtypeStruct((slab_depth, band_rows, row_length), jnp.float32)
         anywhere = pl.BlockSpec(memory_space=pl.ANY)
-        in_vmem = pl.BlockSpec(memory_space=pltpu.VMEM)
         in_specs = [pl.BlockSpec(memory_space=pltpu.SMEM), anywhere, anywhere, anywhere]
         operands = [dilations, low, middle, high]
         if not first:
-            in_specs.append(in_vmem)
+            in_specs.append(anywhere)
             operands.append(prev)
+        total_rows = planes + 2 * HALO - 2
         return pl.pallas_call(
             kernel,
             out_shape=(block, block),
             in_specs=in_specs,
-            out_specs=(in_vmem, in_vmem),
+            out_specs=(anywhere, anywhere),
             scratch_shapes=[
-                pltpu.VMEM((planes + 2 * HALO - 2, band_rows + 2, row_length), jnp.float32),
+                pltpu.VMEM((total_rows, band_rows + 2, row_length), jnp.float32),
                 pltpu.VMEM((planes, band_rows + 2, row_length), jnp.float32),
-                pltpu.SemaphoreType.DMA((3,)),
+                pltpu.VMEM((slab_depth, band_rows, row_length), jnp.float32),
+                pltpu.VMEM((slab_depth, band_rows, row_length), jnp.float32),
+                pltpu.VMEM((slab_depth, band_rows, row_length), jnp.float32),
+                pltpu.SemaphoreType.DMA((total_rows,)),
+                pltpu.SemaphoreType.DMA((2, slab_depth)),
+                pltpu.SemaphoreType.DMA((1,)),
             ],
             compiler_params=pltpu.CompilerParams(vmem_limit_bytes=56 * 1024 * 1024),
         )(*operands)

time: 167 us -> 165 us (0.988)
  Pallas kernels: 39.2 us -> 34 us
  waiting for transfers between devices: 61.4 us -> 64.4 us
    pallas_call x3, Pallas kernels: 39.2 us -> 34 us  [run(): pl.pallas_call(kernel, out_shape=(block, block), in_specs=in_specs, out_s...]
  transfers between devices with their start and end apart: 8 -> 8, of which waited for: 6 -> 6; matrix products, arithmetic and copies ran while one was open for 4% -> 4% of each run, Pallas kernels for 15% -> 14%
where the time goes in v7:
time: 165 us
  waiting for transfers between devices  64.4 us (39%)
  Pallas kernels  34 us (21%)
  starting transfers between devices  16.9 us (10%)
  blocking collectives  14.8 us (9%)
  between operations  10.7 us (6%)
  local copies, waits for them, and re-layouts  10.4 us (6%)
  matrix products  7.46 us (5%)
  other arithmetic  6.04 us (4%)
    ppermute x1, waiting for transfers between devices, with_halo(): lax.ppermute(lax.slice_in_dim(block, 0, width, axis=dim), axis, backward)  40 us
    pallas_call x3, Pallas kernels, run(): pl.pallas_call(kernel, out_shape=(block, block), in_specs=in_specs, out_s...  34 us
    all_to_all x1, blocking collectives, per_device(): lax.all_to_all(spread.reshape(SCALES, groups, HOWN), 'gy', split_axis=1,...  14.8 us
    ppermute x3, waiting for transfers between devices, z_neighbours(): lax.ppermute(lax.slice_in_dim(block, 0, width, axis=0), 'gz', backward)  13.7 us
    ppermute x3, starting transfers between devices, z_neighbours(): lax.ppermute(lax.slice_in_dim(block, 0, width, axis=0), 'gz', backward)  13.2 us
    ppermute x3, waiting for transfers between devices, z_neighbours(): lax.ppermute(lax.slice_in_dim(block, block.shape[0] - width, None, axis=0...  10.7 us
    dot_general x3, matrix products, per_device(): jnp.dot(feature, pick_x, precision=lax.Precision.HIGHEST, preferred_eleme...  6.64 us
    add x1, other arithmetic, smooth_padded(): running = summand if running is None else running + summand  4.9 us
  transfers between devices with their start and end apart: 8, of which 6 were waited for; matrix products, arithmetic and copies ran while one was open for 4% of the time, Pallas kernels for 14%

profile of v7, /device:TPU:2, one launch (start us, length us, event | category | flops | bytes accessed | tf_op | source)
XLA Modules:
  0.0 164.6 jit_solution(16791618244319301686)
XLA Ops:
  0.6 2.0 %fusion.24 = (f32[10,9,2048]{2,1,0:T(8,128)S(1)}, f32[10,9,2048]{2,1,0:T(8,128)S(1)}) fusion(f32[10,16,2048]{2,1,0:T(8,128)} %param.6), kind=kLoop, calls=%fused_computation.66 | loop fusion | bytes 2949120 | tf_op jit(solution)/shard_map/slice | solution.py:25
  2.7 0.0 copy-start.6
  2.7 0.0 copy-start.10
  2.7 0.0 copy-start.8
  2.7 0.0 copy-start.9
  2.7 0.4 copy.14
  3.2 3.2 %collective-permute-start.1 = (f32[10,9,2048]{2,0,1:T(8,128)S(1)}, f32[10,9,2048]{2,0,1:T(8,128)S(1)}, u32[]{:S(2)}, u32[]{:S(2)}) collective-permute-start(f32[10,9,2048]{2,0,1:T(8,128)S(1)} %copy.14), channel_id=1, source_target_pairs={{1,0},{2,1},{3,2},{4,3},{5,4},{6,5},{7,6},{0,7},{9,8},{10,9},{11,1... | collective-permute-start | bytes 2211848 | tf_op jit(solution)/shard_map/ppermute | solution.py:27
  6.4 0.4 copy.13
  6.9 0.4 collective-permute-start
  7.3 0.6 fusion.26
  17.6 0.0 copy-done.8
  17.7 0.0 copy-start.3
  17.7 40.0 %collective-permute-done.1 = f32[10,9,2048]{2,0,1:T(8,128)S(1)} collective-permute-done((f32[10,9,2048]{2,0,1:T(8,128)S(1)}, f32[10,9,2048]{2,0,1:T(8,128)S(1)}, u32[]{:S(2)}, u32[]{:S(2)}) %collective-permute-start.1) | collective-permute-done | bytes 737312 | tf_op jit(solution)/shard_map/ppermute | solution.py:27
  57.7 0.5 copy.11
  58.2 0.0 collective-permute-done
  58.2 1.7 %copy.10 = f32[10,9,2048]{2,1,0:T(8,128)S(1)} copy(f32[10,9,2048]{2,0,1:T(8,128)} %collective-permute-done) | data formatting | bytes 1474560 | tf_op jit(solution)/shard_map/ppermute | solution.py:24
  60.0 0.4 pad_maximum_fusion
  60.4 4.9 %multiply_add_fusion = (f32[10,18,2048]{2,1,0:T(8,128)S(1)}, f32[10,18,2048]{2,1,0:T(8,128)S(1)}, f32[10,18,2048]{2,1,0:T(8,128)S(1)}) fusion(f32[10,34,2048]{2,1,0:T(8,128)S(1)} %pad_maximum_fusion, s32[]{:T(128)S(6)} %select_n.83, s32[]{:T(128)S(6)} %select_n.82, s32[]{:T(128)S(6)} %select_n.81, s32[]{:T(128)S(6)} %select_n.80, s32[]{:T(128)S(6)} %select_n.79, ...), kind=kLoop, calls=%fused_computation.11 | loop fusion | flops 9216000 | bytes 23593008 | tf_op jit(solution)/shard_map/add | solution.py:39
  65.3 0.0 copy-start
  65.3 0.0 copy-start.2
  65.3 0.0 copy-start.1
  65.3 0.4 fusion.21
  65.8 0.8 copy-done
  66.6 5.4 %collective-permute-start.7 = (f32[9,18,2048]{2,1,0:T(8,128)S(1)}, f32[9,18,2048]{2,1,0:T(8,128)S(1)}, u32[]{:S(2)}, u32[]{:S(2)}) collective-permute-start(f32[9,18,2048]{2,1,0:T(8,128)S(1)} %get-tuple-element.25), channel_id=1, source_target_pairs={{8,0},{16,8},{24,16},{32,24},{40,32},{48,40},{56,48},{64,56},{72,6... | collective-permute-start | bytes 3981320 | tf_op jit(solution)/shard_map/ppermute | solution.py:200
  72.0 0.0 collective-permute-start.6
  72.0 0.4 fusion.22
  72.5 3.9 %collective-permute-start.5 = (f32[9,18,2048]{2,1,0:T(8,128)S(1)}, f32[9,18,2048]{2,1,0:T(8,128)}, u32[]{:S(2)}, u32[]{:S(2)}) collective-permute-start(f32[9,18,2048]{2,1,0:T(8,128)S(1)} %get-tuple-element.27), channel_id=1, source_target_pairs={{8,0},{16,8},{24,16},{32,24},{40,32},{48,40},{56,48},{64,56},{72,6... | collective-permute-start | bytes 3981320 | tf_op jit(solution)/shard_map/ppermute | solution.py:200
  76.4 0.0 collective-permute-start.4
  76.4 0.0 copy-start.7
  76.5 1.8 %fusion.23 = (f32[9,18,2048]{2,1,0:T(8,128)}, f32[9,18,2048]{2,1,0:T(8,128)S(1)}) fusion(f32[10,18,2048]{2,1,0:T(8,128)S(1)} %get-tuple-element.24.refs_2_), kind=kLoop, calls=%fused_computation.65 | loop fusion | bytes 5308416 | tf_op jit(solution)/shard_map/slice | solution.py:200
  78.2 3.8 %collective-permute-start.3 = (f32[9,18,2048]{2,1,0:T(8,128)}, f32[9,18,2048]{2,1,0:T(8,128)S(1)}, u32[]{:S(2)}, u32[]{:S(2)}) collective-permute-start(f32[9,18,2048]{2,1,0:T(8,128)} %get-tuple-element.29), channel_id=1, source_target_pairs={{8,0},{16,8},{24,16},{32,24},{40,32},{48,40},{56,48},{64,56},{72,6... | collective-permute-start | bytes 3981320 | tf_op jit(solution)/shard_map/ppermute | solution.py:200
  82.1 10.0 %collective-permute-done.7.refs_3_ = f32[9,18,2048]{2,1,0:T(8,128)S(1)} collective-permute-done((f32[9,18,2048]{2,1,0:T(8,128)S(1)}, f32[9,18,2048]{2,1,0:T(8,128)S(1)}, u32[]{:S(2)}, u32[]{:S(2)}) %collective-permute-start.7) | collective-permute-done | bytes 1327136 | tf_op jit(solution)/shard_map/ppermute | solution.py:200
  92.1 0.0 collective-permute-start.2
  92.1 1.2 copy-done.5
  93.3 2.9 %collective-permute-done.6.refs_1_ = f32[9,18,2048]{2,1,0:T(8,128)} collective-permute-done((f32[9,18,2048]{2,1,0:T(8,128)S(1)}, f32[9,18,2048]{2,1,0:T(8,128)}, u32[]{:S(2)}, u32[]{:S(2)}) %collective-permute-start.6) | collective-permute-done | bytes 1327136 | tf_op jit(solution)/shard_map/ppermute | solution.py:199
  96.2 11.1 %shard_map.77 = (f32[10,16,2048]{2,1,0:T(8,128)}, f32[10,16,2048]{2,1,0:T(8,128)}) custom-call(s32[3]{0:T(128)} %refs_0_.5, f32[9,18,2048]{2,1,0:T(8,128)} %collective-permute-done.6.refs_1_, f32[10,18,2048]{2,1,0:T(8,128)} %copy-done, f32[9,18,2048]{2,1,0:T(8,128)} %copy-done.5), custom_call_target="tpu_custom_call" | custom-call | tf_op jit(solution)/shard_map/pallas_call | solution.py:173
  107.3 3.7 %collective-permute-done.5.refs_3_ = f32[9,18,2048]{2,1,0:T(8,128)} collective-permute-done((f32[9,18,2048]{2,1,0:T(8,128)S(1)}, f32[9,18,2048]{2,1,0:T(8,128)}, u32[]{:S(2)}, u32[]{:S(2)}) %collective-permute-start.5) | collective-permute-done | bytes 1327136 | tf_op jit(solution)/shard_map/ppermute | solution.py:200
  111.0 4.1 %collective-permute-done.4.refs_1_ = f32[9,18,2048]{2,1,0:T(8,128)} collective-permute-done((f32[9,18,2048]{2,1,0:T(8,128)S(1)}, f32[9,18,2048]{2,1,0:T(8,128)}, u32[]{:S(2)}, u32[]{:S(2)}) %collective-permute-start.4) | collective-permute-done | bytes 1327136 | tf_op jit(solution)/shard_map/ppermute | solution.py:199
  115.1 11.7 %shard_map.78 = (f32[10,16,2048]{2,1,0:T(8,128)}, f32[10,16,2048]{2,1,0:T(8,128)}) custom-call(s32[3]{0:T(128)} %refs_0_.5, f32[9,18,2048]{2,1,0:T(8,128)} %collective-permute-done.4.refs_1_, f32[10,18,2048]{2,1,0:T(8,128)} %copy-done.2, f32[9,18,2048]{2,1,0:T(8,128)} %collective-permute-done.5.refs_3_, f32[10,16,2048]{2,1,0:T(8,128)} %get-tuple-element.8.refs_4_), custom_call_target="tpu_custom_call" | custom-call | tf_op jit(solution)/shard_map/pallas_call | solution.py:173
  126.8 1.8 %fusion.12 = f32[512]{0:T(512)S(1)} fusion(f32[160,2048]{1,0:T(8,128)S(1)} %bitcast.56, s32[512]{0:T(512)S(1)} %get-tuple-element.46, f32[512]{0:T(512)S(1)} %get-tuple-element.53, s32[512]{0:T(512)S(1)} %pad_add_fusion.4, f32[512]{0:T(512)S(1)} %get-tuple-element.52, s32[512]{0:T(512)S(1)} %get-tuple-element.49, f32[512]{0:T(512)S(1)} %get-tuple-element.51, ...), kind=kOutput, calls=%fused_computation.19 | convolution fusion | flops 2015378944 | bytes 1331200 | tf_op jit(solution)/shard_map/dot_general | solution.py:289
  128.6 1.8 %fusion.11 = f32[512]{0:T(512)S(1)} fusion(f32[160,2048]{1,0:T(8,128)S(1)} %bitcast.57, s32[512]{0:T(512)S(1)} %get-tuple-element.46, f32[512]{0:T(512)S(1)} %get-tuple-element.53, s32[512]{0:T(512)S(1)} %pad_add_fusion.4, f32[512]{0:T(512)S(1)} %get-tuple-element.52, s32[512]{0:T(512)S(1)} %get-tuple-element.49, f32[512]{0:T(512)S(1)} %get-tuple-element.51, ...), kind=kOutput, calls=%fused_computation.18 | convolution fusion | flops 2015378944 | bytes 1331200 | tf_op jit(solution)/shard_map/dot_general | solution.py:289
  130.4 0.0 collective-permute-done.3.refs_3_
  130.4 3.7 %collective-permute-done.2.refs_1_ = f32[9,18,2048]{2,1,0:T(8,128)} collective-permute-done((f32[9,18,2048]{2,1,0:T(8,128)S(1)}, f32[9,18,2048]{2,1,0:T(8,128)}, u32[]{:S(2)}, u32[]{:S(2)}) %collective-permute-start.2) | collective-permute-done | bytes 1327136 | tf_op jit(solution)/shard_map/ppermute | solution.py:199
  134.1 11.2 %shard_map.79 = (f32[10,16,2048]{2,1,0:T(8,128)}, f32[10,16,2048]{2,1,0:T(8,128)}) custom-call(s32[3]{0:T(128)} %refs_0_.5, f32[9,18,2048]{2,1,0:T(8,128)} %collective-permute-done.2.refs_1_, f32[10,18,2048]{2,1,0:T(8,128)} %copy-done.1, f32[9,18,2048]{2,1,0:T(8,128)} %copy-done.4, f32[10,16,2048]{2,1,0:T(8,128)} %get-tuple-element.9.refs_4_), custom_call_target="tpu_custom_call" | custom-call | tf_op jit(solution)/shard_map/pallas_call | solution.py:173
  145.3 3.1 %fusion.10 = f32[512]{0:T(512)S(1)} fusion(f32[160,2048]{1,0:T(8,128)} %bitcast.58, s32[512]{0:T(512)S(1)} %get-tuple-element.46, f32[512]{0:T(512)S(1)} %get-tuple-element.53, s32[512]{0:T(512)S(1)} %pad_add_fusion.4, f32[512]{0:T(512)S(1)} %get-tuple-element.52, s32[512]{0:T(512)S(1)} %get-tuple-element.49, f32[512]{0:T(512)S(1)} %get-tuple-element.51, ...), kind=kOutput, calls=%fused_computation.17 | convolution fusion | flops 2015378944 | bytes 1331200 | tf_op jit(solution)/shard_map/dot_general | solution.py:289
  148.4 0.8 fusion.6
  149.2 14.8 %all_to_all.5 = f32[3,8,256]{2,0,1:T(4,128)S(1)} all-to-all(f32[3,8,256]{2,0,1:T(4,128)S(1)} %bitcast.43), channel_id=1, replica_groups=mesh['gz'=32,'gy'=8] {'gy'}, dimensions={1} | all-to-all | bytes 49152 | tf_op jit(solution)/shard_map/all_to_all | solution.py:304
  164.0 0.6 reduce_sum.39
  (27 shorter events, 0.1 us)
Async XLA Ops:
  2.7 4.6 %copy-start.6 = (s32[3]{0:T(128)S(1)}, s32[3]{0:T(128)}, u32[]{:S(2)}) copy-start(s32[3]{0:T(128)} %refs_0_.5) | copy-start | bytes 40
  2.7 14.9 %copy-start.10 = (s32[256,1]{0,1:T(1,128)S(1)}, s32[256,1]{0,1:T(1,128)}, u32[]{:S(2)}) copy-start(s32[256,1]{0,1:T(1,128)} %param.8) | copy-start | bytes 3076
  2.7 14.9 %copy-start.8 = (s32[256]{0:T(256)S(1)}, s32[256]{0:T(256)}, u32[]{:S(2)}) copy-start(s32[256]{0:T(256)} %param.9) | copy-start | bytes 3076
  2.7 15.0 %copy-start.9 = (s32[256]{0:T(256)S(1)}, s32[256]{0:T(256)}, u32[]{:S(2)}) copy-start(s32[256]{0:T(256)} %param.10) | copy-start | bytes 3076
  3.2 54.6 %collective-permute-start.1 = (f32[10,9,2048]{2,0,1:T(8,128)S(1)}, f32[10,9,2048]{2,0,1:T(8,128)S(1)}, u32[]{:S(2)}, u32[]{:S(2)}) collective-permute-start(f32[10,9,2048]{2,0,1:T(8,128)S(1)} %copy.14), channel_id=1, source_target_pairs={{1,0},{2,1},{3,2},{4,3},{5,4},{6,5},{7,6},{0,7},{9,8},{10,9},{11,1... | collective-permute-start | bytes 2211848 | tf_op jit(solution)/shard_map/ppermute | solution.py:27
  6.9 51.3 %collective-permute-start = (f32[10,9,2048]{2,0,1:T(8,128)S(1)}, f32[10,9,2048]{2,0,1:T(8,128)}, u32[]{:S(2)}, u32[]{:S(2)}) collective-permute-start(f32[10,9,2048]{2,0,1:T(8,128)S(1)} %copy.13), channel_id=1, source_target_pairs={{0,1},{1,2},{2,3},{3,4},{4,5},{5,6},{6,7},{7,0},{8,9},{9,10},{10,1... | collective-permute-start | bytes 2211848 | tf_op jit(solution)/shard_map/ppermute | solution.py:24
  17.7 42.2 %copy-start.3 = (f32[10,16,2048]{2,1,0:T(8,128)S(1)}, f32[10,16,2048]{2,1,0:T(8,128)}, u32[]{:S(2)}) copy-start(f32[10,16,2048]{2,1,0:T(8,128)} %param.6) | copy-start | bytes 3932164
  65.3 1.3 copy-start
  65.3 6.7 %copy-start.2 = (f32[10,18,2048]{2,1,0:T(8,128)}, f32[10,18,2048]{2,1,0:T(8,128)S(1)}, u32[]{:S(2)}) copy-start(f32[10,18,2048]{2,1,0:T(8,128)S(1)} %get-tuple-element.23.refs_2_) | copy-start | bytes 4423684
  65.3 11.1 %copy-start.1 = (f32[10,18,2048]{2,1,0:T(8,128)}, f32[10,18,2048]{2,1,0:T(8,128)S(1)}, u32[]{:S(2)}) copy-start(f32[10,18,2048]{2,1,0:T(8,128)S(1)} %get-tuple-element.24.refs_2_) | copy-start | bytes 4423684
  66.6 25.5 %collective-permute-start.7 = (f32[9,18,2048]{2,1,0:T(8,128)S(1)}, f32[9,18,2048]{2,1,0:T(8,128)S(1)}, u32[]{:S(2)}, u32[]{:S(2)}) collective-permute-start(f32[9,18,2048]{2,1,0:T(8,128)S(1)} %get-tuple-element.25), channel_id=1, source_target_pairs={{8,0},{16,8},{24,16},{32,24},{40,32},{48,40},{56,48},{64,56},{72,6... | collective-permute-start | bytes 3981320 | tf_op jit(solution)/shard_map/ppermute | solution.py:200
  72.0 24.2 %collective-permute-start.6 = (f32[9,18,2048]{2,1,0:T(8,128)S(1)}, f32[9,18,2048]{2,1,0:T(8,128)}, u32[]{:S(2)}, u32[]{:S(2)}) collective-permute-start(f32[9,18,2048]{2,1,0:T(8,128)S(1)} %get-tuple-element.26), channel_id=1, source_target_pairs={{0,8},{8,16},{16,24},{24,32},{32,40},{40,48},{48,56},{56,64},{64,7... | collective-permute-start | bytes 3981320 | tf_op jit(solution)/shard_map/ppermute | solution.py:199
  72.5 38.6 %collective-permute-start.5 = (f32[9,18,2048]{2,1,0:T(8,128)S(1)}, f32[9,18,2048]{2,1,0:T(8,128)}, u32[]{:S(2)}, u32[]{:S(2)}) collective-permute-start(f32[9,18,2048]{2,1,0:T(8,128)S(1)} %get-tuple-element.27), channel_id=1, source_target_pairs={{8,0},{16,8},{24,16},{32,24},{40,32},{48,40},{56,48},{64,56},{72,6... | collective-permute-start | bytes 3981320 | tf_op jit(solution)/shard_map/ppermute | solution.py:200
  76.4 38.8 %collective-permute-start.4 = (f32[9,18,2048]{2,1,0:T(8,128)S(1)}, f32[9,18,2048]{2,1,0:T(8,128)}, u32[]{:S(2)}, u32[]{:S(2)}) collective-permute-start(f32[9,18,2048]{2,1,0:T(8,128)S(1)} %get-tuple-element.28), channel_id=1, source_target_pairs={{0,8},{8,16},{16,24},{24,32},{32,40},{40,48},{48,56},{56,64},{64,7... | collective-permute-start | bytes 3981320 | tf_op jit(solution)/shard_map/ppermute | solution.py:199
  76.4 16.8 %copy-start.7 = (f32[8,256]{1,0:T(8,128)S(1)}, f32[8,256]{1,0:T(8,128)}, u32[]{:S(2)}) copy-start(f32[8,256]{1,0:T(8,128)} %param.11) | copy-start | bytes 24580
  78.2 52.2 %collective-permute-start.3 = (f32[9,18,2048]{2,1,0:T(8,128)}, f32[9,18,2048]{2,1,0:T(8,128)S(1)}, u32[]{:S(2)}, u32[]{:S(2)}) collective-permute-start(f32[9,18,2048]{2,1,0:T(8,128)} %get-tuple-element.29), channel_id=1, source_target_pairs={{8,0},{16,8},{24,16},{32,24},{40,32},{48,40},{56,48},{64,56},{72,6... | collective-permute-start | bytes 3981320 | tf_op jit(solution)/shard_map/ppermute | solution.py:200
  92.1 1.2 copy-start.5
  92.1 42.0 %collective-permute-start.2 = (f32[9,18,2048]{2,1,0:T(8,128)S(1)}, f32[9,18,2048]{2,1,0:T(8,128)}, u32[]{:S(2)}, u32[]{:S(2)}) collective-permute-start(f32[9,18,2048]{2,1,0:T(8,128)S(1)} %get-tuple-element.30), channel_id=1, source_target_pairs={{0,8},{8,16},{16,24},{24,32},{32,40},{40,48},{48,56},{56,64},{64,7... | collective-permute-start | bytes 3981320 | tf_op jit(solution)/shard_map/ppermute | solution.py:199
  115.1 11.7 %copy-start.11 = (f32[10,16,2048]{2,1,0:T(8,128)S(1)}, f32[10,16,2048]{2,1,0:T(8,128)}, u32[]{:S(2)}) copy-start(f32[10,16,2048]{2,1,0:T(8,128)} %get-tuple-element.11) | copy-start | bytes 3932164
  126.8 1.8 %copy-start.12 = (f32[10,16,2048]{2,1,0:T(8,128)S(1)}, f32[10,16,2048]{2,1,0:T(8,128)}, u32[]{:S(2)}) copy-start(f32[10,16,2048]{2,1,0:T(8,128)} %get-tuple-element.12) | copy-start | bytes 3932164
  130.4 3.7 %copy-start.4 = (f32[9,18,2048]{2,1,0:T(8,128)}, f32[9,18,2048]{2,1,0:T(8,128)S(1)}, u32[]{:S(2)}) copy-start(f32[9,18,2048]{2,1,0:T(8,128)S(1)} %collective-permute-done.3.refs_3_) | copy-start | bytes 3981316

commit v8 on v7

--- a/solution.py
+++ b/solution.py
@@ -15,16 +15,22 @@
 hessian_scale = 4.0
 
 
+def flat_ppermute(part, axis, pairs):
+    rows = part.shape[0] * part.shape[1]
+    moved = lax.ppermute(part.reshape(rows, part.shape[2]), axis, pairs)
+    return moved.reshape(part.shape)
+
+
 def with_halo(block, sides, width):
     for axis, dim in sides:
         count = lax.axis_size(axis)
         forward = [(i, i + 1) for i in range(count - 1)]
         forward.append((count - 1, 0))
         backward = [(target, source) for source, target in forward]
-        low = lax.ppermute(
+        low = flat_ppermute(
             lax.slice_in_dim(block, block.shape[dim] - width, None, axis=dim), axis, forward
         )
-        high = lax.ppermute(lax.slice_in_dim(block, 0, width, axis=dim), axis, backward)
+        high = flat_ppermute(lax.slice_in_dim(block, 0, width, axis=dim), axis, backward)
         block = jnp.concatenate([low, block, high], axis=dim)
     return block
 
@@ -196,8 +202,8 @@
     forward = [(i, i + 1) for i in range(count - 1)]
     forward.append((count - 1, 0))
     backward = [(target, source) for source, target in forward]
-    low = lax.ppermute(lax.slice_in_dim(block, block.shape[0] - width, None, axis=0), "gz", forward)
-    high = lax.ppermute(lax.slice_in_dim(block, 0, width, axis=0), "gz", backward)
+    low = flat_ppermute(lax.slice_in_dim(block, block.shape[0] - width, None, axis=0), "gz", forward)
+    high = flat_ppermute(lax.slice_in_dim(block, 0, width, axis=0), "gz", backward)
     return low, high
 
 

time: 165 us -> 152 us (0.921)
  waiting for transfers between devices: 64.4 us -> 23.7 us
  local copies, waits for them, and re-layouts: 10.4 us -> 38.4 us
  other arithmetic: 6.04 us -> 8.59 us
  blocking collectives: 14.8 us -> 12.5 us
    ppermute x8, waiting for transfers between devices: 64.4 us -> 23.7 us  [flat_ppermute(): moved = lax.ppermute(part.reshape(rows, part.shape[2]), axis, pairs)]
    reshape x0 -> x16, local copies, waits for them, and re-layouts: none -> 30.4 us  [the longest x8 18.3 us: flat_ppermute(): return moved.reshape(part.shape)]
    unnamed x28 -> x24, local copies, waits for them, and re-layouts: 2.99 us -> 0.16 us
    slice x3 -> x2, local copies, waits for them, and re-layouts: 2.59 us -> 5.26 us  [z_neighbours(): lax.slice_in_dim(block, 0, width, axis=0)]
    all_to_all x1, blocking collectives: 14.8 us -> 12.5 us  [per_device(): lax.all_to_all(spread.reshape(SCALES, groups, HOWN), 'gy', split_axis=1,...]
    ppermute x2 -> x0, local copies, waits for them, and re-layouts: 2.19 us -> none  [the longest x1 1.73 us: with_halo(): lax.ppermute(lax.slice_in_dim(block, block.shape[dim] - width, None, axis...]
  transfers between devices with their start and end apart: 8 -> 8, of which waited for: 6 -> 3; matrix products, arithmetic and copies ran while one was open for 4% -> 18% of each run, Pallas kernels for 14% -> 15%
where the time goes in v8:
time: 152 us
  local copies, waits for them, and re-layouts  38.4 us (25%)
  Pallas kernels  34.1 us (22%)
  waiting for transfers between devices  23.7 us (16%)
  starting transfers between devices  16.8 us (11%)
  blocking collectives  12.5 us (8%)
  between operations  10.3 us (7%)
  other arithmetic  8.59 us (6%)
  matrix products  7.56 us (5%)
    pallas_call x3, Pallas kernels, run(): pl.pallas_call(kernel, out_shape=(block, block), in_specs=in_specs, out_s...  34.1 us
    ppermute x8, waiting for transfers between devices, flat_ppermute(): moved = lax.ppermute(part.reshape(rows, part.shape[2]), axis, pairs)  23.7 us
    reshape x8, local copies, waits for them, and re-layouts, flat_ppermute(): return moved.reshape(part.shape)  18.3 us
    ppermute x8, starting transfers between devices, flat_ppermute(): moved = lax.ppermute(part.reshape(rows, part.shape[2]), axis, pairs)  16.8 us
    all_to_all x1, blocking collectives, per_device(): lax.all_to_all(spread.reshape(SCALES, groups, HOWN), 'gy', split_axis=1,...  12.5 us
    reshape x8, local copies, waits for them, and re-layouts, flat_ppermute(): moved = lax.ppermute(part.reshape(rows, part.shape[2]), axis, pairs)  12.1 us
    dot_general x3, matrix products, per_device(): jnp.dot(feature, pick_x, precision=lax.Precision.HIGHEST, preferred_eleme...  6.74 us
    add x1, other arithmetic, smooth_padded(): running = summand if running is None else running + summand  6.05 us
  transfers between devices with their start and end apart: 8, of which 3 were waited for; matrix products, arithmetic and copies ran while one was open for 18% of the time, Pallas kernels for 15%

profile of v8, /device:TPU:2, one launch (start us, length us, event | category | flops | bytes accessed | tf_op | source)
XLA Modules:
  0.0 152.0 jit_solution(16884187144406355870)
XLA Ops:
  0.6 2.0 %fusion.24 = (f32[10,9,2048]{2,1,0:T(8,128)S(1)}, f32[10,9,2048]{2,1,0:T(8,128)S(1)}) fusion(f32[10,16,2048]{2,1,0:T(8,128)} %param.6), kind=kLoop, calls=%fused_computation.66 | loop fusion | bytes 2949120 | tf_op jit(solution)/shard_map/slice | solution.py:31
  2.6 0.0 copy-start.5
  2.6 0.1 reshape.142
  2.8 3.3 %collective-permute-start = (f32[90,2048]{1,0:T(8,128)S(1)}, f32[90,2048]{1,0:T(8,128)}, u32[]{:S(2)}, u32[]{:S(2)}) collective-permute-start(f32[90,2048]{1,0:T(8,128)S(1)} %reshape.142), channel_id=1, source_target_pairs={{0,1},{1,2},{2,3},{3,4},{4,5},{5,6},{6,7},{7,0},{8,9},{9,10},{10,1... | collective-permute-start | bytes 2211848 | tf_op jit(solution)/shard_map/ppermute | solution.py:20
  6.0 1.0 reshape.144
  7.0 1.2 collective-permute-start.1
  8.2 0.6 fusion.26
  18.3 0.0 copy-start.3
  18.3 21.3 %collective-permute-done = f32[90,2048]{1,0:T(8,128)} collective-permute-done((f32[90,2048]{1,0:T(8,128)S(1)}, f32[90,2048]{1,0:T(8,128)}, u32[]{:S(2)}, u32[]{:S(2)}) %collective-permute-start) | collective-permute-done | bytes 737312 | tf_op jit(solution)/shard_map/ppermute | solution.py:20
  39.7 1.2 reshape.143
  40.9 0.6 collective-permute-done.1
  41.5 2.3 %reshape.145 = f32[10,9,2048]{2,1,0:T(8,128)} reshape(f32[90,2048]{1,0:T(8,128)} %collective-permute-done.1) | data formatting | bytes 1474560 | tf_op jit(solution)/shard_map/reshape | solution.py:21
  43.8 1.8 %pad_maximum_fusion = f32[10,34,2048]{2,1,0:T(8,128)S(1)} fusion(f32[10,9,2048]{2,1,0:T(8,128)} %reshape.145, f32[10,16,2048]{2,1,0:T(8,128)S(1)} %copy-done.3, f32[10,9,2048]{2,1,0:T(8,128)S(1)} %reshape.143), kind=kLoop, calls=%fused_computation.4 | loop fusion | flops 1392640 | bytes 5570560 | tf_op jit(solution)/shard_map/concatenate | solution.py:34
  45.6 6.0 %multiply_add_fusion = (f32[10,18,2048]{2,1,0:T(8,128)S(1)}, f32[10,18,2048]{2,1,0:T(8,128)S(1)}, f32[10,18,2048]{2,1,0:T(8,128)}) fusion(f32[10,34,2048]{2,1,0:T(8,128)S(1)} %pad_maximum_fusion, s32[]{:T(128)S(6)} %select_n.83, s32[]{:T(128)S(6)} %select_n.82, s32[]{:T(128)S(6)} %select_n.81, s32[]{:T(128)S(6)} %select_n.80, s32[]{:T(128)S(6)} %select_n.79, ...), kind=kLoop, calls=%fused_computation.11 | loop fusion | flops 9216000 | bytes 23593008 | tf_op jit(solution)/shard_map/add | solution.py:45
  51.7 3.1 %fusion.21 = (f32[9,18,2048]{2,1,0:T(8,128)S(1)}, f32[9,18,2048]{2,1,0:T(8,128)}, f32[9,18,2048]{2,1,0:T(8,128)S(1)}, f32[9,18,2048]{2,1,0:T(8,128)}) fusion(f32[10,18,2048]{2,1,0:T(8,128)S(1)} %get-tuple-element.22.refs_2_, f32[10,18,2048]{2,1,0:T(8,128)S(1)} %get-tuple-element.23.refs_2_), kind=kLoop, calls=%fused_computation.63 | loop fusion | bytes 10616832 | tf_op jit(solution)/shard_map/slice | solution.py:206
  54.7 2.7 %reshape.154 = f32[162,2048]{1,0:T(8,128)} reshape(f32[9,18,2048]{2,1,0:T(8,128)} %get-tuple-element.26) | data formatting | bytes 2654208 | tf_op jit(solution)/shard_map/reshape | solution.py:20
  57.4 0.0 collective-permute-start.6
  57.4 1.2 reshape.156
  58.7 6.5 %collective-permute-start.7 = (f32[162,2048]{1,0:T(8,128)}, f32[162,2048]{1,0:T(8,128)}, u32[]{:S(2)}, u32[]{:S(2)}) collective-permute-start(f32[162,2048]{1,0:T(8,128)} %reshape.156), channel_id=1, source_target_pairs={{8,0},{16,8},{24,16},{32,24},{40,32},{48,40},{56,48},{64,56},{72,6... | collective-permute-start | bytes 3981320 | tf_op jit(solution)/shard_map/ppermute | solution.py:20
  65.2 1.3 reshape.150
  66.4 2.8 %reshape.152 = f32[162,2048]{1,0:T(8,128)} reshape(f32[9,18,2048]{2,1,0:T(8,128)} %get-tuple-element.51) | data formatting | bytes 2654208 | tf_op jit(solution)/shard_map/reshape | solution.py:20
  69.3 3.7 %collective-permute-start.5 = (f32[162,2048]{1,0:T(8,128)}, f32[162,2048]{1,0:T(8,128)}, u32[]{:S(2)}, u32[]{:S(2)}) collective-permute-start(f32[162,2048]{1,0:T(8,128)} %reshape.152), channel_id=1, source_target_pairs={{8,0},{16,8},{24,16},{32,24},{40,32},{48,40},{56,48},{64,56},{72,6... | collective-permute-start | bytes 3981320 | tf_op jit(solution)/shard_map/ppermute | solution.py:20
  73.0 2.2 %fusion.23 = (f32[9,18,2048]{2,1,0:T(8,128)}, f32[9,18,2048]{2,1,0:T(8,128)}) fusion(f32[10,18,2048]{2,1,0:T(8,128)S(1)} %copy-done.2), kind=kLoop, calls=%fused_computation.65 | loop fusion | bytes 5308416 | tf_op jit(solution)/shard_map/slice | solution.py:206
  75.2 1.8 %reshape.146 = f32[162,2048]{1,0:T(8,128)S(1)} reshape(f32[9,18,2048]{2,1,0:T(8,128)} %get-tuple-element.30) | data formatting | bytes 2654208 | tf_op jit(solution)/shard_map/reshape | solution.py:20
  76.9 0.0 copy-start.9
  76.9 0.0 copy-start.7
  76.9 0.0 copy-start.8
  77.0 0.0 copy-start.6
  77.0 0.1 collective-permute-start.2
  77.1 0.1 copy-done.4
  77.2 1.3 reshape.148
  78.4 1.8 %collective-permute-done.6 = f32[162,2048]{1,0:T(8,128)} collective-permute-done((f32[162,2048]{1,0:T(8,128)}, f32[162,2048]{1,0:T(8,128)}, u32[]{:S(2)}, u32[]{:S(2)}) %collective-permute-start.6) | collective-permute-done | bytes 1327136 | tf_op jit(solution)/shard_map/ppermute | solution.py:20
  80.2 2.0 %collective-permute-start.3 = (f32[162,2048]{1,0:T(8,128)}, f32[162,2048]{1,0:T(8,128)S(1)}, u32[]{:S(2)}, u32[]{:S(2)}) collective-permute-start(f32[162,2048]{1,0:T(8,128)} %reshape.148), channel_id=1, source_target_pairs={{8,0},{16,8},{24,16},{32,24},{40,32},{48,40},{56,48},{64,56},{72,6... | collective-permute-start | bytes 3981320 | tf_op jit(solution)/shard_map/ppermute | solution.py:20
  82.4 2.6 %reshape.155.refs_1_ = f32[9,18,2048]{2,1,0:T(8,128)} reshape(f32[162,2048]{1,0:T(8,128)} %collective-permute-done.6) | data formatting | bytes 2654208 | tf_op jit(solution)/shard_map/reshape | solution.py:21
  85.0 2.7 %reshape.157.refs_3_ = f32[9,18,2048]{2,1,0:T(8,128)} reshape(f32[162,2048]{1,0:T(8,128)} %collective-permute-done.7) | data formatting | bytes 2654208 | tf_op jit(solution)/shard_map/reshape | solution.py:21
  87.7 11.5 %shard_map.77 = (f32[10,16,2048]{2,1,0:T(8,128)}, f32[10,16,2048]{2,1,0:T(8,128)}) custom-call(s32[3]{0:T(128)} %refs_0_.5, f32[9,18,2048]{2,1,0:T(8,128)} %reshape.155.refs_1_, f32[10,18,2048]{2,1,0:T(8,128)} %copy-done.1, f32[9,18,2048]{2,1,0:T(8,128)} %reshape.157.refs_3_), custom_call_target="tpu_custom_call" | custom-call | tf_op jit(solution)/shard_map/pallas_call | solution.py:179
  99.2 2.7 %reshape.151.refs_1_ = f32[9,18,2048]{2,1,0:T(8,128)} reshape(f32[162,2048]{1,0:T(8,128)} %collective-permute-done.4) | data formatting | bytes 2654208 | tf_op jit(solution)/shard_map/reshape | solution.py:21
  101.9 2.6 %reshape.153.refs_3_ = f32[9,18,2048]{2,1,0:T(8,128)} reshape(f32[162,2048]{1,0:T(8,128)} %collective-permute-done.5) | data formatting | bytes 2654208 | tf_op jit(solution)/shard_map/reshape | solution.py:21
  104.5 11.2 %shard_map.78 = (f32[10,16,2048]{2,1,0:T(8,128)}, f32[10,16,2048]{2,1,0:T(8,128)}) custom-call(s32[3]{0:T(128)} %refs_0_.5, f32[9,18,2048]{2,1,0:T(8,128)} %reshape.151.refs_1_, f32[10,18,2048]{2,1,0:T(8,128)} %copy-done, f32[9,18,2048]{2,1,0:T(8,128)} %reshape.153.refs_3_, f32[10,16,2048]{2,1,0:T(8,128)} %get-tuple-element.8.refs_4_), custom_call_target="tpu_custom_call" | custom-call | tf_op jit(solution)/shard_map/pallas_call | solution.py:179
  115.7 2.6 %reshape.147.refs_1_ = f32[9,18,2048]{2,1,0:T(8,128)} reshape(f32[162,2048]{1,0:T(8,128)} %collective-permute-done.2) | data formatting | bytes 2654208 | tf_op jit(solution)/shard_map/reshape | solution.py:21
  118.4 1.4 reshape.149.refs_3_
  119.8 11.4 %shard_map.79 = (f32[10,16,2048]{2,1,0:T(8,128)}, f32[10,16,2048]{2,1,0:T(8,128)}) custom-call(s32[3]{0:T(128)} %refs_0_.5, f32[9,18,2048]{2,1,0:T(8,128)} %reshape.147.refs_1_, f32[10,18,2048]{2,1,0:T(8,128)} %get-tuple-element.24.refs_2_, f32[9,18,2048]{2,1,0:T(8,128)} %reshape.149.refs_3_, f32[10,16,2048]{2,1,0:T(8,128)} %get-tuple-element.9.refs_4_), custom_call_target="tpu_custom_call" | custom-call | tf_op jit(solution)/shard_map/pallas_call | solution.py:179
  131.2 3.2 %fusion.10 = f32[512]{0:T(512)S(1)} fusion(f32[160,2048]{1,0:T(8,128)} %bitcast.58, s32[512]{0:T(512)S(1)} %get-tuple-element.46, f32[512]{0:T(512)S(1)} %get-tuple-element.55, s32[512]{0:T(512)S(1)} %pad_add_fusion.4, f32[512]{0:T(512)S(1)} %get-tuple-element.54, s32[512]{0:T(512)S(1)} %get-tuple-element.49, f32[512]{0:T(512)S(1)} %get-tuple-element.53, ...), kind=kOutput, calls=%fused_computation.17 | convolution fusion | flops 2015378944 | bytes 1331200 | tf_op jit(solution)/shard_map/dot_general | solution.py:295
  134.4 1.8 %fusion.11 = f32[512]{0:T(512)S(1)} fusion(f32[160,2048]{1,0:T(8,128)S(1)} %bitcast.57, s32[512]{0:T(512)S(1)} %get-tuple-element.46, f32[512]{0:T(512)S(1)} %get-tuple-element.55, s32[512]{0:T(512)S(1)} %pad_add_fusion.4, f32[512]{0:T(512)S(1)} %get-tuple-element.54, s32[512]{0:T(512)S(1)} %get-tuple-element.49, f32[512]{0:T(512)S(1)} %get-tuple-element.53, ...), kind=kOutput, calls=%fused_computation.18 | convolution fusion | flops 2015378944 | bytes 1331200 | tf_op jit(solution)/shard_map/dot_general | solution.py:295
  136.2 1.8 %fusion.12 = f32[512]{0:T(512)S(1)} fusion(f32[160,2048]{1,0:T(8,128)S(1)} %bitcast.56, s32[512]{0:T(512)S(1)} %get-tuple-element.46, f32[512]{0:T(512)S(1)} %get-tuple-element.55, s32[512]{0:T(512)S(1)} %pad_add_fusion.4, f32[512]{0:T(512)S(1)} %get-tuple-element.54, s32[512]{0:T(512)S(1)} %get-tuple-element.49, f32[512]{0:T(512)S(1)} %get-tuple-element.53, ...), kind=kOutput, calls=%fused_computation.19 | convolution fusion | flops 2015378944 | bytes 1331200 | tf_op jit(solution)/shard_map/dot_general | solution.py:295
  138.0 0.8 fusion.6
  138.8 12.5 %all_to_all.5 = f32[3,8,256]{2,0,1:T(4,128)S(1)} all-to-all(f32[3,8,256]{2,0,1:T(4,128)S(1)} %bitcast.43), channel_id=1, replica_groups=mesh['gz'=32,'gy'=8] {'gy'}, dimensions={1} | all-to-all | bytes 49152 | tf_op jit(solution)/shard_map/all_to_all | solution.py:310
  151.4 0.6 reduce_sum.39
  (36 shorter events, 0.2 us)
Async XLA Ops:
  2.6 5.6 %copy-start.5 = (s32[3]{0:T(128)S(1)}, s32[3]{0:T(128)}, u32[]{:S(2)}) copy-start(s32[3]{0:T(128)} %refs_0_.5) | copy-start | bytes 40
  2.8 36.9 %collective-permute-start = (f32[90,2048]{1,0:T(8,128)S(1)}, f32[90,2048]{1,0:T(8,128)}, u32[]{:S(2)}, u32[]{:S(2)}) collective-permute-start(f32[90,2048]{1,0:T(8,128)S(1)} %reshape.142), channel_id=1, source_target_pairs={{0,1},{1,2},{2,3},{3,4},{4,5},{5,6},{6,7},{7,0},{8,9},{9,10},{10,1... | collective-permute-start | bytes 2211848 | tf_op jit(solution)/shard_map/ppermute | solution.py:20
  7.0 34.5 %collective-permute-start.1 = (f32[90,2048]{1,0:T(8,128)}, f32[90,2048]{1,0:T(8,128)}, u32[]{:S(2)}, u32[]{:S(2)}) collective-permute-start(f32[90,2048]{1,0:T(8,128)} %reshape.144), channel_id=1, source_target_pairs={{1,0},{2,1},{3,2},{4,3},{5,4},{6,5},{7,6},{0,7},{9,8},{10,9},{11,1... | collective-permute-start | bytes 2211848 | tf_op jit(solution)/shard_map/ppermute | solution.py:20
  18.3 25.4 %copy-start.3 = (f32[10,16,2048]{2,1,0:T(8,128)S(1)}, f32[10,16,2048]{2,1,0:T(8,128)}, u32[]{:S(2)}) copy-start(f32[10,16,2048]{2,1,0:T(8,128)} %param.6) | copy-start | bytes 3932164
  51.7 3.1 %copy-start = (f32[10,18,2048]{2,1,0:T(8,128)}, f32[10,18,2048]{2,1,0:T(8,128)S(1)}, u32[]{:S(2)}) copy-start(f32[10,18,2048]{2,1,0:T(8,128)S(1)} %get-tuple-element.23.refs_2_) | copy-start | bytes 4423684
  51.7 3.1 %copy-start.1 = (f32[10,18,2048]{2,1,0:T(8,128)}, f32[10,18,2048]{2,1,0:T(8,128)S(1)}, u32[]{:S(2)}) copy-start(f32[10,18,2048]{2,1,0:T(8,128)S(1)} %get-tuple-element.22.refs_2_) | copy-start | bytes 4423684
  57.4 22.8 %collective-permute-start.6 = (f32[162,2048]{1,0:T(8,128)}, f32[162,2048]{1,0:T(8,128)}, u32[]{:S(2)}, u32[]{:S(2)}) collective-permute-start(f32[162,2048]{1,0:T(8,128)} %reshape.154), channel_id=1, source_target_pairs={{0,8},{8,16},{16,24},{24,32},{32,40},{40,48},{48,56},{56,64},{64,7... | collective-permute-start | bytes 3981320 | tf_op jit(solution)/shard_map/ppermute | solution.py:20
  58.7 26.3 %collective-permute-start.7 = (f32[162,2048]{1,0:T(8,128)}, f32[162,2048]{1,0:T(8,128)}, u32[]{:S(2)}, u32[]{:S(2)}) collective-permute-start(f32[162,2048]{1,0:T(8,128)} %reshape.156), channel_id=1, source_target_pairs={{8,0},{16,8},{24,16},{32,24},{40,32},{48,40},{56,48},{64,56},{72,6... | collective-permute-start | bytes 3981320 | tf_op jit(solution)/shard_map/ppermute | solution.py:20
  66.4 6.6 %copy-start.2 = (f32[10,18,2048]{2,1,0:T(8,128)S(1)}, f32[10,18,2048]{2,1,0:T(8,128)}, u32[]{:S(2)}) copy-start(f32[10,18,2048]{2,1,0:T(8,128)} %get-tuple-element.24.refs_2_) | copy-start | bytes 4423684
  66.4 32.8 %collective-permute-start.4 = (f32[162,2048]{1,0:T(8,128)}, f32[162,2048]{1,0:T(8,128)}, u32[]{:S(2)}, u32[]{:S(2)}) collective-permute-start(f32[162,2048]{1,0:T(8,128)} %reshape.150), channel_id=1, source_target_pairs={{0,8},{8,16},{16,24},{24,32},{32,40},{40,48},{48,56},{56,64},{64,7... | collective-permute-start | bytes 3981320 | tf_op jit(solution)/shard_map/ppermute | solution.py:20
  69.3 32.6 %collective-permute-start.5 = (f32[162,2048]{1,0:T(8,128)}, f32[162,2048]{1,0:T(8,128)}, u32[]{:S(2)}, u32[]{:S(2)}) collective-permute-start(f32[162,2048]{1,0:T(8,128)} %reshape.152), channel_id=1, source_target_pairs={{8,0},{16,8},{24,16},{32,24},{40,32},{48,40},{56,48},{64,56},{72,6... | collective-permute-start | bytes 3981320 | tf_op jit(solution)/shard_map/ppermute | solution.py:20
  75.2 2.0 %copy-start.4 = (f32[9,18,2048]{2,1,0:T(8,128)S(1)}, f32[9,18,2048]{2,1,0:T(8,128)}, u32[]{:S(2)}) copy-start(f32[9,18,2048]{2,1,0:T(8,128)} %get-tuple-element.29) | copy-start | bytes 3981316
  76.9 5.3 %copy-start.9 = (s32[256,1]{0,1:T(1,128)S(1)}, s32[256,1]{0,1:T(1,128)}, u32[]{:S(2)}) copy-start(s32[256,1]{0,1:T(1,128)} %param.8) | copy-start | bytes 3076
  76.9 5.3 %copy-start.7 = (s32[256]{0:T(256)S(1)}, s32[256]{0:T(256)}, u32[]{:S(2)}) copy-start(s32[256]{0:T(256)} %param.9) | copy-start | bytes 3076
  76.9 5.3 %copy-start.8 = (s32[256]{0:T(256)S(1)}, s32[256]{0:T(256)}, u32[]{:S(2)}) copy-start(s32[256]{0:T(256)} %param.10) | copy-start | bytes 3076
  77.0 5.3 %copy-start.6 = (f32[8,256]{1,0:T(8,128)S(1)}, f32[8,256]{1,0:T(8,128)}, u32[]{:S(2)}) copy-start(f32[8,256]{1,0:T(8,128)} %param.11) | copy-start | bytes 24580
  77.0 38.7 %collective-permute-start.2 = (f32[162,2048]{1,0:T(8,128)S(1)}, f32[162,2048]{1,0:T(8,128)}, u32[]{:S(2)}, u32[]{:S(2)}) collective-permute-start(f32[162,2048]{1,0:T(8,128)S(1)} %reshape.146), channel_id=1, source_target_pairs={{0,8},{8,16},{16,24},{24,32},{32,40},{40,48},{48,56},{56,64},{64,7... | collective-permute-start | bytes 3981320 | tf_op jit(solution)/shard_map/ppermute | solution.py:20
  80.2 38.1 %collective-permute-start.3 = (f32[162,2048]{1,0:T(8,128)}, f32[162,2048]{1,0:T(8,128)S(1)}, u32[]{:S(2)}, u32[]{:S(2)}) collective-permute-start(f32[162,2048]{1,0:T(8,128)} %reshape.148), channel_id=1, source_target_pairs={{8,0},{16,8},{24,16},{32,24},{40,32},{48,40},{56,48},{64,56},{72,6... | collective-permute-start | bytes 3981320 | tf_op jit(solution)/shard_map/ppermute | solution.py:20
  131.2 3.2 %copy-start.11 = (f32[10,16,2048]{2,1,0:T(8,128)S(1)}, f32[10,16,2048]{2,1,0:T(8,128)}, u32[]{:S(2)}) copy-start(f32[10,16,2048]{2,1,0:T(8,128)} %get-tuple-element.12) | copy-start | bytes 3932164
  134.4 1.8 %copy-start.10 = (f32[10,16,2048]{2,1,0:T(8,128)S(1)}, f32[10,16,2048]{2,1,0:T(8,128)}, u32[]{:S(2)}) copy-start(f32[10,16,2048]{2,1,0:T(8,128)} %get-tuple-element.11) | copy-start | bytes 3932164

commit v9 on v8

--- a/solution.py
+++ b/solution.py
@@ -57,13 +57,19 @@
 def level_kernel(level_index, first, slab_depth, band_rows, row_length):
     planes = slab_depth + 2
 
-    def compute(dilation, a_scr, s_scr, feature_ref, prev_ref, best_ref, row_wait, prev_copy, out_copy):
+    def compute(dilation, a_scr, s_scr, feature_ref, prev_ref, best_ref, row_wait, prev_copy,
+                out_copy, edges_in):
         reach = HALO - 1 + 2 * dilation
-        for row in range(reach):
+        last_mid = HALO + slab_depth - 1
+        edges_in()
+        for row in range(HALO, min(reach, last_mid + 1)):
             row_wait(row)
 
         def smooth_plane(plane, carry):
-            row_wait(reach + plane)
+            @pl.when(reach + plane <= last_mid)
+            def _():
+                row_wait(reach + plane)
+
             for first_row in range(0, band_rows + 2, 8):
                 rows = min(8, band_rows + 2 - first_row)
                 along_z = None
@@ -81,7 +87,7 @@
             return carry
 
         lax.fori_loop(0, planes, smooth_plane, 0)
-        for row in range(reach + planes, planes + 2 * HALO - 2):
+        for row in range(max(reach + planes, HALO), last_mid + 1):
             row_wait(row)
         if prev_copy is not None:
             prev_copy.wait()
@@ -134,16 +140,21 @@
     def kernel(*refs):
         if first:
             (dil_ref, lo_hbm, mid_hbm, hi_hbm, feature_hbm, best_hbm,
-             a_scr, s_scr, f_scr, b_scr, p_scr, row_sems, out_sems, prev_sem) = refs
+             a_scr, s_scr, f_scr, b_scr, p_scr, lo_scr, hi_scr, row_sems, out_sems, prev_sem,
+             edge_sems) = refs
         else:
             (dil_ref, lo_hbm, mid_hbm, hi_hbm, prev_hbm, feature_hbm, best_hbm,
-             a_scr, s_scr, f_scr, b_scr, p_scr, row_sems, out_sems, prev_sem) = refs
-        pieces = [(lo_hbm, HALO), (mid_hbm, slab_depth), (hi_hbm, HALO)]
-        row = 0
-        for source, count in pieces:
-            for index in range(count):
-                pltpu.make_async_copy(source.at[index], a_scr.at[row], row_sems.at[row]).start()
-                row += 1
+             a_scr, s_scr, f_scr, b_scr, p_scr, lo_scr, hi_scr, row_sems, out_sems, prev_sem,
+             edge_sems) = refs
+        edge_copies = [
+            pltpu.make_async_copy(lo_hbm, lo_scr, edge_sems.at[0]),
+            pltpu.make_async_copy(hi_hbm, hi_scr, edge_sems.at[1]),
+        ]
+        for copy in edge_copies:
+            copy.start()
+        for index in range(slab_depth):
+            row = HALO + index
+            pltpu.make_async_copy(mid_hbm.at[index], a_scr.at[row], row_sems.at[row]).start()
         prev_copy = None
         if not first:
             prev_copy = pltpu.make_async_copy(prev_hbm, p_scr, prev_sem.at[0])
@@ -151,6 +162,14 @@
 
         def row_wait(row):
             pltpu.make_async_copy(mid_hbm.at[0], a_scr.at[row], row_sems.at[row]).wait()
+
+        width = band_rows + 2
+
+        def edges_in():
+            for copy, flat, first_row in zip(edge_copies, (lo_scr, hi_scr), (0, HALO + slab_depth)):
+                copy.wait()
+                for index in range(HALO):
+                    a_scr[first_row + index] = flat[pl.ds(index * width, width), :]
 
         def out_copy(z):
             return [
@@ -161,7 +180,7 @@
         def branch(value):
             def run_branch():
                 compute(value, a_scr, s_scr, f_scr, None if first else p_scr, b_scr,
-                        row_wait, prev_copy, out_copy)
+                        row_wait, prev_copy, out_copy, edges_in)
             return run_branch
 
         pick = jnp.clip(dil_ref[level_index], 1, DMAX) - 1
@@ -187,9 +206,12 @@
                 pltpu.VMEM((slab_depth, band_rows, row_length), jnp.float32),
                 pltpu.VMEM((slab_depth, band_rows, row_length), jnp.float32),
                 pltpu.VMEM((slab_depth, band_rows, row_length), jnp.float32),
+                pltpu.VMEM((HALO * (band_rows + 2), row_length), jnp.float32),
+                pltpu.VMEM((HALO * (band_rows + 2), row_length), jnp.float32),
                 pltpu.SemaphoreType.DMA((total_rows,)),
                 pltpu.SemaphoreType.DMA((2, slab_depth)),
                 pltpu.SemaphoreType.DMA((1,)),
+                pltpu.SemaphoreType.DMA((2,)),
             ],
             compiler_params=pltpu.CompilerParams(vmem_limit_bytes=56 * 1024 * 1024),
         )(*operands)
@@ -202,8 +224,11 @@
     forward = [(i, i + 1) for i in range(count - 1)]
     forward.append((count - 1, 0))
     backward = [(target, source) for source, target in forward]
-    low = flat_ppermute(lax.slice_in_dim(block, block.shape[0] - width, None, axis=0), "gz", forward)
-    high = flat_ppermute(lax.slice_in_dim(block, 0, width, axis=0), "gz", backward)
+    def flat(part):
+        return part.reshape(part.shape[0] * part.shape[1], part.shape[2])
+
+    low = lax.ppermute(flat(lax.slice_in_dim(block, block.shape[0] - width, None, axis=0)), "gz", forward)
+    high = lax.ppermute(flat(lax.slice_in_dim(block, 0, width, axis=0)), "gz", backward)
     return low, high
 
 

time: 152 us -> 146 us (0.961)
  local copies, waits for them, and re-layouts: 38.4 us -> 26.6 us
  Pallas kernels: 34.1 us -> 36.1 us
    reshape x8 -> x2, local copies, waits for them, and re-layouts: 18.3 us -> 3.54 us  [flat_ppermute(): return moved.reshape(part.shape)]
    ppermute x0 -> x6, starting transfers between devices: none -> 13.4 us  [the longest x3 13.3 us: z_neighbours(): lax.ppermute(flat(lax.slice_in_dim(block, 0, width, axis=0)), 'gz', backw...]
    ppermute x8 -> x2, starting transfers between devices: 16.8 us -> 4.51 us  [flat_ppermute(): moved = lax.ppermute(part.reshape(rows, part.shape[2]), axis, pairs)]
    reshape x0 -> x6, local copies, waits for them, and re-layouts: none -> 12.1 us  [flat(): return part.reshape(part.shape[0] * part.shape[1], part.shape[2])]
    reshape x8 -> x2, local copies, waits for them, and re-layouts: 12.1 us -> 1.07 us  [flat_ppermute(): moved = lax.ppermute(part.reshape(rows, part.shape[2]), axis, pairs)]
    ppermute x0 -> x6, waiting for transfers between devices: none -> 3.36 us  [the longest x3 1.76 us: z_neighbours(): lax.ppermute(flat(lax.slice_in_dim(block, block.shape[0] - width, None, a...]
    pallas_call x3, Pallas kernels: 34.1 us -> 36.1 us  [run(): pl.pallas_call(kernel, out_shape=(block, block), in_specs=in_specs, out_s...]
    ppermute x8 -> x2, waiting for transfers between devices: 23.7 us -> 21.8 us  [flat_ppermute(): moved = lax.ppermute(part.reshape(rows, part.shape[2]), axis, pairs)]
  transfers between devices with their start and end apart: 8 -> 8, of which waited for: 3 -> 6; matrix products, arithmetic and copies ran while one was open for 18% -> 10% of each run, Pallas kernels for 15% -> 17%
where the time goes in v9:
time: 146 us; the launch traced here: 145 us
  Pallas kernels  36.1 us (25%)
  local copies, waits for them, and re-layouts  26.6 us (18%)
  waiting for transfers between devices  25.2 us (17%)
  starting transfers between devices  17.9 us (12%)
  blocking collectives  12.5 us (9%)
  between operations  10.4 us (7%)
  other arithmetic  8.58 us (6%)
  matrix products  7.56 us (5%)
    pallas_call x3, Pallas kernels, run(): pl.pallas_call(kernel, out_shape=(block, block), in_specs=in_specs, out_s...  36.1 us
    ppermute x2, waiting for transfers between devices, flat_ppermute(): moved = lax.ppermute(part.reshape(rows, part.shape[2]), axis, pairs)  21.8 us
    ppermute x3, starting transfers between devices, z_neighbours(): lax.ppermute(flat(lax.slice_in_dim(block, 0, width, axis=0)), 'gz', backw...  13.3 us
    all_to_all x1, blocking collectives, per_device(): lax.all_to_all(spread.reshape(SCALES, groups, HOWN), 'gy', split_axis=1,...  12.5 us
    reshape x6, local copies, waits for them, and re-layouts, flat(): return part.reshape(part.shape[0] * part.shape[1], part.shape[2])  12.1 us
    dot_general x3, matrix products, per_device(): jnp.dot(feature, pick_x, precision=lax.Precision.HIGHEST, preferred_eleme...  6.74 us
    add x1, other arithmetic, smooth_padded(): running = summand if running is None else running + summand  6.05 us
    slice x2, local copies, waits for them, and re-layouts, z_neighbours(): lax.slice_in_dim(block, 0, width, axis=0)  5.36 us
  transfers between devices with their start and end apart: 8, of which 6 were waited for; matrix products, arithmetic and copies ran while one was open for 10% of the time, Pallas kernels for 17%

profile of v9, /device:TPU:2, one launch (start us, length us, event | category | flops | bytes accessed | tf_op | source)
XLA Modules:
  0.0 144.9 jit_solution(4372024955760352985)
XLA Ops:
  0.6 2.1 %fusion.24 = (f32[10,9,2048]{2,1,0:T(8,128)S(1)}, f32[10,9,2048]{2,1,0:T(8,128)S(1)}) fusion(f32[10,16,2048]{2,1,0:T(8,128)} %param.6), kind=kLoop, calls=%fused_computation.66 | loop fusion | bytes 2949120 | tf_op jit(solution)/shard_map/slice | solution.py:31
  2.8 0.0 copy-start.7
  2.8 0.1 reshape.124
  2.9 3.3 %collective-permute-start = (f32[90,2048]{1,0:T(8,128)S(1)}, f32[90,2048]{1,0:T(8,128)}, u32[]{:S(2)}, u32[]{:S(2)}) collective-permute-start(f32[90,2048]{1,0:T(8,128)S(1)} %reshape.124), channel_id=1, source_target_pairs={{0,1},{1,2},{2,3},{3,4},{4,5},{5,6},{6,7},{7,0},{8,9},{9,10},{10,1... | collective-permute-start | bytes 2211848 | tf_op jit(solution)/shard_map/ppermute | solution.py:20
  6.2 1.0 reshape.126
  7.1 1.2 collective-permute-start.1
  8.4 0.0 copy-done.7
  8.4 0.6 fusion.26
  18.5 0.0 copy-start.3
  18.5 21.3 %collective-permute-done = f32[90,2048]{1,0:T(8,128)} collective-permute-done((f32[90,2048]{1,0:T(8,128)S(1)}, f32[90,2048]{1,0:T(8,128)}, u32[]{:S(2)}, u32[]{:S(2)}) %collective-permute-start) | collective-permute-done | bytes 737312 | tf_op jit(solution)/shard_map/ppermute | solution.py:20
  39.8 1.2 reshape.125
  41.1 0.6 collective-permute-done.1
  41.6 2.3 %reshape.127 = f32[10,9,2048]{2,1,0:T(8,128)} reshape(f32[90,2048]{1,0:T(8,128)} %collective-permute-done.1) | data formatting | bytes 1474560 | tf_op jit(solution)/shard_map/reshape | solution.py:21
  43.9 1.8 %pad_maximum_fusion = f32[10,34,2048]{2,1,0:T(8,128)S(1)} fusion(f32[10,9,2048]{2,1,0:T(8,128)} %reshape.127, f32[10,16,2048]{2,1,0:T(8,128)S(1)} %copy-done.3, f32[10,9,2048]{2,1,0:T(8,128)S(1)} %reshape.125), kind=kLoop, calls=%fused_computation.4 | loop fusion | flops 1392640 | bytes 5570560 | tf_op jit(solution)/shard_map/concatenate | solution.py:34
  45.7 6.0 %multiply_add_fusion = (f32[10,18,2048]{2,1,0:T(8,128)S(1)}, f32[10,18,2048]{2,1,0:T(8,128)S(1)}, f32[10,18,2048]{2,1,0:T(8,128)}) fusion(f32[10,34,2048]{2,1,0:T(8,128)S(1)} %pad_maximum_fusion, s32[]{:T(128)S(6)} %select_n.83, s32[]{:T(128)S(6)} %select_n.82, s32[]{:T(128)S(6)} %select_n.81, s32[]{:T(128)S(6)} %select_n.80, s32[]{:T(128)S(6)} %select_n.79, ...), kind=kLoop, calls=%fused_computation.11 | loop fusion | flops 9216000 | bytes 23593008 | tf_op jit(solution)/shard_map/add | solution.py:45
  51.8 3.1 %fusion.21 = (f32[9,18,2048]{2,1,0:T(8,128)S(1)}, f32[9,18,2048]{2,1,0:T(8,128)}, f32[9,18,2048]{2,1,0:T(8,128)S(1)}, f32[9,18,2048]{2,1,0:T(8,128)}) fusion(f32[10,18,2048]{2,1,0:T(8,128)S(1)} %get-tuple-element.22.refs_2_, f32[10,18,2048]{2,1,0:T(8,128)S(1)} %get-tuple-element.23.refs_2_), kind=kLoop, calls=%fused_computation.63 | loop fusion | bytes 10616832 | tf_op jit(solution)/shard_map/slice | solution.py:231
  54.9 2.7 %reshape.132 = f32[162,2048]{1,0:T(8,128)} reshape(f32[9,18,2048]{2,1,0:T(8,128)} %get-tuple-element.26) | data formatting | bytes 2654208 | tf_op jit(solution)/shard_map/reshape | solution.py:228
  57.6 0.0 collective-permute-start.6
  57.6 1.2 reshape.133
  58.8 6.5 %collective-permute-start.7 = (f32[162,2048]{1,0:T(8,128)}, f32[162,2048]{1,0:T(8,128)}, u32[]{:S(2)}, u32[]{:S(2)}) collective-permute-start(f32[162,2048]{1,0:T(8,128)} %reshape.133), channel_id=1, source_target_pairs={{8,0},{16,8},{24,16},{32,24},{40,32},{48,40},{56,48},{64,56},{72,6... | collective-permute-start | bytes 3981320 | tf_op jit(solution)/shard_map/ppermute | solution.py:231
  65.3 1.3 reshape.130
  66.6 0.0 collective-permute-start.4
  66.6 2.9 %reshape.131 = f32[162,2048]{1,0:T(8,128)} reshape(f32[9,18,2048]{2,1,0:T(8,128)} %get-tuple-element.51) | data formatting | bytes 2654208 | tf_op jit(solution)/shard_map/reshape | solution.py:228
  69.5 3.7 %collective-permute-start.5 = (f32[162,2048]{1,0:T(8,128)}, f32[162,2048]{1,0:T(8,128)}, u32[]{:S(2)}, u32[]{:S(2)}) collective-permute-start(f32[162,2048]{1,0:T(8,128)} %reshape.131), channel_id=1, source_target_pairs={{8,0},{16,8},{24,16},{32,24},{40,32},{48,40},{56,48},{64,56},{72,6... | collective-permute-start | bytes 3981320 | tf_op jit(solution)/shard_map/ppermute | solution.py:231
  73.2 2.3 %fusion.23 = (f32[9,18,2048]{2,1,0:T(8,128)}, f32[9,18,2048]{2,1,0:T(8,128)}) fusion(f32[10,18,2048]{2,1,0:T(8,128)S(1)} %copy-done.2), kind=kLoop, calls=%fused_computation.65 | loop fusion | bytes 5308416 | tf_op jit(solution)/shard_map/slice | solution.py:231
  75.5 2.8 %reshape.128 = f32[162,2048]{1,0:T(8,128)} reshape(f32[9,18,2048]{2,1,0:T(8,128)} %get-tuple-element.30) | data formatting | bytes 2654208 | tf_op jit(solution)/shard_map/reshape | solution.py:228
  78.3 0.1 collective-permute-start.2
  78.4 1.3 reshape.129
  79.6 0.7 collective-permute-done.6.refs_1_
  80.4 3.1 %collective-permute-start.3 = (f32[162,2048]{1,0:T(8,128)}, f32[162,2048]{1,0:T(8,128)S(1)}, u32[]{:S(2)}, u32[]{:S(2)}) collective-permute-start(f32[162,2048]{1,0:T(8,128)} %reshape.129), channel_id=1, source_target_pairs={{8,0},{16,8},{24,16},{32,24},{40,32},{48,40},{56,48},{64,56},{72,6... | collective-permute-start | bytes 3981320 | tf_op jit(solution)/shard_map/ppermute | solution.py:231
  83.5 0.0 copy-done.9
  83.6 0.0 copy-done.8
  83.7 0.0 collective-permute-done.7.refs_3_
  83.7 12.0 %shard_map.77 = (f32[10,16,2048]{2,1,0:T(8,128)}, f32[10,16,2048]{2,1,0:T(8,128)}) custom-call(s32[3]{0:T(128)} %refs_0_.5, f32[162,2048]{1,0:T(8,128)} %collective-permute-done.6.refs_1_, f32[10,18,2048]{2,1,0:T(8,128)} %copy-done.1, f32[162,2048]{1,0:T(8,128)} %collective-permute-done.7.refs_3_), custom_call_target="tpu_custom_call" | custom-call | tf_op jit(solution)/shard_map/pallas_call | solution.py:198
  95.7 0.0 collective-permute-done.4.refs_1_
  95.7 0.5 collective-permute-done.5.refs_3_
  96.2 0.6 copy-done.5
  96.8 12.0 %shard_map.78 = (f32[10,16,2048]{2,1,0:T(8,128)}, f32[10,16,2048]{2,1,0:T(8,128)}) custom-call(s32[3]{0:T(128)} %refs_0_.5, f32[162,2048]{1,0:T(8,128)} %copy-done.5, f32[10,18,2048]{2,1,0:T(8,128)} %copy-done, f32[162,2048]{1,0:T(8,128)} %collective-permute-done.5.refs_3_, f32[10,16,2048]{2,1,0:T(8,128)} %get-tuple-element.8.refs_4_), custom_call_target="tpu_custom_call" | custom-call | tf_op jit(solution)/shard_map/pallas_call | solution.py:198
  108.8 1.0 collective-permute-done.2.refs_1_
  109.9 1.1 collective-permute-done.3.refs_3_
  111.0 1.1 copy-done.6
  112.1 12.0 %shard_map.79 = (f32[10,16,2048]{2,1,0:T(8,128)}, f32[10,16,2048]{2,1,0:T(8,128)}) custom-call(s32[3]{0:T(128)} %refs_0_.5, f32[162,2048]{1,0:T(8,128)} %collective-permute-done.2.refs_1_, f32[10,18,2048]{2,1,0:T(8,128)} %get-tuple-element.24.refs_2_, f32[162,2048]{1,0:T(8,128)} %copy-done.6, f32[10,16,2048]{2,1,0:T(8,128)} %get-tuple-element.9.refs_4_), custom_call_target="tpu_custom_call" | custom-call | tf_op jit(solution)/shard_map/pallas_call | solution.py:198
  124.1 3.2 %fusion.10 = f32[512]{0:T(512)S(1)} fusion(f32[160,2048]{1,0:T(8,128)} %bitcast.58, s32[512]{0:T(512)S(1)} %get-tuple-element.46, f32[512]{0:T(512)S(1)} %get-tuple-element.55, s32[512]{0:T(512)S(1)} %pad_add_fusion.4, f32[512]{0:T(512)S(1)} %get-tuple-element.54, s32[512]{0:T(512)S(1)} %get-tuple-element.49, f32[512]{0:T(512)S(1)} %get-tuple-element.53, ...), kind=kOutput, calls=%fused_computation.17 | convolution fusion | flops 2015378944 | bytes 1331200 | tf_op jit(solution)/shard_map/dot_general | solution.py:320
  127.3 1.8 %fusion.11 = f32[512]{0:T(512)S(1)} fusion(f32[160,2048]{1,0:T(8,128)S(1)} %bitcast.57, s32[512]{0:T(512)S(1)} %get-tuple-element.46, f32[512]{0:T(512)S(1)} %get-tuple-element.55, s32[512]{0:T(512)S(1)} %pad_add_fusion.4, f32[512]{0:T(512)S(1)} %get-tuple-element.54, s32[512]{0:T(512)S(1)} %get-tuple-element.49, f32[512]{0:T(512)S(1)} %get-tuple-element.53, ...), kind=kOutput, calls=%fused_computation.18 | convolution fusion | flops 2015378944 | bytes 1331200 | tf_op jit(solution)/shard_map/dot_general | solution.py:320
  129.1 1.8 %fusion.12 = f32[512]{0:T(512)S(1)} fusion(f32[160,2048]{1,0:T(8,128)S(1)} %bitcast.56, s32[512]{0:T(512)S(1)} %get-tuple-element.46, f32[512]{0:T(512)S(1)} %get-tuple-element.55, s32[512]{0:T(512)S(1)} %pad_add_fusion.4, f32[512]{0:T(512)S(1)} %get-tuple-element.54, s32[512]{0:T(512)S(1)} %get-tuple-element.49, f32[512]{0:T(512)S(1)} %get-tuple-element.53, ...), kind=kOutput, calls=%fused_computation.19 | convolution fusion | flops 2015378944 | bytes 1331200 | tf_op jit(solution)/shard_map/dot_general | solution.py:320
  130.9 0.8 fusion.6
  131.7 12.5 %all_to_all.5 = f32[3,8,256]{2,0,1:T(4,128)S(1)} all-to-all(f32[3,8,256]{2,0,1:T(4,128)S(1)} %bitcast.43), channel_id=1, replica_groups=mesh['gz'=32,'gy'=8] {'gy'}, dimensions={1} | all-to-all | bytes 49152 | tf_op jit(solution)/shard_map/all_to_all | solution.py:335
  144.3 0.6 reduce_sum.39
  (34 shorter events, 0.2 us)
Async XLA Ops:
  2.8 5.6 %copy-start.7 = (s32[3]{0:T(128)S(1)}, s32[3]{0:T(128)}, u32[]{:S(2)}) copy-start(s32[3]{0:T(128)} %refs_0_.5) | copy-start | bytes 40
  2.9 36.9 %collective-permute-start = (f32[90,2048]{1,0:T(8,128)S(1)}, f32[90,2048]{1,0:T(8,128)}, u32[]{:S(2)}, u32[]{:S(2)}) collective-permute-start(f32[90,2048]{1,0:T(8,128)S(1)} %reshape.124), channel_id=1, source_target_pairs={{0,1},{1,2},{2,3},{3,4},{4,5},{5,6},{6,7},{7,0},{8,9},{9,10},{10,1... | collective-permute-start | bytes 2211848 | tf_op jit(solution)/shard_map/ppermute | solution.py:20
  7.1 34.5 %collective-permute-start.1 = (f32[90,2048]{1,0:T(8,128)}, f32[90,2048]{1,0:T(8,128)}, u32[]{:S(2)}, u32[]{:S(2)}) collective-permute-start(f32[90,2048]{1,0:T(8,128)} %reshape.126), channel_id=1, source_target_pairs={{1,0},{2,1},{3,2},{4,3},{5,4},{6,5},{7,6},{0,7},{9,8},{10,9},{11,1... | collective-permute-start | bytes 2211848 | tf_op jit(solution)/shard_map/ppermute | solution.py:20
  18.5 25.4 %copy-start.3 = (f32[10,16,2048]{2,1,0:T(8,128)S(1)}, f32[10,16,2048]{2,1,0:T(8,128)}, u32[]{:S(2)}) copy-start(f32[10,16,2048]{2,1,0:T(8,128)} %param.6) | copy-start | bytes 3932164
  51.8 3.1 %copy-start = (f32[10,18,2048]{2,1,0:T(8,128)}, f32[10,18,2048]{2,1,0:T(8,128)S(1)}, u32[]{:S(2)}) copy-start(f32[10,18,2048]{2,1,0:T(8,128)S(1)} %get-tuple-element.23.refs_2_) | copy-start | bytes 4423684
  51.8 3.1 %copy-start.1 = (f32[10,18,2048]{2,1,0:T(8,128)}, f32[10,18,2048]{2,1,0:T(8,128)S(1)}, u32[]{:S(2)}) copy-start(f32[10,18,2048]{2,1,0:T(8,128)S(1)} %get-tuple-element.22.refs_2_) | copy-start | bytes 4423684
  57.6 22.8 %collective-permute-start.6 = (f32[162,2048]{1,0:T(8,128)}, f32[162,2048]{1,0:T(8,128)}, u32[]{:S(2)}, u32[]{:S(2)}) collective-permute-start(f32[162,2048]{1,0:T(8,128)} %reshape.132), channel_id=1, source_target_pairs={{0,8},{8,16},{16,24},{24,32},{32,40},{40,48},{48,56},{56,64},{64,7... | collective-permute-start | bytes 3981320 | tf_op jit(solution)/shard_map/ppermute | solution.py:230
  58.8 24.8 %collective-permute-start.7 = (f32[162,2048]{1,0:T(8,128)}, f32[162,2048]{1,0:T(8,128)}, u32[]{:S(2)}, u32[]{:S(2)}) collective-permute-start(f32[162,2048]{1,0:T(8,128)} %reshape.133), channel_id=1, source_target_pairs={{8,0},{16,8},{24,16},{32,24},{40,32},{48,40},{56,48},{64,56},{72,6... | collective-permute-start | bytes 3981320 | tf_op jit(solution)/shard_map/ppermute | solution.py:231
  66.6 6.6 %copy-start.2 = (f32[10,18,2048]{2,1,0:T(8,128)S(1)}, f32[10,18,2048]{2,1,0:T(8,128)}, u32[]{:S(2)}) copy-start(f32[10,18,2048]{2,1,0:T(8,128)} %get-tuple-element.24.refs_2_) | copy-start | bytes 4423684
  66.6 29.1 %collective-permute-start.4 = (f32[162,2048]{1,0:T(8,128)}, f32[162,2048]{1,0:T(8,128)S(1)}, u32[]{:S(2)}, u32[]{:S(2)}) collective-permute-start(f32[162,2048]{1,0:T(8,128)} %reshape.130), channel_id=1, source_target_pairs={{0,8},{8,16},{16,24},{24,32},{32,40},{40,48},{48,56},{56,64},{64,7... | collective-permute-start | bytes 3981320 | tf_op jit(solution)/shard_map/ppermute | solution.py:230
  69.5 26.7 %collective-permute-start.5 = (f32[162,2048]{1,0:T(8,128)}, f32[162,2048]{1,0:T(8,128)}, u32[]{:S(2)}, u32[]{:S(2)}) collective-permute-start(f32[162,2048]{1,0:T(8,128)} %reshape.131), channel_id=1, source_target_pairs={{8,0},{16,8},{24,16},{32,24},{40,32},{48,40},{56,48},{64,56},{72,6... | collective-permute-start | bytes 3981320 | tf_op jit(solution)/shard_map/ppermute | solution.py:231
  75.5 2.9 %copy-start.4 = (f32[9,18,2048]{2,1,0:T(8,128)S(1)}, f32[9,18,2048]{2,1,0:T(8,128)}, u32[]{:S(2)}) copy-start(f32[9,18,2048]{2,1,0:T(8,128)} %get-tuple-element.29) | copy-start | bytes 3981316
  78.3 5.2 %copy-start.11 = (s32[256,1]{0,1:T(1,128)S(1)}, s32[256,1]{0,1:T(1,128)}, u32[]{:S(2)}) copy-start(s32[256,1]{0,1:T(1,128)} %param.8) | copy-start | bytes 3076
  78.3 5.2 %copy-start.9 = (s32[256]{0:T(256)S(1)}, s32[256]{0:T(256)}, u32[]{:S(2)}) copy-start(s32[256]{0:T(256)} %param.9) | copy-start | bytes 3076
  78.3 5.2 %copy-start.10 = (s32[256]{0:T(256)S(1)}, s32[256]{0:T(256)}, u32[]{:S(2)}) copy-start(s32[256]{0:T(256)} %param.10) | copy-start | bytes 3076
  78.3 5.3 %copy-start.8 = (f32[8,256]{1,0:T(8,128)S(1)}, f32[8,256]{1,0:T(8,128)}, u32[]{:S(2)}) copy-start(f32[8,256]{1,0:T(8,128)} %param.11) | copy-start | bytes 24580
  78.3 31.6 %collective-permute-start.2 = (f32[162,2048]{1,0:T(8,128)}, f32[162,2048]{1,0:T(8,128)}, u32[]{:S(2)}, u32[]{:S(2)}) collective-permute-start(f32[162,2048]{1,0:T(8,128)} %reshape.128), channel_id=1, source_target_pairs={{0,8},{8,16},{16,24},{24,32},{32,40},{40,48},{48,56},{56,64},{64,7... | collective-permute-start | bytes 3981320 | tf_op jit(solution)/shard_map/ppermute | solution.py:230
  80.4 30.6 %collective-permute-start.3 = (f32[162,2048]{1,0:T(8,128)}, f32[162,2048]{1,0:T(8,128)S(1)}, u32[]{:S(2)}, u32[]{:S(2)}) collective-permute-start(f32[162,2048]{1,0:T(8,128)} %reshape.129), channel_id=1, source_target_pairs={{8,0},{16,8},{24,16},{32,24},{40,32},{48,40},{56,48},{64,56},{72,6... | collective-permute-start | bytes 3981320 | tf_op jit(solution)/shard_map/ppermute | solution.py:231
  95.7 1.1 copy-start.5
  111.0 1.1 copy-start.6
  124.1 3.2 %copy-start.13 = (f32[10,16,2048]{2,1,0:T(8,128)S(1)}, f32[10,16,2048]{2,1,0:T(8,128)}, u32[]{:S(2)}) copy-start(f32[10,16,2048]{2,1,0:T(8,128)} %get-tuple-element.12) | copy-start | bytes 3932164
  127.3 1.8 %copy-start.12 = (f32[10,16,2048]{2,1,0:T(8,128)S(1)}, f32[10,16,2048]{2,1,0:T(8,128)}, u32[]{:S(2)}) copy-start(f32[10,16,2048]{2,1,0:T(8,128)} %get-tuple-element.11) | copy-start | bytes 3932164

commit v10 on v9

--- a/solution.py
+++ b/solution.py
@@ -318,7 +318,7 @@
     partials = []
     for feature in features:
         picked = jnp.dot(
-            feature, pick_x, precision=lax.Precision.HIGHEST, preferred_element_type=jnp.float32
+            feature, pick_x, precision=lax.Precision.HIGH, preferred_element_type=jnp.float32
         )
         per_column = jnp.sum(picked * weight_grid, axis=0)
         partials.append(per_column[:entries] + per_column[entries:])
@@ -330,7 +330,7 @@
         jnp.float32
     )
     spread = jnp.dot(
-        partial_value, onehot, precision=lax.Precision.HIGHEST, preferred_element_type=jnp.float32
+        partial_value, onehot, precision=lax.Precision.HIGH, preferred_element_type=jnp.float32
     )
     exchanged = lax.all_to_all(
         spread.reshape(SCALES, groups, HOWN), "gy", split_axis=1, concat_axis=1, tiled=True

time: 146 us -> 145 us (level)
  no operation moved by 1% of the time
where the time goes in v10:
time: 145 us; the launch traced here: 143 us
  Pallas kernels  36.1 us (25%)
  local copies, waits for them, and re-layouts  26.6 us (18%)
  waiting for transfers between devices  25.2 us (17%)
  starting transfers between devices  17.9 us (12%)
  blocking collectives  12.5 us (9%)
  between operations  10.4 us (7%)
  other arithmetic  8.57 us (6%)
  matrix products  6.15 us (4%)
    pallas_call x3, Pallas kernels, run(): pl.pallas_call(kernel, out_shape=(block, block), in_specs=in_specs, out_s...  36.1 us
    ppermute x2, waiting for transfers between devices, flat_ppermute(): moved = lax.ppermute(part.reshape(rows, part.shape[2]), axis, pairs)  21.8 us
    ppermute x3, starting transfers between devices, z_neighbours(): lax.ppermute(flat(lax.slice_in_dim(block, 0, width, axis=0)), 'gz', backw...  13.3 us
    all_to_all x1, blocking collectives, per_device(): lax.all_to_all(spread.reshape(SCALES, groups, HOWN), 'gy', split_axis=1,...  12.5 us
    reshape x6, local copies, waits for them, and re-layouts, flat(): return part.reshape(part.shape[0] * part.shape[1], part.shape[2])  12.1 us
    add x1, other arithmetic, smooth_padded(): running = summand if running is None else running + summand  6.03 us
    dot_general x3, matrix products, per_device(): jnp.dot(feature, pick_x, precision=lax.Precision.HIGH, preferred_element_...  5.47 us
    slice x2, local copies, waits for them, and re-layouts, z_neighbours(): lax.slice_in_dim(block, 0, width, axis=0)  5.36 us
  transfers between devices with their start and end apart: 8, of which 6 were waited for; matrix products, arithmetic and copies ran while one was open for 10% of the time, Pallas kernels for 17%

profile of v10, /device:TPU:2, one launch (start us, length us, event | category | flops | bytes accessed | tf_op | source)
XLA Modules:
  0.0 143.4 jit_solution(256806692307636170)
XLA Ops:
  0.6 2.1 %fusion.24 = (f32[10,9,2048]{2,1,0:T(8,128)S(1)}, f32[10,9,2048]{2,1,0:T(8,128)S(1)}) fusion(f32[10,16,2048]{2,1,0:T(8,128)} %param.6), kind=kLoop, calls=%fused_computation.66 | loop fusion | bytes 2949120 | tf_op jit(solution)/shard_map/slice | solution.py:31
  2.8 0.0 copy-start.7
  2.8 0.1 reshape.124
  2.9 3.3 %collective-permute-start = (f32[90,2048]{1,0:T(8,128)S(1)}, f32[90,2048]{1,0:T(8,128)}, u32[]{:S(2)}, u32[]{:S(2)}) collective-permute-start(f32[90,2048]{1,0:T(8,128)S(1)} %reshape.124), channel_id=1, source_target_pairs={{0,1},{1,2},{2,3},{3,4},{4,5},{5,6},{6,7},{7,0},{8,9},{9,10},{10,1... | collective-permute-start | bytes 2211848 | tf_op jit(solution)/shard_map/ppermute | solution.py:20
  6.2 1.0 reshape.126
  7.1 1.2 collective-permute-start.1
  8.4 0.0 copy-done.7
  8.4 0.6 fusion.26
  18.5 0.0 copy-start.3
  18.5 21.3 %collective-permute-done = f32[90,2048]{1,0:T(8,128)} collective-permute-done((f32[90,2048]{1,0:T(8,128)S(1)}, f32[90,2048]{1,0:T(8,128)}, u32[]{:S(2)}, u32[]{:S(2)}) %collective-permute-start) | collective-permute-done | bytes 737312 | tf_op jit(solution)/shard_map/ppermute | solution.py:20
  39.8 1.2 reshape.125
  41.1 0.6 collective-permute-done.1
  41.6 2.3 %reshape.127 = f32[10,9,2048]{2,1,0:T(8,128)} reshape(f32[90,2048]{1,0:T(8,128)} %collective-permute-done.1) | data formatting | bytes 1474560 | tf_op jit(solution)/shard_map/reshape | solution.py:21
  43.9 1.8 %pad_maximum_fusion = f32[10,34,2048]{2,1,0:T(8,128)S(1)} fusion(f32[10,9,2048]{2,1,0:T(8,128)} %reshape.127, f32[10,16,2048]{2,1,0:T(8,128)S(1)} %copy-done.3, f32[10,9,2048]{2,1,0:T(8,128)S(1)} %reshape.125), kind=kLoop, calls=%fused_computation.4 | loop fusion | flops 1392640 | bytes 5570560 | tf_op jit(solution)/shard_map/concatenate | solution.py:34
  45.7 6.0 %multiply_add_fusion = (f32[10,18,2048]{2,1,0:T(8,128)S(1)}, f32[10,18,2048]{2,1,0:T(8,128)S(1)}, f32[10,18,2048]{2,1,0:T(8,128)}) fusion(f32[10,34,2048]{2,1,0:T(8,128)S(1)} %pad_maximum_fusion, s32[]{:T(128)S(6)} %select_n.83, s32[]{:T(128)S(6)} %select_n.82, s32[]{:T(128)S(6)} %select_n.81, s32[]{:T(128)S(6)} %select_n.80, s32[]{:T(128)S(6)} %select_n.79, ...), kind=kLoop, calls=%fused_computation.11 | loop fusion | flops 9216000 | bytes 23593008 | tf_op jit(solution)/shard_map/add | solution.py:45
  51.8 3.1 %fusion.21 = (f32[9,18,2048]{2,1,0:T(8,128)S(1)}, f32[9,18,2048]{2,1,0:T(8,128)}, f32[9,18,2048]{2,1,0:T(8,128)S(1)}, f32[9,18,2048]{2,1,0:T(8,128)}) fusion(f32[10,18,2048]{2,1,0:T(8,128)S(1)} %get-tuple-element.22.refs_2_, f32[10,18,2048]{2,1,0:T(8,128)S(1)} %get-tuple-element.23.refs_2_), kind=kLoop, calls=%fused_computation.63 | loop fusion | bytes 10616832 | tf_op jit(solution)/shard_map/slice | solution.py:231
  54.9 0.0 copy-done.1
  54.9 2.7 %reshape.132 = f32[162,2048]{1,0:T(8,128)} reshape(f32[9,18,2048]{2,1,0:T(8,128)} %get-tuple-element.26) | data formatting | bytes 2654208 | tf_op jit(solution)/shard_map/reshape | solution.py:228
  57.6 0.0 collective-permute-start.6
  57.6 1.2 reshape.133
  58.8 6.5 %collective-permute-start.7 = (f32[162,2048]{1,0:T(8,128)}, f32[162,2048]{1,0:T(8,128)}, u32[]{:S(2)}, u32[]{:S(2)}) collective-permute-start(f32[162,2048]{1,0:T(8,128)} %reshape.133), channel_id=1, source_target_pairs={{8,0},{16,8},{24,16},{32,24},{40,32},{48,40},{56,48},{64,56},{72,6... | collective-permute-start | bytes 3981320 | tf_op jit(solution)/shard_map/ppermute | solution.py:231
  65.3 1.3 reshape.130
  66.6 0.0 collective-permute-start.4
  66.6 2.9 %reshape.131 = f32[162,2048]{1,0:T(8,128)} reshape(f32[9,18,2048]{2,1,0:T(8,128)} %get-tuple-element.51) | data formatting | bytes 2654208 | tf_op jit(solution)/shard_map/reshape | solution.py:228
  69.5 3.7 %collective-permute-start.5 = (f32[162,2048]{1,0:T(8,128)}, f32[162,2048]{1,0:T(8,128)}, u32[]{:S(2)}, u32[]{:S(2)}) collective-permute-start(f32[162,2048]{1,0:T(8,128)} %reshape.131), channel_id=1, source_target_pairs={{8,0},{16,8},{24,16},{32,24},{40,32},{48,40},{56,48},{64,56},{72,6... | collective-permute-start | bytes 3981320 | tf_op jit(solution)/shard_map/ppermute | solution.py:231
  73.2 0.0 copy-done.2
  73.2 2.3 %fusion.23 = (f32[9,18,2048]{2,1,0:T(8,128)}, f32[9,18,2048]{2,1,0:T(8,128)}) fusion(f32[10,18,2048]{2,1,0:T(8,128)S(1)} %copy-done.2), kind=kLoop, calls=%fused_computation.65 | loop fusion | bytes 5308416 | tf_op jit(solution)/shard_map/slice | solution.py:231
  75.5 2.8 %reshape.128 = f32[162,2048]{1,0:T(8,128)} reshape(f32[9,18,2048]{2,1,0:T(8,128)} %get-tuple-element.30) | data formatting | bytes 2654208 | tf_op jit(solution)/shard_map/reshape | solution.py:228
  78.3 0.1 collective-permute-start.2
  78.4 1.3 reshape.129
  79.6 0.7 collective-permute-done.6.refs_1_
  80.4 3.1 %collective-permute-start.3 = (f32[162,2048]{1,0:T(8,128)}, f32[162,2048]{1,0:T(8,128)S(1)}, u32[]{:S(2)}, u32[]{:S(2)}) collective-permute-start(f32[162,2048]{1,0:T(8,128)} %reshape.129), channel_id=1, source_target_pairs={{8,0},{16,8},{24,16},{32,24},{40,32},{48,40},{56,48},{64,56},{72,6... | collective-permute-start | bytes 3981320 | tf_op jit(solution)/shard_map/ppermute | solution.py:231
  83.6 0.0 collective-permute-done.7.refs_3_
  83.7 12.0 %shard_map.77 = (f32[10,16,2048]{2,1,0:T(8,128)}, f32[10,16,2048]{2,1,0:T(8,128)}) custom-call(s32[3]{0:T(128)} %refs_0_.5, f32[162,2048]{1,0:T(8,128)} %collective-permute-done.6.refs_1_, f32[10,18,2048]{2,1,0:T(8,128)} %copy-done.1, f32[162,2048]{1,0:T(8,128)} %collective-permute-done.7.refs_3_), custom_call_target="tpu_custom_call" | custom-call | tf_op jit(solution)/shard_map/pallas_call | solution.py:198
  95.7 0.0 collective-permute-done.4.refs_1_
  95.7 0.5 collective-permute-done.5.refs_3_
  96.2 0.6 copy-done.5
  96.8 12.1 %shard_map.78 = (f32[10,16,2048]{2,1,0:T(8,128)}, f32[10,16,2048]{2,1,0:T(8,128)}) custom-call(s32[3]{0:T(128)} %refs_0_.5, f32[162,2048]{1,0:T(8,128)} %copy-done.5, f32[10,18,2048]{2,1,0:T(8,128)} %copy-done, f32[162,2048]{1,0:T(8,128)} %collective-permute-done.5.refs_3_, f32[10,16,2048]{2,1,0:T(8,128)} %get-tuple-element.8.refs_4_), custom_call_target="tpu_custom_call" | custom-call | tf_op jit(solution)/shard_map/pallas_call | solution.py:198
  108.9 1.0 collective-permute-done.2.refs_1_
  109.9 1.1 collective-permute-done.3.refs_3_
  110.9 1.1 copy-done.6
  112.0 12.0 %shard_map.79 = (f32[10,16,2048]{2,1,0:T(8,128)}, f32[10,16,2048]{2,1,0:T(8,128)}) custom-call(s32[3]{0:T(128)} %refs_0_.5, f32[162,2048]{1,0:T(8,128)} %collective-permute-done.2.refs_1_, f32[10,18,2048]{2,1,0:T(8,128)} %get-tuple-element.24.refs_2_, f32[162,2048]{1,0:T(8,128)} %copy-done.6, f32[10,16,2048]{2,1,0:T(8,128)} %get-tuple-element.9.refs_4_), custom_call_target="tpu_custom_call" | custom-call | tf_op jit(solution)/shard_map/pallas_call | solution.py:198
  124.1 2.8 %fusion.10 = f32[512]{0:T(512)S(1)} fusion(f32[160,2048]{1,0:T(8,128)} %bitcast.58, s32[512]{0:T(512)S(1)} %get-tuple-element.46, f32[512]{0:T(512)S(1)} %get-tuple-element.55, s32[512]{0:T(512)S(1)} %pad_add_fusion.4, f32[512]{0:T(512)S(1)} %get-tuple-element.54, s32[512]{0:T(512)S(1)} %get-tuple-element.49, f32[512]{0:T(512)S(1)} %get-tuple-element.53, ...), kind=kOutput, calls=%fused_computation.17 | convolution fusion | flops 1008745984 | bytes 1331200 | tf_op jit(solution)/shard_map/dot_general | solution.py:320
  126.9 1.3 fusion.11
  128.2 1.3 fusion.12
  129.6 0.7 fusion.6
  130.3 12.5 %all_to_all.5 = f32[3,8,256]{2,0,1:T(4,128)S(1)} all-to-all(f32[3,8,256]{2,0,1:T(4,128)S(1)} %bitcast.43), channel_id=1, replica_groups=mesh['gz'=32,'gy'=8] {'gy'}, dimensions={1} | all-to-all | bytes 49152 | tf_op jit(solution)/shard_map/all_to_all | solution.py:335
  142.8 0.6 reduce_sum.39
  (34 shorter events, 0.2 us)
Async XLA Ops:
  2.8 5.6 %copy-start.7 = (s32[3]{0:T(128)S(1)}, s32[3]{0:T(128)}, u32[]{:S(2)}) copy-start(s32[3]{0:T(128)} %refs_0_.5) | copy-start | bytes 40
  2.9 36.9 %collective-permute-start = (f32[90,2048]{1,0:T(8,128)S(1)}, f32[90,2048]{1,0:T(8,128)}, u32[]{:S(2)}, u32[]{:S(2)}) collective-permute-start(f32[90,2048]{1,0:T(8,128)S(1)} %reshape.124), channel_id=1, source_target_pairs={{0,1},{1,2},{2,3},{3,4},{4,5},{5,6},{6,7},{7,0},{8,9},{9,10},{10,1... | collective-permute-start | bytes 2211848 | tf_op jit(solution)/shard_map/ppermute | solution.py:20
  7.1 34.5 %collective-permute-start.1 = (f32[90,2048]{1,0:T(8,128)}, f32[90,2048]{1,0:T(8,128)}, u32[]{:S(2)}, u32[]{:S(2)}) collective-permute-start(f32[90,2048]{1,0:T(8,128)} %reshape.126), channel_id=1, source_target_pairs={{1,0},{2,1},{3,2},{4,3},{5,4},{6,5},{7,6},{0,7},{9,8},{10,9},{11,1... | collective-permute-start | bytes 2211848 | tf_op jit(solution)/shard_map/ppermute | solution.py:20
  18.5 25.4 %copy-start.3 = (f32[10,16,2048]{2,1,0:T(8,128)S(1)}, f32[10,16,2048]{2,1,0:T(8,128)}, u32[]{:S(2)}) copy-start(f32[10,16,2048]{2,1,0:T(8,128)} %param.6) | copy-start | bytes 3932164
  51.8 3.1 %copy-start = (f32[10,18,2048]{2,1,0:T(8,128)}, f32[10,18,2048]{2,1,0:T(8,128)S(1)}, u32[]{:S(2)}) copy-start(f32[10,18,2048]{2,1,0:T(8,128)S(1)} %get-tuple-element.23.refs_2_) | copy-start | bytes 4423684
  51.8 3.1 %copy-start.1 = (f32[10,18,2048]{2,1,0:T(8,128)}, f32[10,18,2048]{2,1,0:T(8,128)S(1)}, u32[]{:S(2)}) copy-start(f32[10,18,2048]{2,1,0:T(8,128)S(1)} %get-tuple-element.22.refs_2_) | copy-start | bytes 4423684
  57.6 22.8 %collective-permute-start.6 = (f32[162,2048]{1,0:T(8,128)}, f32[162,2048]{1,0:T(8,128)}, u32[]{:S(2)}, u32[]{:S(2)}) collective-permute-start(f32[162,2048]{1,0:T(8,128)} %reshape.132), channel_id=1, source_target_pairs={{0,8},{8,16},{16,24},{24,32},{32,40},{40,48},{48,56},{56,64},{64,7... | collective-permute-start | bytes 3981320 | tf_op jit(solution)/shard_map/ppermute | solution.py:230
  58.8 24.8 %collective-permute-start.7 = (f32[162,2048]{1,0:T(8,128)}, f32[162,2048]{1,0:T(8,128)}, u32[]{:S(2)}, u32[]{:S(2)}) collective-permute-start(f32[162,2048]{1,0:T(8,128)} %reshape.133), channel_id=1, source_target_pairs={{8,0},{16,8},{24,16},{32,24},{40,32},{48,40},{56,48},{64,56},{72,6... | collective-permute-start | bytes 3981320 | tf_op jit(solution)/shard_map/ppermute | solution.py:231
  66.6 6.6 %copy-start.2 = (f32[10,18,2048]{2,1,0:T(8,128)S(1)}, f32[10,18,2048]{2,1,0:T(8,128)}, u32[]{:S(2)}) copy-start(f32[10,18,2048]{2,1,0:T(8,128)} %get-tuple-element.24.refs_2_) | copy-start | bytes 4423684
  66.6 29.1 %collective-permute-start.4 = (f32[162,2048]{1,0:T(8,128)}, f32[162,2048]{1,0:T(8,128)S(1)}, u32[]{:S(2)}, u32[]{:S(2)}) collective-permute-start(f32[162,2048]{1,0:T(8,128)} %reshape.130), channel_id=1, source_target_pairs={{0,8},{8,16},{16,24},{24,32},{32,40},{40,48},{48,56},{56,64},{64,7... | collective-permute-start | bytes 3981320 | tf_op jit(solution)/shard_map/ppermute | solution.py:230
  69.5 26.7 %collective-permute-start.5 = (f32[162,2048]{1,0:T(8,128)}, f32[162,2048]{1,0:T(8,128)}, u32[]{:S(2)}, u32[]{:S(2)}) collective-permute-start(f32[162,2048]{1,0:T(8,128)} %reshape.131), channel_id=1, source_target_pairs={{8,0},{16,8},{24,16},{32,24},{40,32},{48,40},{56,48},{64,56},{72,6... | collective-permute-start | bytes 3981320 | tf_op jit(solution)/shard_map/ppermute | solution.py:231
  75.5 2.9 %copy-start.4 = (f32[9,18,2048]{2,1,0:T(8,128)S(1)}, f32[9,18,2048]{2,1,0:T(8,128)}, u32[]{:S(2)}) copy-start(f32[9,18,2048]{2,1,0:T(8,128)} %get-tuple-element.29) | copy-start | bytes 3981316
  78.2 5.2 %copy-start.11 = (s32[256,1]{0,1:T(1,128)S(1)}, s32[256,1]{0,1:T(1,128)}, u32[]{:S(2)}) copy-start(s32[256,1]{0,1:T(1,128)} %param.8) | copy-start | bytes 3076
  78.2 5.2 %copy-start.9 = (s32[256]{0:T(256)S(1)}, s32[256]{0:T(256)}, u32[]{:S(2)}) copy-start(s32[256]{0:T(256)} %param.9) | copy-start | bytes 3076
  78.2 5.2 %copy-start.10 = (s32[256]{0:T(256)S(1)}, s32[256]{0:T(256)}, u32[]{:S(2)}) copy-start(s32[256]{0:T(256)} %param.10) | copy-start | bytes 3076
  78.2 5.3 %copy-start.8 = (f32[8,256]{1,0:T(8,128)S(1)}, f32[8,256]{1,0:T(8,128)}, u32[]{:S(2)}) copy-start(f32[8,256]{1,0:T(8,128)} %param.11) | copy-start | bytes 24580
  78.3 31.6 %collective-permute-start.2 = (f32[162,2048]{1,0:T(8,128)}, f32[162,2048]{1,0:T(8,128)}, u32[]{:S(2)}, u32[]{:S(2)}) collective-permute-start(f32[162,2048]{1,0:T(8,128)} %reshape.128), channel_id=1, source_target_pairs={{0,8},{8,16},{16,24},{24,32},{32,40},{40,48},{48,56},{56,64},{64,7... | collective-permute-start | bytes 3981320 | tf_op jit(solution)/shard_map/ppermute | solution.py:230
  80.4 30.6 %collective-permute-start.3 = (f32[162,2048]{1,0:T(8,128)}, f32[162,2048]{1,0:T(8,128)S(1)}, u32[]{:S(2)}, u32[]{:S(2)}) collective-permute-start(f32[162,2048]{1,0:T(8,128)} %reshape.129), channel_id=1, source_target_pairs={{8,0},{16,8},{24,16},{32,24},{40,32},{48,40},{56,48},{64,56},{72,6... | collective-permute-start | bytes 3981320 | tf_op jit(solution)/shard_map/ppermute | solution.py:231
  95.7 1.1 copy-start.5
  110.9 1.1 copy-start.6
  124.1 2.8 %copy-start.13 = (f32[10,16,2048]{2,1,0:T(8,128)S(1)}, f32[10,16,2048]{2,1,0:T(8,128)}, u32[]{:S(2)}) copy-start(f32[10,16,2048]{2,1,0:T(8,128)} %get-tuple-element.12) | copy-start | bytes 3932164
  126.8 1.4 copy-start.12

commit v11 on v10

--- a/solution.py
+++ b/solution.py
@@ -287,15 +287,6 @@
     band_rows = density.shape[1]
     row_length = density.shape[2]
     banded = with_halo(density, (("gy", 1),), HALO)
-    response = None
-    features = []
-    for level_index in range(SCALES):
-        dilation = dilations[level_index]
-        along_y = smooth_padded(banded, dilation, 1, band_rows)
-        low, high = z_neighbours(along_y, HALO)
-        run = level_kernel(level_index, level_index == 0, slab_depth, band_rows, row_length)
-        feature, response = run(dilations, low, along_y, high, response)
-        features.append(feature.reshape(slab_depth * band_rows, row_length))
     plane = (band_rows - 1) * row_length
     z_index = base_cell // plane
     remainder = base_cell % plane
@@ -316,12 +307,24 @@
             term = jnp.where(cells == jnp.concatenate([row, row])[None, :], weights[None, :], 0.0)
             weight_grid = term if weight_grid is None else weight_grid + term
     partials = []
-    for feature in features:
+
+    def partial_of(feature):
         picked = jnp.dot(
             feature, pick_x, precision=lax.Precision.HIGH, preferred_element_type=jnp.float32
         )
         per_column = jnp.sum(picked * weight_grid, axis=0)
-        partials.append(per_column[:entries] + per_column[entries:])
+        return per_column[:entries] + per_column[entries:]
+
+    response = None
+    for level_index in range(SCALES):
+        dilation = dilations[level_index]
+        along_y = smooth_padded(banded, dilation, 1, band_rows)
+        low, high = z_neighbours(along_y, HALO)
+        if partials:
+            low, high, partials[-1] = lax.optimization_barrier((low, high, partials[-1]))
+        run = level_kernel(level_index, level_index == 0, slab_depth, band_rows, row_length)
+        feature, response = run(dilations, low, along_y, high, response)
+        partials.append(partial_of(feature.reshape(slab_depth * band_rows, row_length)))
     partial_value = jnp.stack(partials)
     owner_group = owner_rank[:, 0]
     groups = lax.axis_size("gy")

time: 145 us -> 146 us (level)
  waiting for transfers between devices: 25.2 us -> 21.3 us
  other arithmetic: 8.57 us -> 11.9 us
  matrix products: 6.15 us -> 8.69 us
    dot_general x3, matrix products: 5.47 us -> 8.01 us  [partial_of(): jnp.dot(feature, pick_x, precision=lax.Precision.HIGH, preferred_element_...]
    ppermute x3, waiting for transfers between devices: 1.73 us -> 0.01 us  [z_neighbours(): lax.ppermute(flat(lax.slice_in_dim(block, block.shape[0] - width, None, a...]
    ppermute x3, waiting for transfers between devices: 1.6 us -> 0.01 us  [z_neighbours(): lax.ppermute(flat(lax.slice_in_dim(block, 0, width, axis=0)), 'gz', backw...]
    concatenate x2, other arithmetic: 0.02 us -> 1.5 us  [per_device(): jnp.concatenate([row, row])[None, :]]
  transfers between devices with their start and end apart: 8 -> 8, of which waited for: 6 -> 2; matrix products, arithmetic and copies ran while one was open for 10% -> 16% of each run, Pallas kernels for 17% -> 17%
where the time goes in v11:
time: 146 us
  Pallas kernels  36.1 us (25%)
  local copies, waits for them, and re-layouts  26.2 us (18%)
  waiting for transfers between devices  21.3 us (15%)
  starting transfers between devices  18.6 us (13%)
  blocking collectives  12.5 us (9%)
  other arithmetic  11.9 us (8%)
  between operations  10.3 us (7%)
  matrix products  8.69 us (6%)
    pallas_call x3, Pallas kernels, run(): pl.pallas_call(kernel, out_shape=(block, block), in_specs=in_specs, out_s...  36.1 us
    ppermute x2, waiting for transfers between devices, flat_ppermute(): moved = lax.ppermute(part.reshape(rows, part.shape[2]), axis, pairs)  21.3 us
    ppermute x3, starting transfers between devices, z_neighbours(): lax.ppermute(flat(lax.slice_in_dim(block, 0, width, axis=0)), 'gz', backw...  14 us
    all_to_all x1, blocking collectives, per_device(): lax.all_to_all(spread.reshape(SCALES, groups, HOWN), 'gy', split_axis=1,...  12.5 us
    reshape x6, local copies, waits for them, and re-layouts, flat(): return part.reshape(part.shape[0] * part.shape[1], part.shape[2])  12 us
    dot_general x3, matrix products, partial_of(): jnp.dot(feature, pick_x, precision=lax.Precision.HIGH, preferred_element_...  8.01 us
    add x1, other arithmetic, smooth_padded(): running = summand if running is None else running + summand  6.04 us
    slice x2, local copies, waits for them, and re-layouts, z_neighbours(): lax.slice_in_dim(block, 0, width, axis=0)  5.33 us
  transfers between devices with their start and end apart: 8, of which 2 were waited for; matrix products, arithmetic and copies ran while one was open for 16% of the time, Pallas kernels for 17%

profile of v11, /device:TPU:2, one launch (start us, length us, event | category | flops | bytes accessed | tf_op | source)
XLA Modules:
  0.0 145.5 jit_solution(14786781862438020382)
XLA Ops:
  0.6 2.0 %fusion.24 = (f32[10,9,2048]{2,1,0:T(8,128)S(1)}, f32[10,9,2048]{2,1,0:T(8,128)S(1)}) fusion(f32[10,16,2048]{2,1,0:T(8,128)} %param.6), kind=kLoop, calls=%fused_computation.66 | loop fusion | bytes 2949120 | tf_op jit(solution)/shard_map/slice | solution.py:31
  2.6 0.0 copy-start.7
  2.6 0.0 copy-start.11
  2.7 0.0 copy-start.9
  2.7 0.1 reshape.124
  2.8 3.3 %collective-permute-start = (f32[90,2048]{1,0:T(8,128)S(1)}, f32[90,2048]{1,0:T(8,128)}, u32[]{:S(2)}, u32[]{:S(2)}) collective-permute-start(f32[90,2048]{1,0:T(8,128)S(1)} %reshape.124), channel_id=1, source_target_pairs={{0,1},{1,2},{2,3},{3,4},{4,5},{5,6},{6,7},{7,0},{8,9},{9,10},{10,1... | collective-permute-start | bytes 2211848 | tf_op jit(solution)/shard_map/ppermute | solution.py:20
  6.0 1.0 reshape.126
  7.0 1.2 collective-permute-start.1
  8.3 0.6 fusion.26
  18.4 0.6 add.337
  19.0 20.7 %collective-permute-done = f32[90,2048]{1,0:T(8,128)} collective-permute-done((f32[90,2048]{1,0:T(8,128)S(1)}, f32[90,2048]{1,0:T(8,128)}, u32[]{:S(2)}, u32[]{:S(2)}) %collective-permute-start) | collective-permute-done | bytes 737312 | tf_op jit(solution)/shard_map/ppermute | solution.py:20
  39.7 1.2 reshape.125
  40.9 0.6 collective-permute-done.1
  41.5 2.3 %reshape.127 = f32[10,9,2048]{2,1,0:T(8,128)} reshape(f32[90,2048]{1,0:T(8,128)} %collective-permute-done.1) | data formatting | bytes 1474560 | tf_op jit(solution)/shard_map/reshape | solution.py:21
  43.8 1.8 %pad_maximum_fusion = f32[10,34,2048]{2,1,0:T(8,128)S(1)} fusion(f32[10,9,2048]{2,1,0:T(8,128)} %reshape.127, f32[10,16,2048]{2,1,0:T(8,128)S(1)} %copy-done.3, f32[10,9,2048]{2,1,0:T(8,128)S(1)} %reshape.125), kind=kLoop, calls=%fused_computation.4 | loop fusion | flops 1392640 | bytes 5570560 | tf_op jit(solution)/shard_map/concatenate | solution.py:34
  45.6 6.0 %multiply_add_fusion = (f32[10,18,2048]{2,1,0:T(8,128)S(1)}, f32[10,18,2048]{2,1,0:T(8,128)S(1)}, f32[10,18,2048]{2,1,0:T(8,128)}) fusion(f32[10,34,2048]{2,1,0:T(8,128)S(1)} %pad_maximum_fusion, s32[]{:T(128)S(6)} %select_n.83, s32[]{:T(128)S(6)} %select_n.82, s32[]{:T(128)S(6)} %select_n.81, s32[]{:T(128)S(6)} %select_n.80, s32[]{:T(128)S(6)} %select_n.79, ...), kind=kLoop, calls=%fused_computation.11 | loop fusion | flops 9216000 | bytes 23593008 | tf_op jit(solution)/shard_map/add | solution.py:45
  51.7 3.1 %fusion.21 = (f32[9,18,2048]{2,1,0:T(8,128)S(1)}, f32[9,18,2048]{2,1,0:T(8,128)}, f32[9,18,2048]{2,1,0:T(8,128)S(1)}, f32[9,18,2048]{2,1,0:T(8,128)}) fusion(f32[10,18,2048]{2,1,0:T(8,128)S(1)} %get-tuple-element.34.refs_2_, f32[10,18,2048]{2,1,0:T(8,128)S(1)} %get-tuple-element.35.refs_2_), kind=kLoop, calls=%fused_computation.63 | loop fusion | bytes 10616832 | tf_op jit(solution)/shard_map/slice | solution.py:231
  54.8 2.7 %reshape.132 = f32[162,2048]{1,0:T(8,128)} reshape(f32[9,18,2048]{2,1,0:T(8,128)} %get-tuple-element.38) | data formatting | bytes 2654208 | tf_op jit(solution)/shard_map/reshape | solution.py:228
  57.4 0.0 collective-permute-start.6
  57.4 0.7 broadcast_add_fusion.1
  58.1 0.6 broadcast_add_fusion
  58.7 1.2 reshape.133
  60.0 6.5 %collective-permute-start.7 = (f32[162,2048]{1,0:T(8,128)}, f32[162,2048]{1,0:T(8,128)}, u32[]{:S(2)}, u32[]{:S(2)}) collective-permute-start(f32[162,2048]{1,0:T(8,128)} %reshape.133), channel_id=1, source_target_pairs={{8,0},{16,8},{24,16},{32,24},{40,32},{48,40},{56,48},{64,56},{72,6... | collective-permute-start | bytes 3981320 | tf_op jit(solution)/shard_map/ppermute | solution.py:231
  66.4 0.8 pad_add_fusion.4
  67.2 0.7 pad_add_fusion.2
  68.0 1.3 reshape.130
  69.2 0.0 collective-permute-start.4
  69.2 2.8 %reshape.131 = f32[162,2048]{1,0:T(8,128)} reshape(f32[9,18,2048]{2,1,0:T(8,128)} %get-tuple-element.63) | data formatting | bytes 2654208 | tf_op jit(solution)/shard_map/reshape | solution.py:228
  72.0 3.7 %collective-permute-start.5 = (f32[162,2048]{1,0:T(8,128)}, f32[162,2048]{1,0:T(8,128)}, u32[]{:S(2)}, u32[]{:S(2)}) collective-permute-start(f32[162,2048]{1,0:T(8,128)} %reshape.131), channel_id=1, source_target_pairs={{8,0},{16,8},{24,16},{32,24},{40,32},{48,40},{56,48},{64,56},{72,6... | collective-permute-start | bytes 3981320 | tf_op jit(solution)/shard_map/ppermute | solution.py:231
  75.7 2.2 %fusion.23 = (f32[9,18,2048]{2,1,0:T(8,128)}, f32[9,18,2048]{2,1,0:T(8,128)}) fusion(f32[10,18,2048]{2,1,0:T(8,128)S(1)} %copy-done.2), kind=kLoop, calls=%fused_computation.65 | loop fusion | bytes 5308416 | tf_op jit(solution)/shard_map/slice | solution.py:231
  78.0 2.8 %reshape.128 = f32[162,2048]{1,0:T(8,128)} reshape(f32[9,18,2048]{2,1,0:T(8,128)} %get-tuple-element.42) | data formatting | bytes 2654208 | tf_op jit(solution)/shard_map/reshape | solution.py:228
  80.8 1.3 reshape.129
  82.1 0.0 collective-permute-done.6.refs_1_
  82.1 3.9 %collective-permute-start.3 = (f32[162,2048]{1,0:T(8,128)}, f32[162,2048]{1,0:T(8,128)S(1)}, u32[]{:S(2)}, u32[]{:S(2)}) collective-permute-start(f32[162,2048]{1,0:T(8,128)} %reshape.129), channel_id=1, source_target_pairs={{8,0},{16,8},{24,16},{32,24},{40,32},{48,40},{56,48},{64,56},{72,6... | collective-permute-start | bytes 3981320 | tf_op jit(solution)/shard_map/ppermute | solution.py:231
  86.0 0.0 collective-permute-done.7.refs_3_
  86.0 12.0 %shard_map.77 = (f32[10,16,2048]{2,1,0:T(8,128)}, f32[10,16,2048]{2,1,0:T(8,128)}) custom-call(s32[3]{0:T(128)} %refs_0_.5, f32[162,2048]{1,0:T(8,128)} %collective-permute-done.6.refs_1_, f32[10,18,2048]{2,1,0:T(8,128)} %copy-done.1, f32[162,2048]{1,0:T(8,128)} %collective-permute-done.7.refs_3_), custom_call_target="tpu_custom_call" | custom-call | tf_op jit(solution)/shard_map/pallas_call | solution.py:198
  98.0 2.7 %fusion.12 = f32[512]{0:T(512)S(1)} fusion(f32[160,2048]{1,0:T(8,128)} %bitcast.57, s32[512]{0:T(512)S(1)} %get-tuple-element.58, f32[512]{0:T(512)S(1)} %get-tuple-element.67, s32[512]{0:T(512)S(1)} %pad_add_fusion.4, f32[512]{0:T(512)S(1)} %get-tuple-element.66, s32[512]{0:T(512)S(1)} %get-tuple-element.61, f32[512]{0:T(512)S(1)} %get-tuple-element.65, ...), kind=kOutput, calls=%fused_computation.19 | convolution fusion | flops 1008745984 | bytes 1331200 | tf_op jit(solution)/shard_map/dot_general | solution.py:312
  100.6 0.0 collective-permute-done.4.refs_1_
  100.7 12.0 %shard_map.78 = (f32[10,16,2048]{2,1,0:T(8,128)}, f32[10,16,2048]{2,1,0:T(8,128)}) custom-call(s32[3]{0:T(128)} %refs_0_.5, f32[162,2048]{1,0:T(8,128)} %collective-permute-done.4.refs_1_, f32[10,18,2048]{2,1,0:T(8,128)} %copy-done, f32[162,2048]{1,0:T(8,128)} %collective-permute-done.5.refs_3_, f32[10,16,2048]{2,1,0:T(8,128)} %get-tuple-element.17.refs_4_), custom_call_target="tpu_custom_call" | custom-call | tf_op jit(solution)/shard_map/pallas_call | solution.py:198
  112.7 2.7 %fusion.11 = f32[512]{0:T(512)S(1)} fusion(f32[160,2048]{1,0:T(8,128)} %bitcast.58, s32[512]{0:T(512)S(1)} %get-tuple-element.58, f32[512]{0:T(512)S(1)} %get-tuple-element.67, s32[512]{0:T(512)S(1)} %pad_add_fusion.4, f32[512]{0:T(512)S(1)} %get-tuple-element.66, s32[512]{0:T(512)S(1)} %get-tuple-element.61, f32[512]{0:T(512)S(1)} %get-tuple-element.65, ...), kind=kOutput, calls=%fused_computation.18 | convolution fusion | flops 1008745984 | bytes 1331200 | tf_op jit(solution)/shard_map/dot_general | solution.py:312
  115.4 1.1 copy-done.5
  116.5 0.5 copy-done.6
  117.0 12.0 %shard_map.79 = (f32[10,16,2048]{2,1,0:T(8,128)}, f32[10,16,2048]{2,1,0:T(8,128)}) custom-call(s32[3]{0:T(128)} %refs_0_.5, f32[162,2048]{1,0:T(8,128)} %copy-done.5, f32[10,18,2048]{2,1,0:T(8,128)} %get-tuple-element.36.refs_2_, f32[162,2048]{1,0:T(8,128)} %copy-done.6, f32[10,16,2048]{2,1,0:T(8,128)} %get-tuple-element.21.refs_4_), custom_call_target="tpu_custom_call" | custom-call | tf_op jit(solution)/shard_map/pallas_call | solution.py:198
  129.0 0.0 copy-start.10
  129.0 2.7 %fusion.10 = f32[512]{0:T(512)S(1)} fusion(f32[160,2048]{1,0:T(8,128)} %bitcast.56, s32[512]{0:T(512)S(1)} %get-tuple-element.58, f32[512]{0:T(512)S(1)} %get-tuple-element.67, s32[512]{0:T(512)S(1)} %pad_add_fusion.4, f32[512]{0:T(512)S(1)} %get-tuple-element.66, s32[512]{0:T(512)S(1)} %get-tuple-element.61, f32[512]{0:T(512)S(1)} %get-tuple-element.65, ...), kind=kOutput, calls=%fused_computation.17 | convolution fusion | flops 1008745984 | bytes 1331200 | tf_op jit(solution)/shard_map/dot_general | solution.py:312
  131.7 0.7 fusion.6
  132.4 12.5 %all_to_all.5 = f32[3,8,256]{2,0,1:T(4,128)S(1)} all-to-all(f32[3,8,256]{2,0,1:T(4,128)S(1)} %bitcast.43), channel_id=1, replica_groups=mesh['gz'=32,'gy'=8] {'gy'}, dimensions={1} | all-to-all | bytes 49152 | tf_op jit(solution)/shard_map/all_to_all | solution.py:338
  144.9 0.6 reduce_sum.39
  (30 shorter events, 0.1 us)
Async XLA Ops:
  2.6 5.6 %copy-start.7 = (s32[3]{0:T(128)S(1)}, s32[3]{0:T(128)}, u32[]{:S(2)}) copy-start(s32[3]{0:T(128)} %refs_0_.5) | copy-start | bytes 40
  2.6 15.7 %copy-start.11 = (s32[256,1]{0,1:T(1,128)S(1)}, s32[256,1]{0,1:T(1,128)}, u32[]{:S(2)}) copy-start(s32[256,1]{0,1:T(1,128)} %param.8) | copy-start | bytes 3076
  2.7 15.7 %copy-start.9 = (s32[256]{0:T(256)S(1)}, s32[256]{0:T(256)}, u32[]{:S(2)}) copy-start(s32[256]{0:T(256)} %param.9) | copy-start | bytes 3076
  2.8 36.9 %collective-permute-start = (f32[90,2048]{1,0:T(8,128)S(1)}, f32[90,2048]{1,0:T(8,128)}, u32[]{:S(2)}, u32[]{:S(2)}) collective-permute-start(f32[90,2048]{1,0:T(8,128)S(1)} %reshape.124), channel_id=1, source_target_pairs={{0,1},{1,2},{2,3},{3,4},{4,5},{5,6},{6,7},{7,0},{8,9},{9,10},{10,1... | collective-permute-start | bytes 2211848 | tf_op jit(solution)/shard_map/ppermute | solution.py:20
  7.0 34.5 %collective-permute-start.1 = (f32[90,2048]{1,0:T(8,128)}, f32[90,2048]{1,0:T(8,128)}, u32[]{:S(2)}, u32[]{:S(2)}) collective-permute-start(f32[90,2048]{1,0:T(8,128)} %reshape.126), channel_id=1, source_target_pairs={{1,0},{2,1},{3,2},{4,3},{5,4},{6,5},{7,6},{0,7},{9,8},{10,9},{11,1... | collective-permute-start | bytes 2211848 | tf_op jit(solution)/shard_map/ppermute | solution.py:20
  19.0 24.8 %copy-start.3 = (f32[10,16,2048]{2,1,0:T(8,128)S(1)}, f32[10,16,2048]{2,1,0:T(8,128)}, u32[]{:S(2)}) copy-start(f32[10,16,2048]{2,1,0:T(8,128)} %param.6) | copy-start | bytes 3932164
  51.7 3.1 %copy-start = (f32[10,18,2048]{2,1,0:T(8,128)}, f32[10,18,2048]{2,1,0:T(8,128)S(1)}, u32[]{:S(2)}) copy-start(f32[10,18,2048]{2,1,0:T(8,128)S(1)} %get-tuple-element.35.refs_2_) | copy-start | bytes 4423684
  51.7 3.1 %copy-start.1 = (f32[10,18,2048]{2,1,0:T(8,128)}, f32[10,18,2048]{2,1,0:T(8,128)S(1)}, u32[]{:S(2)}) copy-start(f32[10,18,2048]{2,1,0:T(8,128)S(1)} %get-tuple-element.34.refs_2_) | copy-start | bytes 4423684
  57.4 24.6 %collective-permute-start.6 = (f32[162,2048]{1,0:T(8,128)}, f32[162,2048]{1,0:T(8,128)}, u32[]{:S(2)}, u32[]{:S(2)}) collective-permute-start(f32[162,2048]{1,0:T(8,128)} %reshape.132), channel_id=1, source_target_pairs={{0,8},{8,16},{16,24},{24,32},{32,40},{40,48},{48,56},{56,64},{64,7... | collective-permute-start | bytes 3981320 | tf_op jit(solution)/shard_map/ppermute | solution.py:230
  60.0 26.0 %collective-permute-start.7 = (f32[162,2048]{1,0:T(8,128)}, f32[162,2048]{1,0:T(8,128)}, u32[]{:S(2)}, u32[]{:S(2)}) collective-permute-start(f32[162,2048]{1,0:T(8,128)} %reshape.133), channel_id=1, source_target_pairs={{8,0},{16,8},{24,16},{32,24},{40,32},{48,40},{56,48},{64,56},{72,6... | collective-permute-start | bytes 3981320 | tf_op jit(solution)/shard_map/ppermute | solution.py:231
  69.2 6.5 %copy-start.2 = (f32[10,18,2048]{2,1,0:T(8,128)S(1)}, f32[10,18,2048]{2,1,0:T(8,128)}, u32[]{:S(2)}) copy-start(f32[10,18,2048]{2,1,0:T(8,128)} %get-tuple-element.36.refs_2_) | copy-start | bytes 4423684
  69.2 31.4 %collective-permute-start.4 = (f32[162,2048]{1,0:T(8,128)}, f32[162,2048]{1,0:T(8,128)}, u32[]{:S(2)}, u32[]{:S(2)}) collective-permute-start(f32[162,2048]{1,0:T(8,128)} %reshape.130), channel_id=1, source_target_pairs={{0,8},{8,16},{16,24},{24,32},{32,40},{40,48},{48,56},{56,64},{64,7... | collective-permute-start | bytes 3981320 | tf_op jit(solution)/shard_map/ppermute | solution.py:230
  72.0 28.6 %collective-permute-start.5 = (f32[162,2048]{1,0:T(8,128)}, f32[162,2048]{1,0:T(8,128)}, u32[]{:S(2)}, u32[]{:S(2)}) collective-permute-start(f32[162,2048]{1,0:T(8,128)} %reshape.131), channel_id=1, source_target_pairs={{8,0},{16,8},{24,16},{32,24},{40,32},{48,40},{56,48},{64,56},{72,6... | collective-permute-start | bytes 3981320 | tf_op jit(solution)/shard_map/ppermute | solution.py:231
  78.0 2.8 %copy-start.4 = (f32[9,18,2048]{2,1,0:T(8,128)S(1)}, f32[9,18,2048]{2,1,0:T(8,128)}, u32[]{:S(2)}) copy-start(f32[9,18,2048]{2,1,0:T(8,128)} %get-tuple-element.41) | copy-start | bytes 3981316
  80.8 5.1 %copy-start.8 = (f32[8,256]{1,0:T(8,128)S(1)}, f32[8,256]{1,0:T(8,128)}, u32[]{:S(2)}) copy-start(f32[8,256]{1,0:T(8,128)} %param.11) | copy-start | bytes 24580
  80.8 34.6 %collective-permute-start.2 = (f32[162,2048]{1,0:T(8,128)}, f32[162,2048]{1,0:T(8,128)S(1)}, u32[]{:S(2)}, u32[]{:S(2)}) collective-permute-start(f32[162,2048]{1,0:T(8,128)} %reshape.128), channel_id=1, source_target_pairs={{0,8},{8,16},{16,24},{24,32},{32,40},{40,48},{48,56},{56,64},{64,7... | collective-permute-start | bytes 3981320 | tf_op jit(solution)/shard_map/ppermute | solution.py:230
  82.1 33.3 %collective-permute-start.3 = (f32[162,2048]{1,0:T(8,128)}, f32[162,2048]{1,0:T(8,128)S(1)}, u32[]{:S(2)}, u32[]{:S(2)}) collective-permute-start(f32[162,2048]{1,0:T(8,128)} %reshape.129), channel_id=1, source_target_pairs={{8,0},{16,8},{24,16},{32,24},{40,32},{48,40},{56,48},{64,56},{72,6... | collective-permute-start | bytes 3981320 | tf_op jit(solution)/shard_map/ppermute | solution.py:231
  115.4 1.1 copy-start.5
  115.4 1.5 %copy-start.6 = (f32[162,2048]{1,0:T(8,128)}, f32[162,2048]{1,0:T(8,128)S(1)}, u32[]{:S(2)}) copy-start(f32[162,2048]{1,0:T(8,128)S(1)} %collective-permute-done.3.refs_3_) | copy-start | bytes 3981316
  129.0 2.7 %copy-start.10 = (s32[256]{0:T(256)S(1)}, s32[256]{0:T(256)}, u32[]{:S(2)}) copy-start(s32[256]{0:T(256)} %add.337) | copy-start | bytes 3076

commit v12 on v10

--- a/solution.py
+++ b/solution.py
@@ -163,7 +163,7 @@
         def row_wait(row):
             pltpu.make_async_copy(mid_hbm.at[0], a_scr.at[row], row_sems.at[row]).wait()
 
-        width = band_rows + 2
+        width = -(-(band_rows + 2) // 8) * 8
 
         def edges_in():
             for copy, flat, first_row in zip(edge_copies, (lo_scr, hi_scr), (0, HALO + slab_depth)):
@@ -201,13 +201,13 @@
             in_specs=in_specs,
             out_specs=(anywhere, anywhere),
             scratch_shapes=[
-                pltpu.VMEM((total_rows, band_rows + 2, row_length), jnp.float32),
+                pltpu.VMEM((total_rows, -(-(band_rows + 2) // 8) * 8, row_length), jnp.float32),
                 pltpu.VMEM((planes, band_rows + 2, row_length), jnp.float32),
                 pltpu.VMEM((slab_depth, band_rows, row_length), jnp.float32),
                 pltpu.VMEM((slab_depth, band_rows, row_length), jnp.float32),
                 pltpu.VMEM((slab_depth, band_rows, row_length), jnp.float32),
-                pltpu.VMEM((HALO * (band_rows + 2), row_length), jnp.float32),
-                pltpu.VMEM((HALO * (band_rows + 2), row_length), jnp.float32),
+                pltpu.VMEM((HALO * -(-(band_rows + 2) // 8) * 8, row_length), jnp.float32),
+                pltpu.VMEM((HALO * -(-(band_rows + 2) // 8) * 8, row_length), jnp.float32),
                 pltpu.SemaphoreType.DMA((total_rows,)),
                 pltpu.SemaphoreType.DMA((2, slab_depth)),
                 pltpu.SemaphoreType.DMA((1,)),
@@ -287,11 +287,14 @@
     band_rows = density.shape[1]
     row_length = density.shape[2]
     banded = with_halo(density, (("gy", 1),), HALO)
+    aligned_rows = -(-(band_rows + 2) // 8) * 8
+    spare = jnp.zeros((slab_depth, aligned_rows - band_rows - 2, row_length), jnp.float32)
+    banded = jnp.concatenate([banded, spare], axis=1)
     response = None
     features = []
     for level_index in range(SCALES):
         dilation = dilations[level_index]
-        along_y = smooth_padded(banded, dilation, 1, band_rows)
+        along_y = smooth_padded(banded, dilation, 1, aligned_rows - 2)
         low, high = z_neighbours(along_y, HALO)
         run = level_kernel(level_index, level_index == 0, slab_depth, band_rows, row_length)
         feature, response = run(dilations, low, along_y, high, response)

time: 145 us -> 164 us (1.13)
  waiting for transfers between devices: 25.2 us -> 61.1 us
  local copies, waits for them, and re-layouts: 26.6 us -> 11.9 us
  starting transfers between devices: 17.9 us -> 12 us
  blocking collectives: 12.5 us -> 14.9 us
    ppermute x3, waiting for transfers between devices: 1.73 us -> 26.6 us  [z_neighbours(): lax.ppermute(flat(lax.slice_in_dim(block, block.shape[0] - width, None, a...]
    reshape x6 -> x0, local copies, waits for them, and re-layouts: 12.1 us -> none  [flat(): return part.reshape(part.shape[0] * part.shape[1], part.shape[2])]
    ppermute x3, starting transfers between devices: 13.3 us -> 5.49 us  [z_neighbours(): lax.ppermute(flat(lax.slice_in_dim(block, 0, width, axis=0)), 'gz', backw...]
    ppermute x3, waiting for transfers between devices: 1.6 us -> 8.58 us  [z_neighbours(): lax.ppermute(flat(lax.slice_in_dim(block, 0, width, axis=0)), 'gz', backw...]
    ppermute x2, waiting for transfers between devices: 21.8 us -> 25.9 us  [flat_ppermute(): moved = lax.ppermute(part.reshape(rows, part.shape[2]), axis, pairs)]
    ppermute x3, starting transfers between devices: 0.1 us -> 2.95 us  [z_neighbours(): lax.ppermute(flat(lax.slice_in_dim(block, block.shape[0] - width, None, a...]
    all_to_all x1, blocking collectives: 12.5 us -> 14.9 us  [per_device(): lax.all_to_all(spread.reshape(SCALES, groups, HOWN), 'gy', split_axis=1,...]
    add x1 -> x2, other arithmetic: 6.03 us -> 6.47 us  [smooth_padded(): running = summand if running is None else running + summand]
  transfers between devices with their start and end apart: 8 -> 8, of which waited for: 6 -> 4; matrix products, arithmetic and copies ran while one was open for 10% -> 4% of each run, Pallas kernels for 17% -> 15%
where the time goes in v12:
time: 164 us
  waiting for transfers between devices  61.1 us (37%)
  Pallas kernels  37 us (23%)
  blocking collectives  14.9 us (9%)
  starting transfers between devices  12 us (7%)
  local copies, waits for them, and re-layouts  11.9 us (7%)
  between operations  10.6 us (6%)
  other arithmetic  9.98 us (6%)
  matrix products  6.15 us (4%)
    pallas_call x3, Pallas kernels, run(): pl.pallas_call(kernel, out_shape=(block, block), in_specs=in_specs, out_s...  37 us
    ppermute x3, waiting for transfers between devices, z_neighbours(): lax.ppermute(flat(lax.slice_in_dim(block, block.shape[0] - width, None, a...  26.6 us
    ppermute x2, waiting for transfers between devices, flat_ppermute(): moved = lax.ppermute(part.reshape(rows, part.shape[2]), axis, pairs)  25.9 us
    all_to_all x1, blocking collectives, per_device(): lax.all_to_all(spread.reshape(SCALES, groups, HOWN), 'gy', split_axis=1,...  14.9 us
    ppermute x3, waiting for transfers between devices, z_neighbours(): lax.ppermute(flat(lax.slice_in_dim(block, 0, width, axis=0)), 'gz', backw...  8.58 us
    add x2, other arithmetic, smooth_padded(): running = summand if running is None else running + summand  6.47 us
    ppermute x3, starting transfers between devices, z_neighbours(): lax.ppermute(flat(lax.slice_in_dim(block, 0, width, axis=0)), 'gz', backw...  5.49 us
    dot_general x3, matrix products, per_device(): jnp.dot(feature, pick_x, precision=lax.Precision.HIGH, preferred_element_...  5.46 us
  transfers between devices with their start and end apart: 8, of which 4 were waited for; matrix products, arithmetic and copies ran while one was open for 4% of the time, Pallas kernels for 15%

profile of v12, /device:TPU:2, one launch (start us, length us, event | category | flops | bytes accessed | tf_op | source)
XLA Modules:
  0.0 163.7 jit_solution(7701284358888543731)
XLA Ops:
  0.6 2.0 %fusion.25 = (f32[10,9,2048]{2,1,0:T(8,128)S(1)}, f32[10,9,2048]{2,1,0:T(8,128)S(1)}) fusion(f32[10,16,2048]{2,1,0:T(8,128)} %param.6), kind=kLoop, calls=%fused_computation.68 | loop fusion | bytes 2949120 | tf_op jit(solution)/shard_map/slice | solution.py:31
  2.7 0.0 copy-start.9
  2.7 0.1 reshape.126
  2.8 3.2 %collective-permute-start.1 = (f32[90,2048]{1,0:T(8,128)S(1)}, f32[90,2048]{1,0:T(8,128)S(1)}, u32[]{:S(2)}, u32[]{:S(2)}) collective-permute-start(f32[90,2048]{1,0:T(8,128)S(1)} %reshape.126), channel_id=1, source_target_pairs={{1,0},{2,1},{3,2},{4,3},{5,4},{6,5},{7,6},{0,7},{9,8},{10,9},{11,1... | collective-permute-start | bytes 2211848 | tf_op jit(solution)/shard_map/ppermute | solution.py:20
  6.0 1.0 reshape.124
  7.0 0.4 collective-permute-start
  7.4 0.6 fusion.27
  14.5 0.1 pad.27.clone
  14.6 25.9 %collective-permute-done.1 = f32[90,2048]{1,0:T(8,128)S(1)} collective-permute-done((f32[90,2048]{1,0:T(8,128)S(1)}, f32[90,2048]{1,0:T(8,128)S(1)}, u32[]{:S(2)}, u32[]{:S(2)}) %collective-permute-start.1) | collective-permute-done | bytes 737312 | tf_op jit(solution)/shard_map/ppermute | solution.py:20
  40.5 1.2 reshape.127
  41.7 0.0 collective-permute-done
  41.7 1.2 reshape.125
  42.9 2.8 %maximum_maximum_fusion = f32[10,40,2048]{2,1,0:T(8,128)S(1)} fusion(f32[10,9,2048]{2,1,0:T(8,128)} %reshape.127, f32[10,16,2048]{2,1,0:T(8,128)} %param.6, f32[10,9,2048]{2,1,0:T(8,128)} %reshape.125, f32[40]{0:T(128)S(1)} %pad.27.clone), kind=kLoop, calls=%fused_computation.4 | loop fusion | flops 2457600 | bytes 6062240 | tf_op jit(solution)/shard_map/concatenate | solution.py:292
  45.7 0.1 copy-done.4
  45.8 0.4 copy-done.5
  46.1 3.1 %multiply_add_fusion = (f32[10,24,2048]{2,1,0:T(8,128)S(1)}, f32[10,24,2048]{2,1,0:T(8,128)S(1)}) fusion(f32[10,40,2048]{2,1,0:T(8,128)S(1)} %maximum_maximum_fusion, s32[]{:T(128)S(6)} %select_n.83, s32[]{:T(128)S(6)} %select_n.82, s32[]{:T(128)S(6)} %select_n.81, s32[]{:T(128)S(6)} %select_n.80, f32[10,9,2048]{2,1,0:T(8,128)S(1)} %copy-done.4, ...), kind=kLoop, calls=%fused_computation.13 | loop fusion | flops 9338880 | bytes 22446112 | tf_op jit(solution)/shard_map/add | solution.py:45
  49.3 3.7 %fusion.22 = (f32[9,24,2048]{2,1,0:T(8,128)}, f32[9,24,2048]{2,1,0:T(8,128)}, f32[9,24,2048]{2,1,0:T(8,128)}, f32[9,24,2048]{2,1,0:T(8,128)}) fusion(f32[10,24,2048]{2,1,0:T(8,128)S(1)} %get-tuple-element.22.refs_2_, f32[10,24,2048]{2,1,0:T(8,128)S(1)} %get-tuple-element.23.refs_2_), kind=kLoop, calls=%fused_computation.65 | loop fusion | bytes 14155776 | tf_op jit(solution)/shard_map/slice | solution.py:231
  52.9 0.4 copy-done.2
  53.3 0.0 collective-permute-start.6
  56.5 3.4 %multiply_add_fusion.2.refs_2_ = f32[10,24,2048]{2,1,0:T(8,128)S(1)} fusion(f32[10,40,2048]{2,1,0:T(8,128)S(1)} %maximum_maximum_fusion, s32[]{:T(128)S(6)} %select_n.75, s32[]{:T(128)S(6)} %select_n.74, s32[]{:T(128)S(6)} %select_n.73, s32[]{:T(128)S(6)} %select_n.72, f32[10,9,2048]{2,1,0:T(8,128)} %reshape.127, f32[10,16,2048]{2,1,0:T(8,128)} %param.6, ...), kind=kLoop, calls=%fused_computation.15 | loop fusion | flops 5406720 | bytes 12615696 | tf_op jit(solution)/shard_map/add | solution.py:45
  59.8 0.0 copy-start.3
  59.8 0.0 copy-start.7
  59.9 0.0 copy-start.13
  59.9 0.0 copy-start.11
  59.9 0.0 copy-start.12
  59.9 0.0 copy-start.10
  59.9 0.6 fusion.24
  60.5 0.6 copy-done.3
  61.1 2.0 %collective-permute-start.2 = (f32[216,2048]{1,0:T(8,128)S(1)}, f32[216,2048]{1,0:T(8,128)}, u32[]{:S(2)}, u32[]{:S(2)}) collective-permute-start(f32[216,2048]{1,0:T(8,128)S(1)} %bitcast.50), channel_id=1, source_target_pairs={{0,8},{8,16},{16,24},{24,32},{32,40},{40,48},{48,56},{56,64},{64,7... | collective-permute-start | bytes 5308424 | tf_op jit(solution)/shard_map/ppermute | solution.py:230
  63.1 0.9 collective-permute-start.4
  64.1 3.9 %collective-permute-start.7 = (f32[216,2048]{1,0:T(8,128)S(1)}, f32[216,2048]{1,0:T(8,128)}, u32[]{:S(2)}, u32[]{:S(2)}) collective-permute-start(f32[216,2048]{1,0:T(8,128)S(1)} %bitcast.53), channel_id=1, source_target_pairs={{8,0},{16,8},{24,16},{32,24},{40,32},{48,40},{56,48},{64,56},{72,6... | collective-permute-start | bytes 5308424 | tf_op jit(solution)/shard_map/ppermute | solution.py:231
  68.0 1.5 collective-permute-start.5
  69.5 9.7 %collective-permute-done.6.refs_1_ = f32[216,2048]{1,0:T(8,128)} collective-permute-done((f32[216,2048]{1,0:T(8,128)}, f32[216,2048]{1,0:T(8,128)}, u32[]{:S(2)}, u32[]{:S(2)}) %collective-permute-start.6) | collective-permute-done | bytes 1769504 | tf_op jit(solution)/shard_map/ppermute | solution.py:230
  79.3 0.0 collective-permute-start.3
  79.5 8.6 %collective-permute-done.7.refs_3_ = f32[216,2048]{1,0:T(8,128)} collective-permute-done((f32[216,2048]{1,0:T(8,128)S(1)}, f32[216,2048]{1,0:T(8,128)}, u32[]{:S(2)}, u32[]{:S(2)}) %collective-permute-start.7) | collective-permute-done | bytes 1769504 | tf_op jit(solution)/shard_map/ppermute | solution.py:231
  88.0 12.3 %shard_map.77 = (f32[10,16,2048]{2,1,0:T(8,128)}, f32[10,16,2048]{2,1,0:T(8,128)}) custom-call(s32[3]{0:T(128)} %refs_0_.5, f32[216,2048]{1,0:T(8,128)} %collective-permute-done.6.refs_1_, f32[10,24,2048]{2,1,0:T(8,128)} %copy-done.2, f32[216,2048]{1,0:T(8,128)} %collective-permute-done.7.refs_3_), custom_call_target="tpu_custom_call" | custom-call | tf_op jit(solution)/shard_map/pallas_call | solution.py:198
  100.4 16.8 %collective-permute-done.4.refs_1_ = f32[216,2048]{1,0:T(8,128)} collective-permute-done((f32[216,2048]{1,0:T(8,128)S(1)}, f32[216,2048]{1,0:T(8,128)}, u32[]{:S(2)}, u32[]{:S(2)}) %collective-permute-start.4) | collective-permute-done | bytes 1769504 | tf_op jit(solution)/shard_map/ppermute | solution.py:230
  117.2 0.0 collective-permute-done.5.refs_3_
  117.2 12.4 %shard_map.78 = (f32[10,16,2048]{2,1,0:T(8,128)}, f32[10,16,2048]{2,1,0:T(8,128)}) custom-call(s32[3]{0:T(128)} %refs_0_.5, f32[216,2048]{1,0:T(8,128)} %collective-permute-done.4.refs_1_, f32[10,24,2048]{2,1,0:T(8,128)} %copy-done.1, f32[216,2048]{1,0:T(8,128)} %collective-permute-done.5.refs_3_, f32[10,16,2048]{2,1,0:T(8,128)} %get-tuple-element.8.refs_4_), custom_call_target="tpu_custom_call" | custom-call | tf_op jit(solution)/shard_map/pallas_call | solution.py:198
  129.6 0.0 collective-permute-done.2.refs_1_
  129.6 0.0 collective-permute-done.3.refs_3_
  129.6 12.3 %shard_map.79 = (f32[10,16,2048]{2,1,0:T(8,128)}, f32[10,16,2048]{2,1,0:T(8,128)}) custom-call(s32[3]{0:T(128)} %refs_0_.5, f32[216,2048]{1,0:T(8,128)} %collective-permute-done.2.refs_1_, f32[10,24,2048]{2,1,0:T(8,128)} %copy-done.3, f32[216,2048]{1,0:T(8,128)} %collective-permute-done.3.refs_3_, f32[10,16,2048]{2,1,0:T(8,128)} %get-tuple-element.9.refs_4_), custom_call_target="tpu_custom_call" | custom-call | tf_op jit(solution)/shard_map/pallas_call | solution.py:198
  141.9 2.8 %fusion.11 = f32[512]{0:T(512)S(1)} fusion(f32[160,2048]{1,0:T(8,128)} %bitcast.69, s32[512]{0:T(512)S(1)} %get-tuple-element.45, f32[512]{0:T(512)S(1)} %get-tuple-element.54, s32[512]{0:T(512)S(1)} %pad_add_fusion.4, f32[512]{0:T(512)S(1)} %get-tuple-element.53, s32[512]{0:T(512)S(1)} %get-tuple-element.48, f32[512]{0:T(512)S(1)} %get-tuple-element.52, ...), kind=kOutput, calls=%fused_computation.19 | convolution fusion | flops 1008745984 | bytes 1331200 | tf_op jit(solution)/shard_map/dot_general | solution.py:323
  144.7 1.3 fusion.12
  146.1 1.3 fusion.13
  147.5 0.7 fusion.6
  148.2 14.9 %all_to_all.5 = f32[3,8,256]{2,0,1:T(4,128)S(1)} all-to-all(f32[3,8,256]{2,0,1:T(4,128)S(1)} %bitcast.54), channel_id=1, replica_groups=mesh['gz'=32,'gy'=8] {'gy'}, dimensions={1} | all-to-all | bytes 49152 | tf_op jit(solution)/shard_map/all_to_all | solution.py:338
  163.1 0.6 reduce_sum.39
  (35 shorter events, 0.2 us)
Async XLA Ops:
  2.7 4.7 %copy-start.9 = (s32[3]{0:T(128)S(1)}, s32[3]{0:T(128)}, u32[]{:S(2)}) copy-start(s32[3]{0:T(128)} %refs_0_.5) | copy-start | bytes 40
  2.8 37.7 %collective-permute-start.1 = (f32[90,2048]{1,0:T(8,128)S(1)}, f32[90,2048]{1,0:T(8,128)S(1)}, u32[]{:S(2)}, u32[]{:S(2)}) collective-permute-start(f32[90,2048]{1,0:T(8,128)S(1)} %reshape.126), channel_id=1, source_target_pairs={{1,0},{2,1},{3,2},{4,3},{5,4},{6,5},{7,6},{0,7},{9,8},{10,9},{11,1... | collective-permute-start | bytes 2211848 | tf_op jit(solution)/shard_map/ppermute | solution.py:20
  7.0 34.7 %collective-permute-start = (f32[90,2048]{1,0:T(8,128)}, f32[90,2048]{1,0:T(8,128)S(1)}, u32[]{:S(2)}, u32[]{:S(2)}) collective-permute-start(f32[90,2048]{1,0:T(8,128)} %reshape.124), channel_id=1, source_target_pairs={{0,1},{1,2},{2,3},{3,4},{4,5},{5,6},{6,7},{7,0},{8,9},{9,10},{10,1... | collective-permute-start | bytes 2211848 | tf_op jit(solution)/shard_map/ppermute | solution.py:20
  42.9 2.8 %copy-start = (f32[10,16,2048]{2,1,0:T(8,128)S(1)}, f32[10,16,2048]{2,1,0:T(8,128)}, u32[]{:S(2)}) copy-start(f32[10,16,2048]{2,1,0:T(8,128)} %param.6) | copy-start | bytes 3932164
  42.9 2.9 %copy-start.4 = (f32[10,9,2048]{2,1,0:T(8,128)S(1)}, f32[10,9,2048]{2,1,0:T(8,128)}, u32[]{:S(2)}) copy-start(f32[10,9,2048]{2,1,0:T(8,128)} %reshape.127) | copy-start | bytes 2211844
  42.9 3.3 %copy-start.5 = (f32[10,9,2048]{2,1,0:T(8,128)S(1)}, f32[10,9,2048]{2,1,0:T(8,128)}, u32[]{:S(2)}) copy-start(f32[10,9,2048]{2,1,0:T(8,128)} %reshape.125) | copy-start | bytes 2211844
  49.3 3.7 %copy-start.1 = (f32[10,24,2048]{2,1,0:T(8,128)}, f32[10,24,2048]{2,1,0:T(8,128)S(1)}, u32[]{:S(2)}) copy-start(f32[10,24,2048]{2,1,0:T(8,128)S(1)} %get-tuple-element.23.refs_2_) | copy-start | bytes 5898244
  49.3 4.1 %copy-start.2 = (f32[10,24,2048]{2,1,0:T(8,128)}, f32[10,24,2048]{2,1,0:T(8,128)S(1)}, u32[]{:S(2)}) copy-start(f32[10,24,2048]{2,1,0:T(8,128)S(1)} %get-tuple-element.22.refs_2_) | copy-start | bytes 5898244
  53.3 26.0 %collective-permute-start.6 = (f32[216,2048]{1,0:T(8,128)}, f32[216,2048]{1,0:T(8,128)}, u32[]{:S(2)}, u32[]{:S(2)}) collective-permute-start(f32[216,2048]{1,0:T(8,128)} %bitcast.28), channel_id=1, source_target_pairs={{0,8},{8,16},{16,24},{24,32},{32,40},{40,48},{48,56},{56,64},{64,7... | collective-permute-start | bytes 5308424 | tf_op jit(solution)/shard_map/ppermute | solution.py:230
  59.8 1.3 copy-start.3
  59.8 3.3 %copy-start.7 = (f32[9,24,2048]{2,1,0:T(8,128)S(1)}, f32[9,24,2048]{2,1,0:T(8,128)}, u32[]{:S(2)}) copy-start(f32[9,24,2048]{2,1,0:T(8,128)} %get-tuple-element.49) | copy-start | bytes 5308420
  59.9 4.2 %copy-start.8 = (f32[9,24,2048]{2,1,0:T(8,128)S(1)}, f32[9,24,2048]{2,1,0:T(8,128)}, u32[]{:S(2)}) copy-start(f32[9,24,2048]{2,1,0:T(8,128)} %get-tuple-element.24) | copy-start | bytes 5308420
  59.9 8.1 %copy-start.6 = (f32[9,24,2048]{2,1,0:T(8,128)S(1)}, f32[9,24,2048]{2,1,0:T(8,128)}, u32[]{:S(2)}) copy-start(f32[9,24,2048]{2,1,0:T(8,128)} %get-tuple-element.50) | copy-start | bytes 5308420
  59.9 19.4 %copy-start.13 = (s32[256,1]{0,1:T(1,128)S(1)}, s32[256,1]{0,1:T(1,128)}, u32[]{:S(2)}) copy-start(s32[256,1]{0,1:T(1,128)} %param.8) | copy-start | bytes 3076
  59.9 19.4 %copy-start.11 = (s32[256]{0:T(256)S(1)}, s32[256]{0:T(256)}, u32[]{:S(2)}) copy-start(s32[256]{0:T(256)} %param.9) | copy-start | bytes 3076
  59.9 19.4 %copy-start.12 = (s32[256]{0:T(256)S(1)}, s32[256]{0:T(256)}, u32[]{:S(2)}) copy-start(s32[256]{0:T(256)} %param.10) | copy-start | bytes 3076
  59.9 19.5 %copy-start.10 = (f32[8,256]{1,0:T(8,128)S(1)}, f32[8,256]{1,0:T(8,128)}, u32[]{:S(2)}) copy-start(f32[8,256]{1,0:T(8,128)} %param.11) | copy-start | bytes 24580
  61.1 68.5 %collective-permute-start.2 = (f32[216,2048]{1,0:T(8,128)S(1)}, f32[216,2048]{1,0:T(8,128)}, u32[]{:S(2)}, u32[]{:S(2)}) collective-permute-start(f32[216,2048]{1,0:T(8,128)S(1)} %bitcast.50), channel_id=1, source_target_pairs={{0,8},{8,16},{16,24},{24,32},{32,40},{40,48},{48,56},{56,64},{64,7... | collective-permute-start | bytes 5308424 | tf_op jit(solution)/shard_map/ppermute | solution.py:230
  63.1 54.1 %collective-permute-start.4 = (f32[216,2048]{1,0:T(8,128)S(1)}, f32[216,2048]{1,0:T(8,128)}, u32[]{:S(2)}, u32[]{:S(2)}) collective-permute-start(f32[216,2048]{1,0:T(8,128)S(1)} %bitcast.52), channel_id=1, source_target_pairs={{0,8},{8,16},{16,24},{24,32},{32,40},{40,48},{48,56},{56,64},{64,7... | collective-permute-start | bytes 5308424 | tf_op jit(solution)/shard_map/ppermute | solution.py:230
  64.1 24.0 %collective-permute-start.7 = (f32[216,2048]{1,0:T(8,128)S(1)}, f32[216,2048]{1,0:T(8,128)}, u32[]{:S(2)}, u32[]{:S(2)}) collective-permute-start(f32[216,2048]{1,0:T(8,128)S(1)} %bitcast.53), channel_id=1, source_target_pairs={{8,0},{16,8},{24,16},{32,24},{40,32},{48,40},{56,48},{64,56},{72,6... | collective-permute-start | bytes 5308424 | tf_op jit(solution)/shard_map/ppermute | solution.py:231
  68.0 49.2 %collective-permute-start.5 = (f32[216,2048]{1,0:T(8,128)S(1)}, f32[216,2048]{1,0:T(8,128)}, u32[]{:S(2)}, u32[]{:S(2)}) collective-permute-start(f32[216,2048]{1,0:T(8,128)S(1)} %bitcast.51), channel_id=1, source_target_pairs={{8,0},{16,8},{24,16},{32,24},{40,32},{48,40},{56,48},{64,56},{72,6... | collective-permute-start | bytes 5308424 | tf_op jit(solution)/shard_map/ppermute | solution.py:231
  79.3 50.3 %collective-permute-start.3 = (f32[216,2048]{1,0:T(8,128)S(1)}, f32[216,2048]{1,0:T(8,128)}, u32[]{:S(2)}, u32[]{:S(2)}) collective-permute-start(f32[216,2048]{1,0:T(8,128)S(1)} %bitcast.49), channel_id=1, source_target_pairs={{8,0},{16,8},{24,16},{32,24},{40,32},{48,40},{56,48},{64,56},{72,6... | collective-permute-start | bytes 5308424 | tf_op jit(solution)/shard_map/ppermute | solution.py:231
  141.9 2.8 %copy-start.15 = (f32[10,16,2048]{2,1,0:T(8,128)S(1)}, f32[10,16,2048]{2,1,0:T(8,128)}, u32[]{:S(2)}) copy-start(f32[10,16,2048]{2,1,0:T(8,128)} %get-tuple-element.12) | copy-start | bytes 3932164
  144.7 1.4 copy-start.14

commit v13 on v10

--- a/solution.py
+++ b/solution.py
@@ -72,17 +72,24 @@
 
             for first_row in range(0, band_rows + 2, 8):
                 rows = min(8, band_rows + 2 - first_row)
-                along_z = None
-                for offset in range(5):
+                def tap(offset):
                     source = HALO - 1 + plane + (offset - 2) * dilation
-                    summand = tap_weights[offset] * a_scr[source, pl.ds(first_row, rows), :]
-                    along_z = summand if along_z is None else along_z + summand
-                running = None
-                for offset in range(5):
-                    shift = (-(offset - 2) * dilation) % row_length
-                    moved = along_z if shift == 0 else pltpu.roll(along_z, shift, 1)
-                    summand = tap_weights[offset] * moved
-                    running = summand if running is None else running + summand
+                    return a_scr[source, pl.ds(first_row, rows), :]
+
+                along_z = (
+                    tap_weights[0] * (tap(0) + tap(4))
+                    + tap_weights[1] * (tap(1) + tap(3))
+                    + tap_weights[2] * tap(2)
+                )
+
+                def moved(offset):
+                    return pltpu.roll(along_z, (-(offset - 2) * dilation) % row_length, 1)
+
+                running = (
+                    tap_weights[0] * (moved(0) + moved(4))
+                    + tap_weights[1] * (moved(1) + moved(3))
+                    + tap_weights[2] * along_z
+                )
                 s_scr[plane, pl.ds(first_row, rows), :] = running
             return carry
 

time: 145 us -> 145 us (level)
  no operation moved by 1% of the time
where the time goes in v13:
time: 145 us; the launch traced here: 143 us
  Pallas kernels  36.2 us (25%)
  local copies, waits for them, and re-layouts  26.6 us (18%)
  waiting for transfers between devices  25.1 us (17%)
  starting transfers between devices  17.9 us (12%)
  blocking collectives  12.5 us (9%)
  between operations  10.4 us (7%)
  other arithmetic  8.59 us (6%)
  matrix products  6.15 us (4%)
    pallas_call x3, Pallas kernels, run(): pl.pallas_call(kernel, out_shape=(block, block), in_specs=in_specs, out_s...  36.2 us
    ppermute x2, waiting for transfers between devices, flat_ppermute(): moved = lax.ppermute(part.reshape(rows, part.shape[2]), axis, pairs)  21.8 us
    ppermute x3, starting transfers between devices, z_neighbours(): lax.ppermute(flat(lax.slice_in_dim(block, 0, width, axis=0)), 'gz', backw...  13.3 us
    all_to_all x1, blocking collectives, per_device(): lax.all_to_all(spread.reshape(SCALES, groups, HOWN), 'gy', split_axis=1,...  12.5 us
    reshape x6, local copies, waits for them, and re-layouts, flat(): return part.reshape(part.shape[0] * part.shape[1], part.shape[2])  12.1 us
    add x1, other arithmetic, smooth_padded(): running = summand if running is None else running + summand  6.05 us
    dot_general x3, matrix products, per_device(): jnp.dot(feature, pick_x, precision=lax.Precision.HIGH, preferred_element_...  5.47 us
    slice x2, local copies, waits for them, and re-layouts, z_neighbours(): lax.slice_in_dim(block, 0, width, axis=0)  5.36 us
  transfers between devices with their start and end apart: 8, of which 6 were waited for; matrix products, arithmetic and copies ran while one was open for 10% of the time, Pallas kernels for 17%

profile of v13, /device:TPU:2, one launch (start us, length us, event | category | flops | bytes accessed | tf_op | source)
XLA Modules:
  0.0 143.5 jit_solution(3045925383563507845)
XLA Ops:
  0.6 2.1 %fusion.24 = (f32[10,9,2048]{2,1,0:T(8,128)S(1)}, f32[10,9,2048]{2,1,0:T(8,128)S(1)}) fusion(f32[10,16,2048]{2,1,0:T(8,128)} %param.6), kind=kLoop, calls=%fused_computation.66 | loop fusion | bytes 2949120 | tf_op jit(solution)/shard_map/slice | solution.py:31
  2.8 0.0 copy-start.7
  2.8 0.1 reshape.124
  2.9 3.3 %collective-permute-start = (f32[90,2048]{1,0:T(8,128)S(1)}, f32[90,2048]{1,0:T(8,128)}, u32[]{:S(2)}, u32[]{:S(2)}) collective-permute-start(f32[90,2048]{1,0:T(8,128)S(1)} %reshape.124), channel_id=1, source_target_pairs={{0,1},{1,2},{2,3},{3,4},{4,5},{5,6},{6,7},{7,0},{8,9},{9,10},{10,1... | collective-permute-start | bytes 2211848 | tf_op jit(solution)/shard_map/ppermute | solution.py:20
  6.2 1.0 reshape.126
  7.1 1.2 collective-permute-start.1
  8.4 0.6 fusion.26
  18.5 0.0 copy-start.3
  18.5 21.3 %collective-permute-done = f32[90,2048]{1,0:T(8,128)} collective-permute-done((f32[90,2048]{1,0:T(8,128)S(1)}, f32[90,2048]{1,0:T(8,128)}, u32[]{:S(2)}, u32[]{:S(2)}) %collective-permute-start) | collective-permute-done | bytes 737312 | tf_op jit(solution)/shard_map/ppermute | solution.py:20
  39.8 1.2 reshape.125
  41.1 0.6 collective-permute-done.1
  41.6 2.3 %reshape.127 = f32[10,9,2048]{2,1,0:T(8,128)} reshape(f32[90,2048]{1,0:T(8,128)} %collective-permute-done.1) | data formatting | bytes 1474560 | tf_op jit(solution)/shard_map/reshape | solution.py:21
  43.9 0.0 copy-done.3
  43.9 1.8 %pad_maximum_fusion = f32[10,34,2048]{2,1,0:T(8,128)S(1)} fusion(f32[10,9,2048]{2,1,0:T(8,128)} %reshape.127, f32[10,16,2048]{2,1,0:T(8,128)S(1)} %copy-done.3, f32[10,9,2048]{2,1,0:T(8,128)S(1)} %reshape.125), kind=kLoop, calls=%fused_computation.4 | loop fusion | flops 1392640 | bytes 5570560 | tf_op jit(solution)/shard_map/concatenate | solution.py:34
  45.7 6.1 %multiply_add_fusion = (f32[10,18,2048]{2,1,0:T(8,128)S(1)}, f32[10,18,2048]{2,1,0:T(8,128)S(1)}, f32[10,18,2048]{2,1,0:T(8,128)}) fusion(f32[10,34,2048]{2,1,0:T(8,128)S(1)} %pad_maximum_fusion, s32[]{:T(128)S(6)} %select_n.83, s32[]{:T(128)S(6)} %select_n.82, s32[]{:T(128)S(6)} %select_n.81, s32[]{:T(128)S(6)} %select_n.80, s32[]{:T(128)S(6)} %select_n.79, ...), kind=kLoop, calls=%fused_computation.11 | loop fusion | flops 9216000 | bytes 23593008 | tf_op jit(solution)/shard_map/add | solution.py:45
  51.8 3.1 %fusion.21 = (f32[9,18,2048]{2,1,0:T(8,128)S(1)}, f32[9,18,2048]{2,1,0:T(8,128)}, f32[9,18,2048]{2,1,0:T(8,128)S(1)}, f32[9,18,2048]{2,1,0:T(8,128)}) fusion(f32[10,18,2048]{2,1,0:T(8,128)S(1)} %get-tuple-element.22.refs_2_, f32[10,18,2048]{2,1,0:T(8,128)S(1)} %get-tuple-element.23.refs_2_), kind=kLoop, calls=%fused_computation.63 | loop fusion | bytes 10616832 | tf_op jit(solution)/shard_map/slice | solution.py:238
  54.9 2.7 %reshape.132 = f32[162,2048]{1,0:T(8,128)} reshape(f32[9,18,2048]{2,1,0:T(8,128)} %get-tuple-element.26) | data formatting | bytes 2654208 | tf_op jit(solution)/shard_map/reshape | solution.py:235
  57.6 0.0 collective-permute-start.6
  57.6 1.2 reshape.133
  58.8 6.5 %collective-permute-start.7 = (f32[162,2048]{1,0:T(8,128)}, f32[162,2048]{1,0:T(8,128)}, u32[]{:S(2)}, u32[]{:S(2)}) collective-permute-start(f32[162,2048]{1,0:T(8,128)} %reshape.133), channel_id=1, source_target_pairs={{8,0},{16,8},{24,16},{32,24},{40,32},{48,40},{56,48},{64,56},{72,6... | collective-permute-start | bytes 3981320 | tf_op jit(solution)/shard_map/ppermute | solution.py:238
  65.3 1.3 reshape.130
  66.6 0.0 collective-permute-start.4
  66.6 2.9 %reshape.131 = f32[162,2048]{1,0:T(8,128)} reshape(f32[9,18,2048]{2,1,0:T(8,128)} %get-tuple-element.51) | data formatting | bytes 2654208 | tf_op jit(solution)/shard_map/reshape | solution.py:235
  69.5 3.7 %collective-permute-start.5 = (f32[162,2048]{1,0:T(8,128)}, f32[162,2048]{1,0:T(8,128)}, u32[]{:S(2)}, u32[]{:S(2)}) collective-permute-start(f32[162,2048]{1,0:T(8,128)} %reshape.131), channel_id=1, source_target_pairs={{8,0},{16,8},{24,16},{32,24},{40,32},{48,40},{56,48},{64,56},{72,6... | collective-permute-start | bytes 3981320 | tf_op jit(solution)/shard_map/ppermute | solution.py:238
  73.2 2.3 %fusion.23 = (f32[9,18,2048]{2,1,0:T(8,128)}, f32[9,18,2048]{2,1,0:T(8,128)}) fusion(f32[10,18,2048]{2,1,0:T(8,128)S(1)} %copy-done.2), kind=kLoop, calls=%fused_computation.65 | loop fusion | bytes 5308416 | tf_op jit(solution)/shard_map/slice | solution.py:238
  75.5 2.8 %reshape.128 = f32[162,2048]{1,0:T(8,128)} reshape(f32[9,18,2048]{2,1,0:T(8,128)} %get-tuple-element.30) | data formatting | bytes 2654208 | tf_op jit(solution)/shard_map/reshape | solution.py:235
  78.3 0.1 collective-permute-start.2
  78.4 0.0 copy-done.4
  78.4 1.3 reshape.129
  79.6 0.7 collective-permute-done.6.refs_1_
  80.4 3.1 %collective-permute-start.3 = (f32[162,2048]{1,0:T(8,128)}, f32[162,2048]{1,0:T(8,128)S(1)}, u32[]{:S(2)}, u32[]{:S(2)}) collective-permute-start(f32[162,2048]{1,0:T(8,128)} %reshape.129), channel_id=1, source_target_pairs={{8,0},{16,8},{24,16},{32,24},{40,32},{48,40},{56,48},{64,56},{72,6... | collective-permute-start | bytes 3981320 | tf_op jit(solution)/shard_map/ppermute | solution.py:238
  83.5 0.0 copy-done.11
  83.7 0.0 collective-permute-done.7.refs_3_
  83.7 12.0 %shard_map.77 = (f32[10,16,2048]{2,1,0:T(8,128)}, f32[10,16,2048]{2,1,0:T(8,128)}) custom-call(s32[3]{0:T(128)} %refs_0_.5, f32[162,2048]{1,0:T(8,128)} %collective-permute-done.6.refs_1_, f32[10,18,2048]{2,1,0:T(8,128)} %copy-done.1, f32[162,2048]{1,0:T(8,128)} %collective-permute-done.7.refs_3_), custom_call_target="tpu_custom_call" | custom-call | tf_op jit(solution)/shard_map/pallas_call | solution.py:205
  95.7 0.0 collective-permute-done.4.refs_1_
  95.7 0.5 collective-permute-done.5.refs_3_
  96.2 0.6 copy-done.5
  96.8 12.1 %shard_map.78 = (f32[10,16,2048]{2,1,0:T(8,128)}, f32[10,16,2048]{2,1,0:T(8,128)}) custom-call(s32[3]{0:T(128)} %refs_0_.5, f32[162,2048]{1,0:T(8,128)} %copy-done.5, f32[10,18,2048]{2,1,0:T(8,128)} %copy-done, f32[162,2048]{1,0:T(8,128)} %collective-permute-done.5.refs_3_, f32[10,16,2048]{2,1,0:T(8,128)} %get-tuple-element.8.refs_4_), custom_call_target="tpu_custom_call" | custom-call | tf_op jit(solution)/shard_map/pallas_call | solution.py:205
  108.9 0.9 collective-permute-done.2.refs_1_
  109.9 1.1 collective-permute-done.3.refs_3_
  111.0 1.1 copy-done.6
  112.1 12.0 %shard_map.79 = (f32[10,16,2048]{2,1,0:T(8,128)}, f32[10,16,2048]{2,1,0:T(8,128)}) custom-call(s32[3]{0:T(128)} %refs_0_.5, f32[162,2048]{1,0:T(8,128)} %collective-permute-done.2.refs_1_, f32[10,18,2048]{2,1,0:T(8,128)} %get-tuple-element.24.refs_2_, f32[162,2048]{1,0:T(8,128)} %copy-done.6, f32[10,16,2048]{2,1,0:T(8,128)} %get-tuple-element.9.refs_4_), custom_call_target="tpu_custom_call" | custom-call | tf_op jit(solution)/shard_map/pallas_call | solution.py:205
  124.1 2.8 %fusion.10 = f32[512]{0:T(512)S(1)} fusion(f32[160,2048]{1,0:T(8,128)} %bitcast.58, s32[512]{0:T(512)S(1)} %get-tuple-element.46, f32[512]{0:T(512)S(1)} %get-tuple-element.55, s32[512]{0:T(512)S(1)} %pad_add_fusion.4, f32[512]{0:T(512)S(1)} %get-tuple-element.54, s32[512]{0:T(512)S(1)} %get-tuple-element.49, f32[512]{0:T(512)S(1)} %get-tuple-element.53, ...), kind=kOutput, calls=%fused_computation.17 | convolution fusion | flops 1008745984 | bytes 1331200 | tf_op jit(solution)/shard_map/dot_general | solution.py:327
  126.9 1.3 fusion.11
  128.3 1.3 fusion.12
  129.7 0.7 fusion.6
  130.3 12.5 %all_to_all.5 = f32[3,8,256]{2,0,1:T(4,128)S(1)} all-to-all(f32[3,8,256]{2,0,1:T(4,128)S(1)} %bitcast.43), channel_id=1, replica_groups=mesh['gz'=32,'gy'=8] {'gy'}, dimensions={1} | all-to-all | bytes 49152 | tf_op jit(solution)/shard_map/all_to_all | solution.py:342
  142.9 0.6 reduce_sum.39
  (34 shorter events, 0.2 us)
Async XLA Ops:
  2.8 5.6 %copy-start.7 = (s32[3]{0:T(128)S(1)}, s32[3]{0:T(128)}, u32[]{:S(2)}) copy-start(s32[3]{0:T(128)} %refs_0_.5) | copy-start | bytes 40
  2.9 36.9 %collective-permute-start = (f32[90,2048]{1,0:T(8,128)S(1)}, f32[90,2048]{1,0:T(8,128)}, u32[]{:S(2)}, u32[]{:S(2)}) collective-permute-start(f32[90,2048]{1,0:T(8,128)S(1)} %reshape.124), channel_id=1, source_target_pairs={{0,1},{1,2},{2,3},{3,4},{4,5},{5,6},{6,7},{7,0},{8,9},{9,10},{10,1... | collective-permute-start | bytes 2211848 | tf_op jit(solution)/shard_map/ppermute | solution.py:20
  7.1 34.5 %collective-permute-start.1 = (f32[90,2048]{1,0:T(8,128)}, f32[90,2048]{1,0:T(8,128)}, u32[]{:S(2)}, u32[]{:S(2)}) collective-permute-start(f32[90,2048]{1,0:T(8,128)} %reshape.126), channel_id=1, source_target_pairs={{1,0},{2,1},{3,2},{4,3},{5,4},{6,5},{7,6},{0,7},{9,8},{10,9},{11,1... | collective-permute-start | bytes 2211848 | tf_op jit(solution)/shard_map/ppermute | solution.py:20
  18.5 25.4 %copy-start.3 = (f32[10,16,2048]{2,1,0:T(8,128)S(1)}, f32[10,16,2048]{2,1,0:T(8,128)}, u32[]{:S(2)}) copy-start(f32[10,16,2048]{2,1,0:T(8,128)} %param.6) | copy-start | bytes 3932164
  51.8 3.1 %copy-start = (f32[10,18,2048]{2,1,0:T(8,128)}, f32[10,18,2048]{2,1,0:T(8,128)S(1)}, u32[]{:S(2)}) copy-start(f32[10,18,2048]{2,1,0:T(8,128)S(1)} %get-tuple-element.23.refs_2_) | copy-start | bytes 4423684
  51.8 3.1 %copy-start.1 = (f32[10,18,2048]{2,1,0:T(8,128)}, f32[10,18,2048]{2,1,0:T(8,128)S(1)}, u32[]{:S(2)}) copy-start(f32[10,18,2048]{2,1,0:T(8,128)S(1)} %get-tuple-element.22.refs_2_) | copy-start | bytes 4423684
  57.6 22.8 %collective-permute-start.6 = (f32[162,2048]{1,0:T(8,128)}, f32[162,2048]{1,0:T(8,128)}, u32[]{:S(2)}, u32[]{:S(2)}) collective-permute-start(f32[162,2048]{1,0:T(8,128)} %reshape.132), channel_id=1, source_target_pairs={{0,8},{8,16},{16,24},{24,32},{32,40},{40,48},{48,56},{56,64},{64,7... | collective-permute-start | bytes 3981320 | tf_op jit(solution)/shard_map/ppermute | solution.py:237
  58.8 24.8 %collective-permute-start.7 = (f32[162,2048]{1,0:T(8,128)}, f32[162,2048]{1,0:T(8,128)}, u32[]{:S(2)}, u32[]{:S(2)}) collective-permute-start(f32[162,2048]{1,0:T(8,128)} %reshape.133), channel_id=1, source_target_pairs={{8,0},{16,8},{24,16},{32,24},{40,32},{48,40},{56,48},{64,56},{72,6... | collective-permute-start | bytes 3981320 | tf_op jit(solution)/shard_map/ppermute | solution.py:238
  66.6 6.6 %copy-start.2 = (f32[10,18,2048]{2,1,0:T(8,128)S(1)}, f32[10,18,2048]{2,1,0:T(8,128)}, u32[]{:S(2)}) copy-start(f32[10,18,2048]{2,1,0:T(8,128)} %get-tuple-element.24.refs_2_) | copy-start | bytes 4423684
  66.6 29.1 %collective-permute-start.4 = (f32[162,2048]{1,0:T(8,128)}, f32[162,2048]{1,0:T(8,128)S(1)}, u32[]{:S(2)}, u32[]{:S(2)}) collective-permute-start(f32[162,2048]{1,0:T(8,128)} %reshape.130), channel_id=1, source_target_pairs={{0,8},{8,16},{16,24},{24,32},{32,40},{40,48},{48,56},{56,64},{64,7... | collective-permute-start | bytes 3981320 | tf_op jit(solution)/shard_map/ppermute | solution.py:237
  69.5 26.7 %collective-permute-start.5 = (f32[162,2048]{1,0:T(8,128)}, f32[162,2048]{1,0:T(8,128)}, u32[]{:S(2)}, u32[]{:S(2)}) collective-permute-start(f32[162,2048]{1,0:T(8,128)} %reshape.131), channel_id=1, source_target_pairs={{8,0},{16,8},{24,16},{32,24},{40,32},{48,40},{56,48},{64,56},{72,6... | collective-permute-start | bytes 3981320 | tf_op jit(solution)/shard_map/ppermute | solution.py:238
  75.5 2.9 %copy-start.4 = (f32[9,18,2048]{2,1,0:T(8,128)S(1)}, f32[9,18,2048]{2,1,0:T(8,128)}, u32[]{:S(2)}) copy-start(f32[9,18,2048]{2,1,0:T(8,128)} %get-tuple-element.29) | copy-start | bytes 3981316
  78.3 5.2 %copy-start.11 = (s32[256,1]{0,1:T(1,128)S(1)}, s32[256,1]{0,1:T(1,128)}, u32[]{:S(2)}) copy-start(s32[256,1]{0,1:T(1,128)} %param.8) | copy-start | bytes 3076
  78.3 5.2 %copy-start.9 = (s32[256]{0:T(256)S(1)}, s32[256]{0:T(256)}, u32[]{:S(2)}) copy-start(s32[256]{0:T(256)} %param.9) | copy-start | bytes 3076
  78.3 5.2 %copy-start.10 = (s32[256]{0:T(256)S(1)}, s32[256]{0:T(256)}, u32[]{:S(2)}) copy-start(s32[256]{0:T(256)} %param.10) | copy-start | bytes 3076
  78.3 5.3 %copy-start.8 = (f32[8,256]{1,0:T(8,128)S(1)}, f32[8,256]{1,0:T(8,128)}, u32[]{:S(2)}) copy-start(f32[8,256]{1,0:T(8,128)} %param.11) | copy-start | bytes 24580
  78.3 31.6 %collective-permute-start.2 = (f32[162,2048]{1,0:T(8,128)}, f32[162,2048]{1,0:T(8,128)}, u32[]{:S(2)}, u32[]{:S(2)}) collective-permute-start(f32[162,2048]{1,0:T(8,128)} %reshape.128), channel_id=1, source_target_pairs={{0,8},{8,16},{16,24},{24,32},{32,40},{40,48},{48,56},{56,64},{64,7... | collective-permute-start | bytes 3981320 | tf_op jit(solution)/shard_map/ppermute | solution.py:237
  80.4 30.6 %collective-permute-start.3 = (f32[162,2048]{1,0:T(8,128)}, f32[162,2048]{1,0:T(8,128)S(1)}, u32[]{:S(2)}, u32[]{:S(2)}) collective-permute-start(f32[162,2048]{1,0:T(8,128)} %reshape.129), channel_id=1, source_target_pairs={{8,0},{16,8},{24,16},{32,24},{40,32},{48,40},{56,48},{64,56},{72,6... | collective-permute-start | bytes 3981320 | tf_op jit(solution)/shard_map/ppermute | solution.py:238
  95.7 1.1 copy-start.5
  111.0 1.1 copy-start.6
  124.1 2.8 %copy-start.13 = (f32[10,16,2048]{2,1,0:T(8,128)S(1)}, f32[10,16,2048]{2,1,0:T(8,128)}, u32[]{:S(2)}) copy-start(f32[10,16,2048]{2,1,0:T(8,128)} %get-tuple-element.12) | copy-start | bytes 3932164
  126.9 1.4 copy-start.12
